TPU v7x, 128 devices: a whole 4x4x4 slice. The times are simulated.
128 devices in a mesh: mom: 16 (over z, y), hist: 8 (over x, core).
Axes of the slice: x: 4, y: 4, z: 4, core: 2. Of those that a mesh axis runs over, the one named last changes fastest.
Arguments:
- hist_panel: float32 [2, 128, 1024, 1024], P(None, 'mom', 'hist')
- free_rows: float32 [2, 128, 4, 1024], P(None, 'mom', None, 'hist'), may hold values from -6 to 6
- screened: float32 [2, 128, 4, 1024], P(None, 'mom', None, 'hist'), may hold values from -0.5 to 0.5
Outputs:
- new_rows: float32 [2, 128, 4, 1024], P(None, 'mom', None, 'hist')
- change_norms: float32 [6], replicated
All inputs are finite; a program needn't handle non-finite values.
Results may differ from a plain program's by a relative error of at most 0.0001.
Values sent between devices are 32-bit elements; how exact they have to be, the bound alone decides.
No kernel may reach another device: no remote copies, remote signals or barrier semaphores. Data moves between devices by JAX's collectives and lax.ppermute only.
A program may use at most 64 MiB of HBM per device.

v0:
```python
import math

import jax
import jax.numpy as jnp
from jax import lax
from jax.sharding import PartitionSpec as P

K = 128
R = 4
ITERS = 6


step_size = 0.25
HIGHEST = lax.Precision.HIGHEST


def tables(rows):
    points = jnp.arange(K, dtype=jnp.int32)
    product = rows[:, None] * points[None, :] % K
    phase = product.astype(jnp.float32) * (2.0 * math.pi / K)
    return (jnp.cos(phase), jnp.sin(phase))


def mm(table, field):
    return jnp.dot(table, field, precision=HIGHEST)


def dft(cosine, sine, real, imag):
    both = jnp.concatenate([real, imag], axis=1)
    cr = mm(cosine, both)
    sr = mm(sine, both)
    n = real.shape[1]
    return (cr[:, :n] + sr[:, n:], cr[:, n:] - sr[:, :n])


def gather_rows(flat, extra):
    pad = jnp.zeros((128,), flat.dtype).at[0].set(extra)
    packed = jnp.concatenate([flat, pad])
    n_mom = lax.axis_size("mom")
    got = lax.all_to_all(jnp.broadcast_to(packed, (n_mom,) + packed.shape), "mom", 0, 0, tiled=True)
    n = flat.shape[0]
    return got[:, :n], jnp.sum(got[:, n])


def to_full_k(rows, lead, k_local, cols):
    g = rows.reshape(rows.shape[0], lead, k_local, R * cols)
    g = jnp.transpose(g, (1, 0, 2, 3))
    return g.reshape(lead, rows.shape[0] * k_local, R * cols)


def hist_reduce(partial, extra, hist_n):
    two, kl, rr, h = partial.shape
    cols = h // hist_n
    x = partial.reshape(two, kl, rr, hist_n, cols)
    x = jnp.transpose(x, (3, 0, 1, 2, 4)).reshape(hist_n, two * kl * rr * cols)
    pad = jnp.zeros((hist_n, 128), x.dtype).at[:, 0].set(extra)
    x = jnp.concatenate([x, pad], axis=1)
    y = lax.all_to_all(x, "hist", 0, 0, tiled=True)
    s = jnp.sum(y, axis=0)
    n = two * kl * rr * cols
    return s[:n].reshape(two, kl, rr, cols), s[n]


def shards(hist_panel, free_rows, screened):
    _, k_local, _, cols = free_rows.shape
    hist_n = hist_panel.shape[3] // cols
    full_hist = hist_panel.shape[3]
    mom_i = lax.axis_index("mom")
    cosine, sine = tables(jnp.arange(K, dtype=jnp.int32))
    own = mom_i * k_local + jnp.arange(k_local, dtype=jnp.int32)
    cos_own, sin_own = tables(own)
    cos_own = cos_own / K
    sin_own = sin_own / K
    nb = 2 * k_local * R * cols

    def sigma_of(full):
        hr, hi = dft(cosine, sine, full[0], full[1])
        pr = hr * screen_hat[0] - hi * screen_hat[1]
        pi = hr * screen_hat[1] + hi * screen_hat[0]
        both = jnp.concatenate([pr, pi], axis=1)
        cb = mm(cos_own, both)
        sb = mm(sin_own, both)
        n = pr.shape[1]
        back_real = cb[:, :n] - sb[:, n:]
        back_imag = cb[:, n:] + sb[:, :n]
        return jnp.stack([-back_imag, back_real]).reshape(2, k_local, R, cols)

    def contract(sigma):
        x = jnp.concatenate([sigma[0], sigma[1]], axis=1)
        a = jnp.einsum("kxs,kst->kxt", x, hist_panel[0], precision=HIGHEST)
        b = jnp.einsum("kxs,kst->kxt", x, hist_panel[1], precision=HIGHEST)
        real = a[:, :R] - b[:, R:]
        imag = b[:, :R] + a[:, R:]
        return jnp.stack([real, imag])

    first = jnp.concatenate([screened.reshape(-1), free_rows.reshape(-1)])
    rows, _ = gather_rows(first, jnp.float32(0.0))
    rows = rows.reshape(rows.shape[0], 2, nb)
    screen_full = to_full_k(rows[:, 0], 2, k_local, cols)
    green_full = to_full_k(rows[:, 1], 2, k_local, cols)
    screen_hat = dft(cosine, sine, screen_full[0], screen_full[1])

    integral, _ = hist_reduce(contract(sigma_of(green_full)), jnp.float32(0.0), hist_n)
    def correction(turn, carry):
        green, integral, deltas = carry
        change = free_rows + step_size * integral - green
        local = jnp.sum(change * change)
        rows, mom_sum = gather_rows(change.reshape(-1), local)
        full = to_full_k(rows, 2, k_local, cols)
        step, total = hist_reduce(contract(sigma_of(full)), mom_sum, hist_n)
        delta = jnp.sqrt(total / (2.0 * K * R * full_hist))
        deltas = lax.dynamic_update_slice(deltas, delta[None], (turn,))
        green = green + change / (1.0 + delta)
        integral = integral + step / (1.0 + delta)
        return (green, integral, deltas)

    carry = (free_rows, integral, jnp.zeros((ITERS,), jnp.float32))
    green, integral, deltas = lax.fori_loop(0, ITERS - 1, correction, carry)
    change = free_rows + step_size * integral - green
    local = jnp.sum(change * change)
    n_dev = lax.axis_size(("mom", "hist"))
    spread = jnp.broadcast_to(local, (n_dev, 1))
    total = jnp.sum(lax.all_to_all(spread, ("mom", "hist"), 0, 0, tiled=True))
    delta = jnp.sqrt(total / (2.0 * K * R * full_hist))
    deltas = deltas.at[ITERS - 1].set(delta)
    green = green + change / (1.0 + delta)
    return (green, deltas)


def solution(mesh):
    placed = (
        P(None, "mom", "hist", None),
        P(None, "mom", None, "hist"),
        P(None, "mom", None, "hist"),
    )
    return jax.shard_map(
        shards,
        mesh=mesh,
        in_specs=placed,
        out_specs=(P(None, "mom", None, "hist"), P()),
        check_vma=False,
    )
```

profile of v0, /device:TPU:1, one launch (start us, length us, event | category | flops | bytes accessed | tf_op | source)
XLA Modules:
  0.0 279.1 jit_solution(11149900544067429110)
XLA Ops:
  1.4 1.5 broadcast_in_dim.26
  2.9 8.6 %all-to-all-start.2 = ((f32[16,1,16512]{2,1,0:T(1,128)}), f32[16,1,16512]{2,1,0:T(1,128)S(1)}, u32[]{:S(2)}, u32[]{:S(2)}) async-start(f32[16,1,16512]{2,1,0:T(1,128)} %broadcast_in_dim.26), calls=%async_computation.2 | async-start | bytes 2113536 | tf_op jit(solution)/shard_map/all_to_all | solution.py:40
  11.6 16.1 %all-to-all-done.2 = f32[16,1,16512]{2,1,0:T(1,128)S(1)} async-done(((f32[16,1,16512]{2,1,0:T(1,128)}), f32[16,1,16512]{2,1,0:T(1,128)S(1)}, u32[]{:S(2)}, u32[]{:S(2)}) %all-to-all-start.2) | async-done | bytes 1056800 | tf_op jit(solution)/shard_map/all_to_all | solution.py:40
  28.7 2.7 slice_reduce_fusion.2
  36.9 2.1 fusion.69
  39.0 2.3 fusion.67
  42.4 6.9 %all-to-all-start.3 = ((f32[8,1,8320]{2,1,0:T(1,128)}), f32[8,1,8320]{2,1,0:T(1,128)S(1)}, u32[]{:S(2)}, u32[]{:S(2)}) async-start(f32[8,1,8320]{2,1,0:T(1,128)} %all_to_all.44), calls=%async_computation.3 | async-start | bytes 532480 | tf_op jit(solution)/shard_map/all_to_all | solution.py:58
  49.6 6.2 %all-to-all-done.3 = f32[8,1,8320]{2,1,0:T(1,128)S(1)} async-done(((f32[8,1,8320]{2,1,0:T(1,128)}), f32[8,1,8320]{2,1,0:T(1,128)S(1)}, u32[]{:S(2)}, u32[]{:S(2)}) %all-to-all-start.3) | async-done | bytes 266272 | tf_op jit(solution)/shard_map/all_to_all | solution.py:58
  56.0 205.4 %while.26 = (s32[]{:T(128)}, f32[2,8,4,128]{3,2,1,0:T(4,128)S(1)}, f32[2,8,4,128]{3,2,1,0:T(4,128)S(1)}, f32[6]{0:T(128)S(1)}, f32[2,8,4,128]{3,2,1,0:T(4,128)S(...) while((s32[]{:T(128)}, f32[2,8,4,128]{3,2,1,0:T(4,128)S(1)}, ...), condition=%wide.region_6.7_spmd.clone.clone, body=%wide.region_1.6_spmd.clone.clone.sunk | while | flops 631083520 | bytes 58899884 | solution.py:118
  58.4 3.6 %all-to-all-start = ((f32[16,1,8320]{2,1,0:T(1,128)}), f32[16,1,8320]{2,1,0:T(1,128)S(1)}, u32[]{:S(2)}, u32[]{:S(2)}) async-start(f32[16,1,8320]{2,1,0:T(1,128)} %broadcast_in_dim.31), calls=%async_computation | async-start | bytes 1064960 | tf_op jit(solution)/shard_map/while/body/eval_jaxpr/all_to_all | solution.py:40
  62.6 9.9 %all-to-all-done = f32[16,1,8320]{2,1,0:T(1,128)S(1)} async-done(((f32[16,1,8320]{2,1,0:T(1,128)}), f32[16,1,8320]{2,1,0:T(1,128)S(1)}, u32[]{:S(2)}, u32[]{:S(2)}) %all-to-all-start) | async-done | bytes 532512 | tf_op jit(solution)/shard_map/while/body/eval_jaxpr/all_to_all | solution.py:40
  72.9 1.1 convolution_bitcast_fusion.9
  76.6 2.1 fusion.160
  78.6 2.1 fusion.159
  83.8 5.3 %all-to-all-start.1 = ((f32[8,1,8320]{2,1,0:T(1,128)}), f32[8,1,8320]{2,1,0:T(1,128)S(1)}, u32[]{:S(2)}, u32[]{:S(2)}) async-start(f32[8,1,8320]{2,1,0:T(1,128)} %all_to_all.59), calls=%async_computation.1 | async-start | bytes 532480 | tf_op jit(solution)/shard_map/while/body/eval_jaxpr/all_to_all | solution.py:58
  89.1 6.5 %all-to-all-done.1 = f32[8,1,8320]{2,1,0:T(1,128)S(1)} async-done(((f32[8,1,8320]{2,1,0:T(1,128)}), f32[8,1,8320]{2,1,0:T(1,128)S(1)}, u32[]{:S(2)}, u32[]{:S(2)}) %all-to-all-start.1) | async-done | bytes 266272 | tf_op jit(solution)/shard_map/while/body/eval_jaxpr/all_to_all | solution.py:58
  99.5 3.6 %all-to-all-start = ((f32[16,1,8320]{2,1,0:T(1,128)}), f32[16,1,8320]{2,1,0:T(1,128)S(1)}, u32[]{:S(2)}, u32[]{:S(2)}) async-start(f32[16,1,8320]{2,1,0:T(1,128)} %broadcast_in_dim.31), calls=%async_computation | async-start | bytes 1064960 | tf_op jit(solution)/shard_map/while/body/eval_jaxpr/all_to_all | solution.py:40
  103.7 9.9 %all-to-all-done = f32[16,1,8320]{2,1,0:T(1,128)S(1)} async-done(((f32[16,1,8320]{2,1,0:T(1,128)}), f32[16,1,8320]{2,1,0:T(1,128)S(1)}, u32[]{:S(2)}, u32[]{:S(2)}) %all-to-all-start) | async-done | bytes 532512 | tf_op jit(solution)/shard_map/while/body/eval_jaxpr/all_to_all | solution.py:40
  114.0 1.1 convolution_bitcast_fusion.9
  117.6 2.1 fusion.160
  119.7 2.1 fusion.159
  124.9 5.3 %all-to-all-start.1 = ((f32[8,1,8320]{2,1,0:T(1,128)}), f32[8,1,8320]{2,1,0:T(1,128)S(1)}, u32[]{:S(2)}, u32[]{:S(2)}) async-start(f32[8,1,8320]{2,1,0:T(1,128)} %all_to_all.59), calls=%async_computation.1 | async-start | bytes 532480 | tf_op jit(solution)/shard_map/while/body/eval_jaxpr/all_to_all | solution.py:58
  130.2 6.5 %all-to-all-done.1 = f32[8,1,8320]{2,1,0:T(1,128)S(1)} async-done(((f32[8,1,8320]{2,1,0:T(1,128)}), f32[8,1,8320]{2,1,0:T(1,128)S(1)}, u32[]{:S(2)}, u32[]{:S(2)}) %all-to-all-start.1) | async-done | bytes 266272 | tf_op jit(solution)/shard_map/while/body/eval_jaxpr/all_to_all | solution.py:58
  140.5 3.6 %all-to-all-start = ((f32[16,1,8320]{2,1,0:T(1,128)}), f32[16,1,8320]{2,1,0:T(1,128)S(1)}, u32[]{:S(2)}, u32[]{:S(2)}) async-start(f32[16,1,8320]{2,1,0:T(1,128)} %broadcast_in_dim.31), calls=%async_computation | async-start | bytes 1064960 | tf_op jit(solution)/shard_map/while/body/eval_jaxpr/all_to_all | solution.py:40
  144.8 9.9 %all-to-all-done = f32[16,1,8320]{2,1,0:T(1,128)S(1)} async-done(((f32[16,1,8320]{2,1,0:T(1,128)}), f32[16,1,8320]{2,1,0:T(1,128)S(1)}, u32[]{:S(2)}, u32[]{:S(2)}) %all-to-all-start) | async-done | bytes 532512 | tf_op jit(solution)/shard_map/while/body/eval_jaxpr/all_to_all | solution.py:40
  155.1 1.1 convolution_bitcast_fusion.9
  156.2 1.1 convolution_bitcast_fusion.8
  158.7 2.1 fusion.160
  160.8 2.1 fusion.159
  166.0 5.3 %all-to-all-start.1 = ((f32[8,1,8320]{2,1,0:T(1,128)}), f32[8,1,8320]{2,1,0:T(1,128)S(1)}, u32[]{:S(2)}, u32[]{:S(2)}) async-start(f32[8,1,8320]{2,1,0:T(1,128)} %all_to_all.59), calls=%async_computation.1 | async-start | bytes 532480 | tf_op jit(solution)/shard_map/while/body/eval_jaxpr/all_to_all | solution.py:58
  171.3 6.5 %all-to-all-done.1 = f32[8,1,8320]{2,1,0:T(1,128)S(1)} async-done(((f32[8,1,8320]{2,1,0:T(1,128)}), f32[8,1,8320]{2,1,0:T(1,128)S(1)}, u32[]{:S(2)}, u32[]{:S(2)}) %all-to-all-start.1) | async-done | bytes 266272 | tf_op jit(solution)/shard_map/while/body/eval_jaxpr/all_to_all | solution.py:58
  181.6 3.6 %all-to-all-start = ((f32[16,1,8320]{2,1,0:T(1,128)}), f32[16,1,8320]{2,1,0:T(1,128)S(1)}, u32[]{:S(2)}, u32[]{:S(2)}) async-start(f32[16,1,8320]{2,1,0:T(1,128)} %broadcast_in_dim.31), calls=%async_computation | async-start | bytes 1064960 | tf_op jit(solution)/shard_map/while/body/eval_jaxpr/all_to_all | solution.py:40
  185.9 9.9 %all-to-all-done = f32[16,1,8320]{2,1,0:T(1,128)S(1)} async-done(((f32[16,1,8320]{2,1,0:T(1,128)}), f32[16,1,8320]{2,1,0:T(1,128)S(1)}, u32[]{:S(2)}, u32[]{:S(2)}) %all-to-all-start) | async-done | bytes 532512 | tf_op jit(solution)/shard_map/while/body/eval_jaxpr/all_to_all | solution.py:40
  196.2 1.1 convolution_bitcast_fusion.9
  197.3 1.1 convolution_bitcast_fusion.8
  199.8 2.1 fusion.160
  201.9 2.1 fusion.159
  207.0 5.3 %all-to-all-start.1 = ((f32[8,1,8320]{2,1,0:T(1,128)}), f32[8,1,8320]{2,1,0:T(1,128)S(1)}, u32[]{:S(2)}, u32[]{:S(2)}) async-start(f32[8,1,8320]{2,1,0:T(1,128)} %all_to_all.59), calls=%async_computation.1 | async-start | bytes 532480 | tf_op jit(solution)/shard_map/while/body/eval_jaxpr/all_to_all | solution.py:58
  212.4 6.5 %all-to-all-done.1 = f32[8,1,8320]{2,1,0:T(1,128)S(1)} async-done(((f32[8,1,8320]{2,1,0:T(1,128)}), f32[8,1,8320]{2,1,0:T(1,128)S(1)}, u32[]{:S(2)}, u32[]{:S(2)}) %all-to-all-start.1) | async-done | bytes 266272 | tf_op jit(solution)/shard_map/while/body/eval_jaxpr/all_to_all | solution.py:58
  222.7 3.6 %all-to-all-start = ((f32[16,1,8320]{2,1,0:T(1,128)}), f32[16,1,8320]{2,1,0:T(1,128)S(1)}, u32[]{:S(2)}, u32[]{:S(2)}) async-start(f32[16,1,8320]{2,1,0:T(1,128)} %broadcast_in_dim.31), calls=%async_computation | async-start | bytes 1064960 | tf_op jit(solution)/shard_map/while/body/eval_jaxpr/all_to_all | solution.py:40
  226.9 9.9 %all-to-all-done = f32[16,1,8320]{2,1,0:T(1,128)S(1)} async-done(((f32[16,1,8320]{2,1,0:T(1,128)}), f32[16,1,8320]{2,1,0:T(1,128)S(1)}, u32[]{:S(2)}, u32[]{:S(2)}) %all-to-all-start) | async-done | bytes 532512 | tf_op jit(solution)/shard_map/while/body/eval_jaxpr/all_to_all | solution.py:40
  237.3 1.1 convolution_bitcast_fusion.9
  238.4 1.1 convolution_bitcast_fusion.8
  240.9 2.1 fusion.160
  243.0 2.1 fusion.159
  248.1 5.3 %all-to-all-start.1 = ((f32[8,1,8320]{2,1,0:T(1,128)}), f32[8,1,8320]{2,1,0:T(1,128)S(1)}, u32[]{:S(2)}, u32[]{:S(2)}) async-start(f32[8,1,8320]{2,1,0:T(1,128)} %all_to_all.59), calls=%async_computation.1 | async-start | bytes 532480 | tf_op jit(solution)/shard_map/while/body/eval_jaxpr/all_to_all | solution.py:58
  253.5 6.5 %all-to-all-done.1 = f32[8,1,8320]{2,1,0:T(1,128)S(1)} async-done(((f32[8,1,8320]{2,1,0:T(1,128)}), f32[8,1,8320]{2,1,0:T(1,128)S(1)}, u32[]{:S(2)}, u32[]{:S(2)}) %all-to-all-start.1) | async-done | bytes 266272 | tf_op jit(solution)/shard_map/while/body/eval_jaxpr/all_to_all | solution.py:58
  262.8 13.7 %all_to_all.66 = f32[128,1,1]{2,1,0:T(1,128)S(1)} all-to-all(f32[128,1,1]{2,1,0:T(1,128)S(1)} %broadcast_in_dim.27), channel_id=1, replica_groups=mesh['mom'=16,'hist'=8] {'mom','hist'}, dimensions={0} | all-to-all | bytes 1024 | tf_op jit(solution)/shard_map/all_to_all | solution.py:123
  (194 shorter events, 50.3 us)
Async XLA Ops:
  2.9 24.7 %all-to-all-start.2 = ((f32[16,1,16512]{2,1,0:T(1,128)}), f32[16,1,16512]{2,1,0:T(1,128)S(1)}, u32[]{:S(2)}, u32[]{:S(2)}) async-start(f32[16,1,16512]{2,1,0:T(1,128)} %broadcast_in_dim.26), calls=%async_computation.2 | async-start | bytes 2113536 | tf_op jit(solution)/shard_map/all_to_all | solution.py:40
  28.7 8.2 %slice-start = ((s8[8388608]{0:T(1024)(128)(4,1)}), s8[4194304]{0:T(1024)(128)(4,1)S(1)}, s32[]{:S(2)}) async-start(s8[8388608]{0:T(1024)(128)(4,1)} %bitcast.119), calls=%async_computation.5 | async-start | bytes 8388608
  33.9 3.1 %slice-start.1 = ((s8[8388608]{0:T(1024)(128)(4,1)}), s8[4194304]{0:T(1024)(128)(4,1)S(1)}, s32[]{:S(2)}) async-start(s8[8388608]{0:T(1024)(128)(4,1)} %bitcast.119), calls=%async_computation.6 | async-start | bytes 8388608
  39.0 10.3 %copy-start.1 = (f32[2,8,4,128]{3,2,1,0:T(4,128)S(1)}, f32[2,8,4,128]{3,2,1,0:T(4,128)}, u32[]{:S(2)}) copy-start(f32[2,8,4,128]{3,2,1,0:T(4,128)} %param.16) | copy-start | bytes 98308
  42.4 13.4 %all-to-all-start.3 = ((f32[8,1,8320]{2,1,0:T(1,128)}), f32[8,1,8320]{2,1,0:T(1,128)S(1)}, u32[]{:S(2)}, u32[]{:S(2)}) async-start(f32[8,1,8320]{2,1,0:T(1,128)} %all_to_all.44), calls=%async_computation.3 | async-start | bytes 532480 | tf_op jit(solution)/shard_map/all_to_all | solution.py:58
  58.4 14.1 %all-to-all-start = ((f32[16,1,8320]{2,1,0:T(1,128)}), f32[16,1,8320]{2,1,0:T(1,128)S(1)}, u32[]{:S(2)}, u32[]{:S(2)}) async-start(f32[16,1,8320]{2,1,0:T(1,128)} %broadcast_in_dim.31), calls=%async_computation | async-start | bytes 1064960 | tf_op jit(solution)/shard_map/while/body/eval_jaxpr/all_to_all | solution.py:40
  72.5 4.0 %copy-start = (f32[2,8,128,1024]{3,2,1,0:T(8,128)S(1)}, f32[2,8,128,1024]{3,2,1,0:T(8,128)}, u32[]{:S(2)}) copy-start(f32[2,8,128,1024]{3,2,1,0:T(8,128)} %get-tuple-element.633) | copy-start | bytes 25165828 | tf_op jit(solution)/shard_map/while
  83.8 11.9 %all-to-all-start.1 = ((f32[8,1,8320]{2,1,0:T(1,128)}), f32[8,1,8320]{2,1,0:T(1,128)S(1)}, u32[]{:S(2)}, u32[]{:S(2)}) async-start(f32[8,1,8320]{2,1,0:T(1,128)} %all_to_all.59), calls=%async_computation.1 | async-start | bytes 532480 | tf_op jit(solution)/shard_map/while/body/eval_jaxpr/all_to_all | solution.py:58
  99.5 14.1 %all-to-all-start = ((f32[16,1,8320]{2,1,0:T(1,128)}), f32[16,1,8320]{2,1,0:T(1,128)S(1)}, u32[]{:S(2)}, u32[]{:S(2)}) async-start(f32[16,1,8320]{2,1,0:T(1,128)} %broadcast_in_dim.31), calls=%async_computation | async-start | bytes 1064960 | tf_op jit(solution)/shard_map/while/body/eval_jaxpr/all_to_all | solution.py:40
  113.6 4.0 %copy-start = (f32[2,8,128,1024]{3,2,1,0:T(8,128)S(1)}, f32[2,8,128,1024]{3,2,1,0:T(8,128)}, u32[]{:S(2)}) copy-start(f32[2,8,128,1024]{3,2,1,0:T(8,128)} %get-tuple-element.633) | copy-start | bytes 25165828 | tf_op jit(solution)/shard_map/while
  124.9 11.9 %all-to-all-start.1 = ((f32[8,1,8320]{2,1,0:T(1,128)}), f32[8,1,8320]{2,1,0:T(1,128)S(1)}, u32[]{:S(2)}, u32[]{:S(2)}) async-start(f32[8,1,8320]{2,1,0:T(1,128)} %all_to_all.59), calls=%async_computation.1 | async-start | bytes 532480 | tf_op jit(solution)/shard_map/while/body/eval_jaxpr/all_to_all | solution.py:58
  140.5 14.1 %all-to-all-start = ((f32[16,1,8320]{2,1,0:T(1,128)}), f32[16,1,8320]{2,1,0:T(1,128)S(1)}, u32[]{:S(2)}, u32[]{:S(2)}) async-start(f32[16,1,8320]{2,1,0:T(1,128)} %broadcast_in_dim.31), calls=%async_computation | async-start | bytes 1064960 | tf_op jit(solution)/shard_map/while/body/eval_jaxpr/all_to_all | solution.py:40
  154.7 4.0 %copy-start = (f32[2,8,128,1024]{3,2,1,0:T(8,128)S(1)}, f32[2,8,128,1024]{3,2,1,0:T(8,128)}, u32[]{:S(2)}) copy-start(f32[2,8,128,1024]{3,2,1,0:T(8,128)} %get-tuple-element.633) | copy-start | bytes 25165828 | tf_op jit(solution)/shard_map/while
  166.0 11.9 %all-to-all-start.1 = ((f32[8,1,8320]{2,1,0:T(1,128)}), f32[8,1,8320]{2,1,0:T(1,128)S(1)}, u32[]{:S(2)}, u32[]{:S(2)}) async-start(f32[8,1,8320]{2,1,0:T(1,128)} %all_to_all.59), calls=%async_computation.1 | async-start | bytes 532480 | tf_op jit(solution)/shard_map/while/body/eval_jaxpr/all_to_all | solution.py:58
  181.6 14.1 %all-to-all-start = ((f32[16,1,8320]{2,1,0:T(1,128)}), f32[16,1,8320]{2,1,0:T(1,128)S(1)}, u32[]{:S(2)}, u32[]{:S(2)}) async-start(f32[16,1,8320]{2,1,0:T(1,128)} %broadcast_in_dim.31), calls=%async_computation | async-start | bytes 1064960 | tf_op jit(solution)/shard_map/while/body/eval_jaxpr/all_to_all | solution.py:40
  195.8 4.0 %copy-start = (f32[2,8,128,1024]{3,2,1,0:T(8,128)S(1)}, f32[2,8,128,1024]{3,2,1,0:T(8,128)}, u32[]{:S(2)}) copy-start(f32[2,8,128,1024]{3,2,1,0:T(8,128)} %get-tuple-element.633) | copy-start | bytes 25165828 | tf_op jit(solution)/shard_map/while
  207.0 11.9 %all-to-all-start.1 = ((f32[8,1,8320]{2,1,0:T(1,128)}), f32[8,1,8320]{2,1,0:T(1,128)S(1)}, u32[]{:S(2)}, u32[]{:S(2)}) async-start(f32[8,1,8320]{2,1,0:T(1,128)} %all_to_all.59), calls=%async_computation.1 | async-start | bytes 532480 | tf_op jit(solution)/shard_map/while/body/eval_jaxpr/all_to_all | solution.py:58
  222.7 14.1 %all-to-all-start = ((f32[16,1,8320]{2,1,0:T(1,128)}), f32[16,1,8320]{2,1,0:T(1,128)S(1)}, u32[]{:S(2)}, u32[]{:S(2)}) async-start(f32[16,1,8320]{2,1,0:T(1,128)} %broadcast_in_dim.31), calls=%async_computation | async-start | bytes 1064960 | tf_op jit(solution)/shard_map/while/body/eval_jaxpr/all_to_all | solution.py:40
  236.9 4.0 %copy-start = (f32[2,8,128,1024]{3,2,1,0:T(8,128)S(1)}, f32[2,8,128,1024]{3,2,1,0:T(8,128)}, u32[]{:S(2)}) copy-start(f32[2,8,128,1024]{3,2,1,0:T(8,128)} %get-tuple-element.633) | copy-start | bytes 25165828 | tf_op jit(solution)/shard_map/while
  248.1 11.9 %all-to-all-start.1 = ((f32[8,1,8320]{2,1,0:T(1,128)}), f32[8,1,8320]{2,1,0:T(1,128)S(1)}, u32[]{:S(2)}, u32[]{:S(2)}) async-start(f32[8,1,8320]{2,1,0:T(1,128)} %all_to_all.59), calls=%async_computation.1 | async-start | bytes 532480 | tf_op jit(solution)/shard_map/while/body/eval_jaxpr/all_to_all | solution.py:58
  278.6 0.5 copy-start.2
where the time goes:
time: 281 us; the launch traced here: 279 us
  waiting for transfers between devices  104 us (37%)
  starting transfers between devices  60 us (21%)
  matrix products  46.6 us (17%)
  other arithmetic  21.3 us (8%)
  local copies, waits for them, and re-layouts  20.8 us (7%)
  blocking collectives  13.7 us (5%)
  loops' own time  10.6 us (4%)
    all_to_all x6, waiting for transfers between devices, gather_rows(): lax.all_to_all(jnp.broadcast_to(packed, (n_mom,) + packed.shape), 'mom',...  65.5 us
    all_to_all x6, waiting for transfers between devices, hist_reduce(): y = lax.all_to_all(x, 'hist', 0, 0, tiled=True)  38.9 us
    all_to_all x6, starting transfers between devices, hist_reduce(): y = lax.all_to_all(x, 'hist', 0, 0, tiled=True)  33.6 us
    all_to_all x6, starting transfers between devices, gather_rows(): lax.all_to_all(jnp.broadcast_to(packed, (n_mom,) + packed.shape), 'mom',...  26.5 us
    dot_general x26, matrix products, mm(): return jnp.dot(table, field, precision=HIGHEST)  21.5 us
    all_to_all x1, blocking collectives, shards(): total = jnp.sum(lax.all_to_all(spread, ('mom', 'hist'), 0, 0, tiled=True))  13.7 us
    dot_general x6, matrix products, contract(): b = jnp.einsum('kxs,kst->kxt', x, hist_panel[1], precision=HIGHEST)  12.7 us
    dot_general x6, matrix products, contract(): a = jnp.einsum('kxs,kst->kxt', x, hist_panel[0], precision=HIGHEST)  12.5 us
  transfers between devices with their start and end apart: 12, of which 12 were waited for; matrix products, arithmetic and copies ran while one was open for 1% of the time, Pallas kernels for 0%

commit v1 on v0

--- a/solution.py
+++ b/solution.py
@@ -33,13 +33,12 @@
     return (cr[:, :n] + sr[:, n:], cr[:, n:] - sr[:, :n])
 
 
-def gather_rows(flat, extra):
-    pad = jnp.zeros((128,), flat.dtype).at[0].set(extra)
-    packed = jnp.concatenate([flat, pad])
+def gather_rows(block, extra):
     n_mom = lax.axis_size("mom")
+    packed = jnp.concatenate([block, jnp.full((8, 128), extra, block.dtype)])
     got = lax.all_to_all(jnp.broadcast_to(packed, (n_mom,) + packed.shape), "mom", 0, 0, tiled=True)
-    n = flat.shape[0]
-    return got[:, :n], jnp.sum(got[:, n])
+    n = block.shape[0]
+    return got[:, :n], jnp.sum(got[:, n, 0])
 
 
 def to_full_k(rows, lead, k_local, cols):
@@ -52,13 +51,12 @@
     two, kl, rr, h = partial.shape
     cols = h // hist_n
     x = partial.reshape(two, kl, rr, hist_n, cols)
-    x = jnp.transpose(x, (3, 0, 1, 2, 4)).reshape(hist_n, two * kl * rr * cols)
-    pad = jnp.zeros((hist_n, 128), x.dtype).at[:, 0].set(extra)
-    x = jnp.concatenate([x, pad], axis=1)
+    x = jnp.transpose(x, (3, 0, 1, 2, 4)).reshape(hist_n, two * kl * rr * cols // 128, 128)
+    x = jnp.concatenate([x, jnp.full((hist_n, 8, 128), extra, x.dtype)], axis=1)
     y = lax.all_to_all(x, "hist", 0, 0, tiled=True)
     s = jnp.sum(y, axis=0)
-    n = two * kl * rr * cols
-    return s[:n].reshape(two, kl, rr, cols), s[n]
+    n = two * kl * rr * cols // 128
+    return s[:n].reshape(two, kl, rr, cols), s[n, 0]
 
 
 def shards(hist_panel, free_rows, screened):
@@ -93,11 +91,11 @@
         imag = b[:, :R] + a[:, R:]
         return jnp.stack([real, imag])
 
-    first = jnp.concatenate([screened.reshape(-1), free_rows.reshape(-1)])
+    first = jnp.concatenate([screened.reshape(-1, 128), free_rows.reshape(-1, 128)])
     rows, _ = gather_rows(first, jnp.float32(0.0))
-    rows = rows.reshape(rows.shape[0], 2, nb)
-    screen_full = to_full_k(rows[:, 0], 2, k_local, cols)
-    green_full = to_full_k(rows[:, 1], 2, k_local, cols)
+    half = nb // 128
+    screen_full = to_full_k(rows[:, :half], 2, k_local, cols)
+    green_full = to_full_k(rows[:, half:], 2, k_local, cols)
     screen_hat = dft(cosine, sine, screen_full[0], screen_full[1])
 
     integral, _ = hist_reduce(contract(sigma_of(green_full)), jnp.float32(0.0), hist_n)
@@ -105,7 +103,7 @@
         green, integral, deltas = carry
         change = free_rows + step_size * integral - green
         local = jnp.sum(change * change)
-        rows, mom_sum = gather_rows(change.reshape(-1), local)
+        rows, mom_sum = gather_rows(change.reshape(-1, 128), local)
         full = to_full_k(rows, 2, k_local, cols)
         step, total = hist_reduce(contract(sigma_of(full)), mom_sum, hist_n)
         delta = jnp.sqrt(total / (2.0 * K * R * full_hist))

time: 281 us -> 279 us (level)
  blocking collectives: 13.7 us -> 83.9 us
  waiting for transfers between devices: 104 us -> 57.3 us
  starting transfers between devices: 60 us -> 42.3 us
  matrix products: 46.6 us -> 59.2 us
  other arithmetic: 21.3 us -> 10.7 us
  loops' own time: 10.6 us -> 4.46 us
    all_to_all x0 -> x5, blocking collectives: none -> 69.9 us  [gather_rows(): lax.all_to_all(jnp.broadcast_to(packed, (n_mom,) + packed.shape), 'mom',...]
    all_to_all x6 -> x1, waiting for transfers between devices: 65.5 us -> 16.7 us  [gather_rows(): lax.all_to_all(jnp.broadcast_to(packed, (n_mom,) + packed.shape), 'mom',...]
    all_to_all x6 -> x1, starting transfers between devices: 26.5 us -> 8.59 us  [gather_rows(): lax.all_to_all(jnp.broadcast_to(packed, (n_mom,) + packed.shape), 'mom',...]
    dot_general x6, matrix products: 12.5 us -> 23.5 us  [contract(): a = jnp.einsum('kxs,kst->kxt', x, hist_panel[0], precision=HIGHEST)]
    concatenate x1 -> x12, local copies, waits for them, and re-layouts: 0.02 us -> 10.8 us  [the longest x6 7.59 us: hist_reduce(): x = jnp.concatenate([x, jnp.full((hist_n, 8, 128), extra, x.dtype)], axis=1)]
    another operation x1, loops' own time: 10.6 us -> 4.46 us  [shards(): green, integral, deltas = lax.fori_loop(0, ITERS - 1, correction, carry)]
    broadcast_in_dim x6, local copies, waits for them, and re-layouts: 6.8 us -> 1.26 us  [gather_rows(): jnp.broadcast_to(packed, (n_mom,) + packed.shape)]
    all_to_all x6 -> x0, local copies, waits for them, and re-layouts: 5.23 us -> none  [hist_reduce(): y = lax.all_to_all(x, 'hist', 0, 0, tiled=True)]
  transfers between devices with their start and end apart: 12 -> 7, of which waited for: 12 -> 7; matrix products, arithmetic and copies ran while one was open for 1% -> 0% of each run, Pallas kernels for 0% -> 0%
where the time goes in v1:
time: 279 us; the launch traced here: 278 us
  blocking collectives  83.9 us (30%)
  matrix products  59.2 us (21%)
  waiting for transfers between devices  57.3 us (21%)
  starting transfers between devices  42.3 us (15%)
  local copies, waits for them, and re-layouts  18.6 us (7%)
  other arithmetic  10.7 us (4%)
  loops' own time  4.46 us (2%)
    all_to_all x5, blocking collectives, gather_rows(): lax.all_to_all(jnp.broadcast_to(packed, (n_mom,) + packed.shape), 'mom',...  69.9 us
    all_to_all x6, waiting for transfers between devices, hist_reduce(): y = lax.all_to_all(x, 'hist', 0, 0, tiled=True)  40.5 us
    all_to_all x6, starting transfers between devices, hist_reduce(): y = lax.all_to_all(x, 'hist', 0, 0, tiled=True)  33.7 us
    dot_general x6, matrix products, contract(): a = jnp.einsum('kxs,kst->kxt', x, hist_panel[0], precision=HIGHEST)  23.5 us
    dot_general x26, matrix products, mm(): return jnp.dot(table, field, precision=HIGHEST)  21.5 us
    all_to_all x1, waiting for transfers between devices, gather_rows(): lax.all_to_all(jnp.broadcast_to(packed, (n_mom,) + packed.shape), 'mom',...  16.7 us
    dot_general x6, matrix products, contract(): b = jnp.einsum('kxs,kst->kxt', x, hist_panel[1], precision=HIGHEST)  14.2 us
    all_to_all x1, blocking collectives, shards(): total = jnp.sum(lax.all_to_all(spread, ('mom', 'hist'), 0, 0, tiled=True))  13.9 us
  transfers between devices with their start and end apart: 7, of which 7 were waited for; matrix products, arithmetic and copies ran while one was open for 0% of the time, Pallas kernels for 0%

profile of v1, /device:TPU:1, one launch (start us, length us, event | category | flops | bytes accessed | tf_op | source)
XLA Modules:
  0.0 278.0 jit_solution(15965208222663612518)
XLA Ops:
  2.6 8.6 %all-to-all-start.2 = ((f32[16,136,128]{2,1,0:T(8,128)}), f32[16,136,128]{2,1,0:T(8,128)S(1)}, u32[]{:S(2)}, u32[]{:S(2)}) async-start(f32[16,136,128]{2,1,0:T(8,128)} %broadcast_in_dim.35), calls=%async_computation.2 | async-start | bytes 2228224 | tf_op jit(solution)/shard_map/all_to_all | solution.py:39
  11.2 16.7 %all-to-all-done.2 = f32[16,136,128]{2,1,0:T(8,128)S(1)} async-done(((f32[16,136,128]{2,1,0:T(8,128)}), f32[16,136,128]{2,1,0:T(8,128)S(1)}, u32[]{:S(2)}, u32[]{:S(2)}) %all-to-all-start.2) | async-done | bytes 1114144 | tf_op jit(solution)/shard_map/all_to_all | solution.py:39
  33.0 3.8 %fusion.67 = f32[8,8,1024]{2,1,0:T(8,128)S(1)} fusion(f32[2,8,128,1024]{3,2,1,0:T(8,128)} %param.7, f32[8,4,128]{2,1,0:T(4,128)S(1)} %copy.49, f32[8,4,128]{2,1,0:T(4,128)S(1)} %copy.48), kind=kOutput, calls=%fused_computation.89 | convolution fusion | flops 100671488 | bytes 4489216 | tf_op jit(solution)/shard_map/kxs,kst->kxt/dot_general | solution.py:88
  36.8 3.8 %fusion.65 = f32[8,8,1024]{2,1,0:T(8,128)S(1)} fusion(f32[2,8,128,1024]{3,2,1,0:T(8,128)} %param.7, f32[8,4,128]{2,1,0:T(4,128)S(1)} %copy.49, f32[8,4,128]{2,1,0:T(4,128)S(1)} %copy.48), kind=kOutput, calls=%fused_computation.87 | convolution fusion | flops 100671488 | bytes 4489216 | tf_op jit(solution)/shard_map/kxs,kst->kxt/dot_general | solution.py:89
  41.6 7.0 %all-to-all-start.3 = ((f32[8,72,128]{2,1,0:T(8,128)}), f32[8,72,128]{2,1,0:T(8,128)S(1)}, u32[]{:S(2)}, u32[]{:S(2)}) async-start(f32[8,72,128]{2,1,0:T(8,128)} %concatenate.60), calls=%async_computation.3 | async-start | bytes 589824 | tf_op jit(solution)/shard_map/all_to_all | solution.py:56
  48.9 6.5 %all-to-all-done.3 = f32[8,72,128]{2,1,0:T(8,128)S(1)} async-done(((f32[8,72,128]{2,1,0:T(8,128)}), f32[8,72,128]{2,1,0:T(8,128)S(1)}, u32[]{:S(2)}, u32[]{:S(2)}) %all-to-all-start.3) | async-done | bytes 294944 | tf_op jit(solution)/shard_map/all_to_all | solution.py:56
  55.4 204.8 %while.20 = (s32[]{:T(128)}, f32[2,8,4,128]{3,2,1,0:T(4,128)S(1)}, f32[2,8,4,128]{3,2,1,0:T(4,128)S(1)}, f32[6]{0:T(128)S(1)}, f32[2,8,4,128]{3,2,1,0:T(4,128)S(...) while((s32[]{:T(128)}, f32[2,8,4,128]{3,2,1,0:T(4,128)S(1)}, ...), condition=%wide.region_5.6_spmd.clone.clone, body=%wide.region_1.5_spmd.clone.clone.sunk | while | flops 630981632 | bytes 57553316 | solution.py:116
  56.8 13.7 %all_to_all.41 = f32[16,72,128]{2,1,0:T(8,128)S(1)} all-to-all(f32[16,72,128]{2,1,0:T(8,128)S(1)} %broadcast_in_dim.42), channel_id=1, replica_groups=mesh['mom'=16,'hist'=8] {'mom'}, dimensions={0} | all-to-all | bytes 1179648 | tf_op jit(solution)/shard_map/while/body/eval_jaxpr/all_to_all | solution.py:39
  70.7 1.1 convolution_bitcast_fusion.9
  71.8 1.1 convolution_bitcast_fusion.8
  74.3 3.9 %fusion.158 = f32[8,8,1024]{2,1,0:T(8,128)S(1)} fusion(f32[2,8,128,1024]{3,2,1,0:T(8,128)} %get-tuple-element.473, f32[8,4,128]{2,1,0:T(4,128)S(1)} %copy.59, f32[8,4,128]{2,1,0:T(4,128)S(1)} %copy.60), kind=kOutput, calls=%fused_computation.6.clone.1 | convolution fusion | flops 100671488 | bytes 4489216 | tf_op jit(solution)/shard_map/while/body/eval_jaxpr/kxs,kst->kxt/dot_general | solution.py:88
  78.2 2.1 fusion.157
  81.2 1.4 concatenate.74
  82.6 5.4 %all-to-all-start.1 = ((f32[8,72,128]{2,1,0:T(8,128)}), f32[8,72,128]{2,1,0:T(8,128)S(1)}, u32[]{:S(2)}, u32[]{:S(2)}) async-start(f32[8,72,128]{2,1,0:T(8,128)} %concatenate.74), calls=%async_computation.1 | async-start | bytes 589824 | tf_op jit(solution)/shard_map/while/body/eval_jaxpr/all_to_all | solution.py:56
  88.0 6.8 %all-to-all-done.1 = f32[8,72,128]{2,1,0:T(8,128)S(1)} async-done(((f32[8,72,128]{2,1,0:T(8,128)}), f32[8,72,128]{2,1,0:T(8,128)S(1)}, u32[]{:S(2)}, u32[]{:S(2)}) %all-to-all-start.1) | async-done | bytes 294944 | tf_op jit(solution)/shard_map/while/body/eval_jaxpr/all_to_all | solution.py:56
  97.5 14.1 %all_to_all.41 = f32[16,72,128]{2,1,0:T(8,128)S(1)} all-to-all(f32[16,72,128]{2,1,0:T(8,128)S(1)} %broadcast_in_dim.42), channel_id=1, replica_groups=mesh['mom'=16,'hist'=8] {'mom'}, dimensions={0} | all-to-all | bytes 1179648 | tf_op jit(solution)/shard_map/while/body/eval_jaxpr/all_to_all | solution.py:39
  111.7 1.1 convolution_bitcast_fusion.9
  112.9 1.1 convolution_bitcast_fusion.8
  115.4 3.9 %fusion.158 = f32[8,8,1024]{2,1,0:T(8,128)S(1)} fusion(f32[2,8,128,1024]{3,2,1,0:T(8,128)} %get-tuple-element.473, f32[8,4,128]{2,1,0:T(4,128)S(1)} %copy.59, f32[8,4,128]{2,1,0:T(4,128)S(1)} %copy.60), kind=kOutput, calls=%fused_computation.6.clone.1 | convolution fusion | flops 100671488 | bytes 4489216 | tf_op jit(solution)/shard_map/while/body/eval_jaxpr/kxs,kst->kxt/dot_general | solution.py:88
  119.3 2.1 fusion.157
  122.3 1.4 concatenate.74
  123.7 5.3 %all-to-all-start.1 = ((f32[8,72,128]{2,1,0:T(8,128)}), f32[8,72,128]{2,1,0:T(8,128)S(1)}, u32[]{:S(2)}, u32[]{:S(2)}) async-start(f32[8,72,128]{2,1,0:T(8,128)} %concatenate.74), calls=%async_computation.1 | async-start | bytes 589824 | tf_op jit(solution)/shard_map/while/body/eval_jaxpr/all_to_all | solution.py:56
  129.0 6.8 %all-to-all-done.1 = f32[8,72,128]{2,1,0:T(8,128)S(1)} async-done(((f32[8,72,128]{2,1,0:T(8,128)}), f32[8,72,128]{2,1,0:T(8,128)S(1)}, u32[]{:S(2)}, u32[]{:S(2)}) %all-to-all-start.1) | async-done | bytes 294944 | tf_op jit(solution)/shard_map/while/body/eval_jaxpr/all_to_all | solution.py:56
  138.5 14.1 %all_to_all.41 = f32[16,72,128]{2,1,0:T(8,128)S(1)} all-to-all(f32[16,72,128]{2,1,0:T(8,128)S(1)} %broadcast_in_dim.42), channel_id=1, replica_groups=mesh['mom'=16,'hist'=8] {'mom'}, dimensions={0} | all-to-all | bytes 1179648 | tf_op jit(solution)/shard_map/while/body/eval_jaxpr/all_to_all | solution.py:39
  152.7 1.1 convolution_bitcast_fusion.9
  153.9 1.1 convolution_bitcast_fusion.8
  156.4 3.9 %fusion.158 = f32[8,8,1024]{2,1,0:T(8,128)S(1)} fusion(f32[2,8,128,1024]{3,2,1,0:T(8,128)} %get-tuple-element.473, f32[8,4,128]{2,1,0:T(4,128)S(1)} %copy.59, f32[8,4,128]{2,1,0:T(4,128)S(1)} %copy.60), kind=kOutput, calls=%fused_computation.6.clone.1 | convolution fusion | flops 100671488 | bytes 4489216 | tf_op jit(solution)/shard_map/while/body/eval_jaxpr/kxs,kst->kxt/dot_general | solution.py:88
  160.3 2.1 fusion.157
  163.3 1.4 concatenate.74
  164.7 5.3 %all-to-all-start.1 = ((f32[8,72,128]{2,1,0:T(8,128)}), f32[8,72,128]{2,1,0:T(8,128)S(1)}, u32[]{:S(2)}, u32[]{:S(2)}) async-start(f32[8,72,128]{2,1,0:T(8,128)} %concatenate.74), calls=%async_computation.1 | async-start | bytes 589824 | tf_op jit(solution)/shard_map/while/body/eval_jaxpr/all_to_all | solution.py:56
  170.0 6.8 %all-to-all-done.1 = f32[8,72,128]{2,1,0:T(8,128)S(1)} async-done(((f32[8,72,128]{2,1,0:T(8,128)}), f32[8,72,128]{2,1,0:T(8,128)S(1)}, u32[]{:S(2)}, u32[]{:S(2)}) %all-to-all-start.1) | async-done | bytes 294944 | tf_op jit(solution)/shard_map/while/body/eval_jaxpr/all_to_all | solution.py:56
  179.5 14.0 %all_to_all.41 = f32[16,72,128]{2,1,0:T(8,128)S(1)} all-to-all(f32[16,72,128]{2,1,0:T(8,128)S(1)} %broadcast_in_dim.42), channel_id=1, replica_groups=mesh['mom'=16,'hist'=8] {'mom'}, dimensions={0} | all-to-all | bytes 1179648 | tf_op jit(solution)/shard_map/while/body/eval_jaxpr/all_to_all | solution.py:39
  193.7 1.1 convolution_bitcast_fusion.9
  194.9 1.1 convolution_bitcast_fusion.8
  197.4 3.9 %fusion.158 = f32[8,8,1024]{2,1,0:T(8,128)S(1)} fusion(f32[2,8,128,1024]{3,2,1,0:T(8,128)} %get-tuple-element.473, f32[8,4,128]{2,1,0:T(4,128)S(1)} %copy.59, f32[8,4,128]{2,1,0:T(4,128)S(1)} %copy.60), kind=kOutput, calls=%fused_computation.6.clone.1 | convolution fusion | flops 100671488 | bytes 4489216 | tf_op jit(solution)/shard_map/while/body/eval_jaxpr/kxs,kst->kxt/dot_general | solution.py:88
  201.3 2.1 fusion.157
  204.3 1.4 concatenate.74
  205.7 5.3 %all-to-all-start.1 = ((f32[8,72,128]{2,1,0:T(8,128)}), f32[8,72,128]{2,1,0:T(8,128)S(1)}, u32[]{:S(2)}, u32[]{:S(2)}) async-start(f32[8,72,128]{2,1,0:T(8,128)} %concatenate.74), calls=%async_computation.1 | async-start | bytes 589824 | tf_op jit(solution)/shard_map/while/body/eval_jaxpr/all_to_all | solution.py:56
  211.0 6.8 %all-to-all-done.1 = f32[8,72,128]{2,1,0:T(8,128)S(1)} async-done(((f32[8,72,128]{2,1,0:T(8,128)}), f32[8,72,128]{2,1,0:T(8,128)S(1)}, u32[]{:S(2)}, u32[]{:S(2)}) %all-to-all-start.1) | async-done | bytes 294944 | tf_op jit(solution)/shard_map/while/body/eval_jaxpr/all_to_all | solution.py:56
  220.5 14.1 %all_to_all.41 = f32[16,72,128]{2,1,0:T(8,128)S(1)} all-to-all(f32[16,72,128]{2,1,0:T(8,128)S(1)} %broadcast_in_dim.42), channel_id=1, replica_groups=mesh['mom'=16,'hist'=8] {'mom'}, dimensions={0} | all-to-all | bytes 1179648 | tf_op jit(solution)/shard_map/while/body/eval_jaxpr/all_to_all | solution.py:39
  234.8 1.1 convolution_bitcast_fusion.9
  235.9 1.1 convolution_bitcast_fusion.8
  238.4 3.9 %fusion.158 = f32[8,8,1024]{2,1,0:T(8,128)S(1)} fusion(f32[2,8,128,1024]{3,2,1,0:T(8,128)} %get-tuple-element.473, f32[8,4,128]{2,1,0:T(4,128)S(1)} %copy.59, f32[8,4,128]{2,1,0:T(4,128)S(1)} %copy.60), kind=kOutput, calls=%fused_computation.6.clone.1 | convolution fusion | flops 100671488 | bytes 4489216 | tf_op jit(solution)/shard_map/while/body/eval_jaxpr/kxs,kst->kxt/dot_general | solution.py:88
  242.3 2.1 fusion.157
  245.3 1.4 concatenate.74
  246.7 5.3 %all-to-all-start.1 = ((f32[8,72,128]{2,1,0:T(8,128)}), f32[8,72,128]{2,1,0:T(8,128)S(1)}, u32[]{:S(2)}, u32[]{:S(2)}) async-start(f32[8,72,128]{2,1,0:T(8,128)} %concatenate.74), calls=%async_computation.1 | async-start | bytes 589824 | tf_op jit(solution)/shard_map/while/body/eval_jaxpr/all_to_all | solution.py:56
  252.0 6.8 %all-to-all-done.1 = f32[8,72,128]{2,1,0:T(8,128)S(1)} async-done(((f32[8,72,128]{2,1,0:T(8,128)}), f32[8,72,128]{2,1,0:T(8,128)S(1)}, u32[]{:S(2)}, u32[]{:S(2)}) %all-to-all-start.1) | async-done | bytes 294944 | tf_op jit(solution)/shard_map/while/body/eval_jaxpr/all_to_all | solution.py:56
  261.5 13.9 %all_to_all.40 = f32[128,1,1]{2,1,0:T(1,128)S(1)} all-to-all(f32[128,1,1]{2,1,0:T(1,128)S(1)} %broadcast_in_dim.36), channel_id=1, replica_groups=mesh['mom'=16,'hist'=8] {'mom','hist'}, dimensions={0} | all-to-all | bytes 1024 | tf_op jit(solution)/shard_map/all_to_all | solution.py:121
  (172 shorter events, 32.7 us)
Async XLA Ops:
  2.6 25.3 %all-to-all-start.2 = ((f32[16,136,128]{2,1,0:T(8,128)}), f32[16,136,128]{2,1,0:T(8,128)S(1)}, u32[]{:S(2)}, u32[]{:S(2)}) async-start(f32[16,136,128]{2,1,0:T(8,128)} %broadcast_in_dim.35), calls=%async_computation.2 | async-start | bytes 2228224 | tf_op jit(solution)/shard_map/all_to_all | solution.py:39
  36.8 11.8 %copy-start.1 = (f32[2,8,4,128]{3,2,1,0:T(4,128)S(1)}, f32[2,8,4,128]{3,2,1,0:T(4,128)}, u32[]{:S(2)}) copy-start(f32[2,8,4,128]{3,2,1,0:T(4,128)} %param.8) | copy-start | bytes 98308
  41.6 13.7 %all-to-all-start.3 = ((f32[8,72,128]{2,1,0:T(8,128)}), f32[8,72,128]{2,1,0:T(8,128)S(1)}, u32[]{:S(2)}, u32[]{:S(2)}) async-start(f32[8,72,128]{2,1,0:T(8,128)} %concatenate.60), calls=%async_computation.3 | async-start | bytes 589824 | tf_op jit(solution)/shard_map/all_to_all | solution.py:56
  71.8 6.4 %copy-start = (f32[2,8,128,1024]{3,2,1,0:T(8,128)S(1)}, f32[2,8,128,1024]{3,2,1,0:T(8,128)}, u32[]{:S(2)}) copy-start(f32[2,8,128,1024]{3,2,1,0:T(8,128)} %get-tuple-element.473) | copy-start | bytes 25165828 | tf_op jit(solution)/shard_map/while
  82.6 12.2 %all-to-all-start.1 = ((f32[8,72,128]{2,1,0:T(8,128)}), f32[8,72,128]{2,1,0:T(8,128)S(1)}, u32[]{:S(2)}, u32[]{:S(2)}) async-start(f32[8,72,128]{2,1,0:T(8,128)} %concatenate.74), calls=%async_computation.1 | async-start | bytes 589824 | tf_op jit(solution)/shard_map/while/body/eval_jaxpr/all_to_all | solution.py:56
  112.9 6.4 %copy-start = (f32[2,8,128,1024]{3,2,1,0:T(8,128)S(1)}, f32[2,8,128,1024]{3,2,1,0:T(8,128)}, u32[]{:S(2)}) copy-start(f32[2,8,128,1024]{3,2,1,0:T(8,128)} %get-tuple-element.473) | copy-start | bytes 25165828 | tf_op jit(solution)/shard_map/while
  123.7 12.1 %all-to-all-start.1 = ((f32[8,72,128]{2,1,0:T(8,128)}), f32[8,72,128]{2,1,0:T(8,128)S(1)}, u32[]{:S(2)}, u32[]{:S(2)}) async-start(f32[8,72,128]{2,1,0:T(8,128)} %concatenate.74), calls=%async_computation.1 | async-start | bytes 589824 | tf_op jit(solution)/shard_map/while/body/eval_jaxpr/all_to_all | solution.py:56
  153.9 6.4 %copy-start = (f32[2,8,128,1024]{3,2,1,0:T(8,128)S(1)}, f32[2,8,128,1024]{3,2,1,0:T(8,128)}, u32[]{:S(2)}) copy-start(f32[2,8,128,1024]{3,2,1,0:T(8,128)} %get-tuple-element.473) | copy-start | bytes 25165828 | tf_op jit(solution)/shard_map/while
  164.7 12.2 %all-to-all-start.1 = ((f32[8,72,128]{2,1,0:T(8,128)}), f32[8,72,128]{2,1,0:T(8,128)S(1)}, u32[]{:S(2)}, u32[]{:S(2)}) async-start(f32[8,72,128]{2,1,0:T(8,128)} %concatenate.74), calls=%async_computation.1 | async-start | bytes 589824 | tf_op jit(solution)/shard_map/while/body/eval_jaxpr/all_to_all | solution.py:56
  194.9 6.4 %copy-start = (f32[2,8,128,1024]{3,2,1,0:T(8,128)S(1)}, f32[2,8,128,1024]{3,2,1,0:T(8,128)}, u32[]{:S(2)}) copy-start(f32[2,8,128,1024]{3,2,1,0:T(8,128)} %get-tuple-element.473) | copy-start | bytes 25165828 | tf_op jit(solution)/shard_map/while
  205.7 12.1 %all-to-all-start.1 = ((f32[8,72,128]{2,1,0:T(8,128)}), f32[8,72,128]{2,1,0:T(8,128)S(1)}, u32[]{:S(2)}, u32[]{:S(2)}) async-start(f32[8,72,128]{2,1,0:T(8,128)} %concatenate.74), calls=%async_computation.1 | async-start | bytes 589824 | tf_op jit(solution)/shard_map/while/body/eval_jaxpr/all_to_all | solution.py:56
  235.9 6.4 %copy-start = (f32[2,8,128,1024]{3,2,1,0:T(8,128)S(1)}, f32[2,8,128,1024]{3,2,1,0:T(8,128)}, u32[]{:S(2)}) copy-start(f32[2,8,128,1024]{3,2,1,0:T(8,128)} %get-tuple-element.473) | copy-start | bytes 25165828 | tf_op jit(solution)/shard_map/while
  246.7 12.1 %all-to-all-start.1 = ((f32[8,72,128]{2,1,0:T(8,128)}), f32[8,72,128]{2,1,0:T(8,128)S(1)}, u32[]{:S(2)}, u32[]{:S(2)}) async-start(f32[8,72,128]{2,1,0:T(8,128)} %concatenate.74), calls=%async_computation.1 | async-start | bytes 589824 | tf_op jit(solution)/shard_map/while/body/eval_jaxpr/all_to_all | solution.py:56
  277.5 0.5 copy-start.2

commit v2 on v1

--- a/solution.py
+++ b/solution.py
@@ -3,6 +3,8 @@
 import jax
 import jax.numpy as jnp
 from jax import lax
+from jax.experimental import pallas as pl
+from jax.experimental.pallas import tpu as pltpu
 from jax.sharding import PartitionSpec as P
 
 K = 128
@@ -59,6 +61,51 @@
     return s[:n].reshape(two, kl, rr, cols), s[n, 0]
 
 
+def contract_kernel(x_ref, e_ref, p_hbm, o_ref, buf, sem):
+    k_local = x_ref.shape[0]
+    hist_n = o_ref.shape[0]
+    copies = [pltpu.make_async_copy(p_hbm.at[:, k], buf.at[k], sem.at[k]) for k in range(k_local)]
+    for c in copies:
+        c.start()
+    n = 2 * k_local * R
+    o_ref[:, n:, :] = jnp.full((hist_n, o_ref.shape[1] - n, 128), e_ref[0], jnp.float32)
+    for k in range(k_local):
+        copies[k].wait()
+        xk = x_ref[k]
+        a = jnp.dot(xk, buf[k, 0], precision=HIGHEST, preferred_element_type=jnp.float32)
+        b = jnp.dot(xk, buf[k, 1], precision=HIGHEST, preferred_element_type=jnp.float32)
+        real = a[:R] - b[R:]
+        imag = b[:R] + a[R:]
+        for h in range(hist_n):
+            o_ref[h, k * R:(k + 1) * R, :] = real[:, h * 128:(h + 1) * 128]
+            o_ref[h, n // 2 + k * R:n // 2 + (k + 1) * R, :] = imag[:, h * 128:(h + 1) * 128]
+
+
+def contract_packed(x, extra, hist_panel, hist_n):
+    k_local = x.shape[0]
+    rows = 2 * k_local * R + 8
+    return pl.pallas_call(
+        contract_kernel,
+        out_shape=jax.ShapeDtypeStruct((hist_n, rows, 128), jnp.float32),
+        in_specs=[
+            pl.BlockSpec(memory_space=pltpu.VMEM),
+            pl.BlockSpec(memory_space=pltpu.SMEM),
+            pl.BlockSpec(memory_space=pl.ANY),
+        ],
+        out_specs=pl.BlockSpec(memory_space=pltpu.VMEM),
+        scratch_shapes=[
+            pltpu.VMEM((k_local,) + hist_panel.shape[0:1] + hist_panel.shape[2:], jnp.float32),
+            pltpu.SemaphoreType.DMA((k_local,)),
+        ],
+    )(x, extra.reshape(1), hist_panel)
+
+
+def hist_reduce_packed(packed, n):
+    y = lax.all_to_all(packed, "hist", 0, 0, tiled=True)
+    s = jnp.sum(y, axis=0)
+    return s[:n], s[n, 0]
+
+
 def shards(hist_panel, free_rows, screened):
     _, k_local, _, cols = free_rows.shape
     hist_n = hist_panel.shape[3] // cols
@@ -98,14 +145,21 @@
     green_full = to_full_k(rows[:, half:], 2, k_local, cols)
     screen_hat = dft(cosine, sine, screen_full[0], screen_full[1])
 
-    integral, _ = hist_reduce(contract(sigma_of(green_full)), jnp.float32(0.0), hist_n)
+    def integral_of(full, extra):
+        sigma = sigma_of(full)
+        x = jnp.concatenate([sigma[0], sigma[1]], axis=1)
+        packed = contract_packed(x, extra, hist_panel, hist_n)
+        got, total = hist_reduce_packed(packed, 2 * k_local * R)
+        return got.reshape(2, k_local, R, cols), total
+
+    integral, _ = integral_of(green_full, jnp.float32(0.0))
     def correction(turn, carry):
         green, integral, deltas = carry
         change = free_rows + step_size * integral - green
         local = jnp.sum(change * change)
         rows, mom_sum = gather_rows(change.reshape(-1, 128), local)
         full = to_full_k(rows, 2, k_local, cols)
-        step, total = hist_reduce(contract(sigma_of(full)), mom_sum, hist_n)
+        step, total = integral_of(full, mom_sum)
         delta = jnp.sqrt(total / (2.0 * K * R * full_hist))
         deltas = lax.dynamic_update_slice(deltas, delta[None], (turn,))
         green = green + change / (1.0 + delta)

time: 279 us -> 283 us (1.014)
  Pallas kernels: 0 us -> 46.6 us
  matrix products: 59.2 us -> 21.5 us
  local copies, waits for them, and re-layouts: 18.6 us -> 10 us
  other arithmetic: 10.7 us -> 14.3 us
    pallas_call x0 -> x6, Pallas kernels: none -> 46.6 us  [contract_packed(): pl.pallas_call(contract_kernel, out_shape=jax.ShapeDtypeStruct((hist_n, r...]
    dot_general x12 -> x0, matrix products: 37.8 us -> none  [the longest x6 23.5 us: contract(): a = jnp.einsum('kxs,kst->kxt', x, hist_panel[0], precision=HIGHEST)]
    concatenate x6 -> x0, local copies, waits for them, and re-layouts: 7.59 us -> none  [hist_reduce(): x = jnp.concatenate([x, jnp.full((hist_n, 8, 128), extra, x.dtype)], axis=1)]
    concatenate x0 -> x6, other arithmetic: none -> 3.76 us  [integral_of(): x = jnp.concatenate([sigma[0], sigma[1]], axis=1)]
where the time goes in v2:
time: 283 us; the launch traced here: 282 us
  blocking collectives  83.9 us (30%)
  waiting for transfers between devices  57.3 us (20%)
  Pallas kernels  46.6 us (16%)
  starting transfers between devices  42.4 us (15%)
  matrix products  21.5 us (8%)
  other arithmetic  14.3 us (5%)
  local copies, waits for them, and re-layouts  10 us (4%)
  loops' own time  4.17 us (1%)
    all_to_all x5, blocking collectives, gather_rows(): lax.all_to_all(jnp.broadcast_to(packed, (n_mom,) + packed.shape), 'mom',...  69.9 us
    pallas_call x6, Pallas kernels, contract_packed(): pl.pallas_call(contract_kernel, out_shape=jax.ShapeDtypeStruct((hist_n, r...  46.6 us
    all_to_all x6, waiting for transfers between devices, hist_reduce_packed(): y = lax.all_to_all(packed, 'hist', 0, 0, tiled=True)  40.5 us
    all_to_all x6, starting transfers between devices, hist_reduce_packed(): y = lax.all_to_all(packed, 'hist', 0, 0, tiled=True)  33.8 us
    dot_general x26, matrix products, mm(): return jnp.dot(table, field, precision=HIGHEST)  21.5 us
    all_to_all x1, waiting for transfers between devices, gather_rows(): lax.all_to_all(jnp.broadcast_to(packed, (n_mom,) + packed.shape), 'mom',...  16.7 us
    all_to_all x1, blocking collectives, shards(): total = jnp.sum(lax.all_to_all(spread, ('mom', 'hist'), 0, 0, tiled=True))  13.9 us
    all_to_all x1, starting transfers between devices, gather_rows(): lax.all_to_all(jnp.broadcast_to(packed, (n_mom,) + packed.shape), 'mom',...  8.59 us
  transfers between devices with their start and end apart: 7, of which 7 were waited for; matrix products, arithmetic and copies ran while one was open for 0% of the time, Pallas kernels for 0%

profile of v2, /device:TPU:1, one launch (start us, length us, event | category | flops | bytes accessed | tf_op | source)
XLA Modules:
  0.0 281.6 jit_solution(6480441688149964355)
XLA Ops:
  0.7 0.9 maximum_maximum_fusion
  1.5 1.1 broadcast_in_dim.31
  2.6 8.6 %all-to-all-start.2 = ((f32[16,136,128]{2,1,0:T(8,128)}), f32[16,136,128]{2,1,0:T(8,128)S(1)}, u32[]{:S(2)}, u32[]{:S(2)}) async-start(f32[16,136,128]{2,1,0:T(8,128)} %broadcast_in_dim.31), calls=%async_computation.2 | async-start | bytes 2228224 | tf_op jit(solution)/shard_map/all_to_all | solution.py:41
  11.2 16.7 %all-to-all-done.2 = f32[16,136,128]{2,1,0:T(8,128)S(1)} async-done(((f32[16,136,128]{2,1,0:T(8,128)}), f32[16,136,128]{2,1,0:T(8,128)S(1)}, u32[]{:S(2)}, u32[]{:S(2)}) %all-to-all-start.2) | async-done | bytes 1114144 | tf_op jit(solution)/shard_map/all_to_all | solution.py:41
  28.2 0.8 fusion.60
  29.0 0.8 fusion.59
  30.0 0.8 fusion.58
  30.9 0.8 fusion.57
  33.6 7.2 %shard_map.50 = f32[8,72,128]{2,1,0:T(8,128)} custom-call(f32[8,8,128]{2,1,0:T(8,128)} %pad_maximum_fusion.16.x_ref, f32[1]{0:T(128)} %constant.118.clone.1.e_ref, f32[2,8,128,1024]{3,2,1,0:T(8,128)} %p_hbm.1), custom_call_target="tpu_custom_call" | custom-call | tf_op jit(solution)/shard_map/pallas_call | solution.py:87
  40.8 7.0 %all-to-all-start.3 = ((f32[8,72,128]{2,1,0:T(8,128)}), f32[8,72,128]{2,1,0:T(8,128)S(1)}, u32[]{:S(2)}, u32[]{:S(2)}) async-start(f32[8,72,128]{2,1,0:T(8,128)} %shard_map.50), calls=%async_computation.3 | async-start | bytes 589824 | tf_op jit(solution)/shard_map/all_to_all | solution.py:104
  48.1 6.5 %all-to-all-done.3 = f32[8,72,128]{2,1,0:T(8,128)S(1)} async-done(((f32[8,72,128]{2,1,0:T(8,128)}), f32[8,72,128]{2,1,0:T(8,128)S(1)}, u32[]{:S(2)}, u32[]{:S(2)}) %all-to-all-start.3) | async-done | bytes 294944 | tf_op jit(solution)/shard_map/all_to_all | solution.py:104
  54.7 209.2 %while.20 = (s32[]{:T(128)}, f32[2,8,4,128]{3,2,1,0:T(4,128)S(1)}, f32[2,8,4,128]{3,2,1,0:T(4,128)S(1)}, f32[6]{0:T(128)S(1)}, f32[2,8,4,128]{3,2,1,0:T(4,128)S(...) while((s32[]{:T(128)}, f32[2,8,4,128]{3,2,1,0:T(4,128)S(1)}, ...), condition=%wide.region_5.6_spmd.clone.clone, body=%wide.region_1.5_spmd.clone.clone.sunk | while | flops 429515776 | bytes 12169605 | solution.py:170
  56.0 13.7 %all_to_all.41 = f32[16,72,128]{2,1,0:T(8,128)S(1)} all-to-all(f32[16,72,128]{2,1,0:T(8,128)S(1)} %broadcast_in_dim.38), channel_id=1, replica_groups=mesh['mom'=16,'hist'=8] {'mom'}, dimensions={0} | all-to-all | bytes 1179648 | tf_op jit(solution)/shard_map/while/body/eval_jaxpr/all_to_all | solution.py:41
  69.9 1.1 convolution_bitcast_fusion.9
  71.0 1.1 convolution_bitcast_fusion.8
  74.1 0.7 slice_reduce_fusion.2
  74.8 7.9 %eval_jaxpr.5 = f32[8,72,128]{2,1,0:T(8,128)} custom-call(f32[8,8,128]{2,1,0:T(8,128)} %pad_maximum_fusion.26.x_ref, f32[1]{0:T(128)} %bitcast.60.e_ref, f32[2,8,128,1024]{3,2,1,0:T(8,128)} %get-tuple-element.454.p_hbm), custom_call_target="tpu_custom_call" | custom-call | tf_op jit(solution)/shard_map/while/body/eval_jaxpr/pallas_call | solution.py:87
  82.7 5.4 %all-to-all-start.1 = ((f32[8,72,128]{2,1,0:T(8,128)}), f32[8,72,128]{2,1,0:T(8,128)S(1)}, u32[]{:S(2)}, u32[]{:S(2)}) async-start(f32[8,72,128]{2,1,0:T(8,128)} %eval_jaxpr.5), calls=%async_computation.1 | async-start | bytes 589824 | tf_op jit(solution)/shard_map/while/body/eval_jaxpr/all_to_all | solution.py:104
  88.1 6.8 %all-to-all-done.1 = f32[8,72,128]{2,1,0:T(8,128)S(1)} async-done(((f32[8,72,128]{2,1,0:T(8,128)}), f32[8,72,128]{2,1,0:T(8,128)S(1)}, u32[]{:S(2)}, u32[]{:S(2)}) %all-to-all-start.1) | async-done | bytes 294944 | tf_op jit(solution)/shard_map/while/body/eval_jaxpr/all_to_all | solution.py:104
  97.6 14.1 %all_to_all.41 = f32[16,72,128]{2,1,0:T(8,128)S(1)} all-to-all(f32[16,72,128]{2,1,0:T(8,128)S(1)} %broadcast_in_dim.38), channel_id=1, replica_groups=mesh['mom'=16,'hist'=8] {'mom'}, dimensions={0} | all-to-all | bytes 1179648 | tf_op jit(solution)/shard_map/while/body/eval_jaxpr/all_to_all | solution.py:41
  111.8 1.1 convolution_bitcast_fusion.9
  113.0 1.1 convolution_bitcast_fusion.8
  116.1 0.7 slice_reduce_fusion.2
  116.8 7.9 %eval_jaxpr.5 = f32[8,72,128]{2,1,0:T(8,128)} custom-call(f32[8,8,128]{2,1,0:T(8,128)} %pad_maximum_fusion.26.x_ref, f32[1]{0:T(128)} %bitcast.60.e_ref, f32[2,8,128,1024]{3,2,1,0:T(8,128)} %get-tuple-element.454.p_hbm), custom_call_target="tpu_custom_call" | custom-call | tf_op jit(solution)/shard_map/while/body/eval_jaxpr/pallas_call | solution.py:87
  124.7 5.4 %all-to-all-start.1 = ((f32[8,72,128]{2,1,0:T(8,128)}), f32[8,72,128]{2,1,0:T(8,128)S(1)}, u32[]{:S(2)}, u32[]{:S(2)}) async-start(f32[8,72,128]{2,1,0:T(8,128)} %eval_jaxpr.5), calls=%async_computation.1 | async-start | bytes 589824 | tf_op jit(solution)/shard_map/while/body/eval_jaxpr/all_to_all | solution.py:104
  130.0 6.8 %all-to-all-done.1 = f32[8,72,128]{2,1,0:T(8,128)S(1)} async-done(((f32[8,72,128]{2,1,0:T(8,128)}), f32[8,72,128]{2,1,0:T(8,128)S(1)}, u32[]{:S(2)}, u32[]{:S(2)}) %all-to-all-start.1) | async-done | bytes 294944 | tf_op jit(solution)/shard_map/while/body/eval_jaxpr/all_to_all | solution.py:104
  139.5 14.1 %all_to_all.41 = f32[16,72,128]{2,1,0:T(8,128)S(1)} all-to-all(f32[16,72,128]{2,1,0:T(8,128)S(1)} %broadcast_in_dim.38), channel_id=1, replica_groups=mesh['mom'=16,'hist'=8] {'mom'}, dimensions={0} | all-to-all | bytes 1179648 | tf_op jit(solution)/shard_map/while/body/eval_jaxpr/all_to_all | solution.py:41
  153.7 1.1 convolution_bitcast_fusion.9
  154.9 1.1 convolution_bitcast_fusion.8
  158.0 0.7 slice_reduce_fusion.2
  158.7 7.9 %eval_jaxpr.5 = f32[8,72,128]{2,1,0:T(8,128)} custom-call(f32[8,8,128]{2,1,0:T(8,128)} %pad_maximum_fusion.26.x_ref, f32[1]{0:T(128)} %bitcast.60.e_ref, f32[2,8,128,1024]{3,2,1,0:T(8,128)} %get-tuple-element.454.p_hbm), custom_call_target="tpu_custom_call" | custom-call | tf_op jit(solution)/shard_map/while/body/eval_jaxpr/pallas_call | solution.py:87
  166.5 5.4 %all-to-all-start.1 = ((f32[8,72,128]{2,1,0:T(8,128)}), f32[8,72,128]{2,1,0:T(8,128)S(1)}, u32[]{:S(2)}, u32[]{:S(2)}) async-start(f32[8,72,128]{2,1,0:T(8,128)} %eval_jaxpr.5), calls=%async_computation.1 | async-start | bytes 589824 | tf_op jit(solution)/shard_map/while/body/eval_jaxpr/all_to_all | solution.py:104
  171.9 6.8 %all-to-all-done.1 = f32[8,72,128]{2,1,0:T(8,128)S(1)} async-done(((f32[8,72,128]{2,1,0:T(8,128)}), f32[8,72,128]{2,1,0:T(8,128)S(1)}, u32[]{:S(2)}, u32[]{:S(2)}) %all-to-all-start.1) | async-done | bytes 294944 | tf_op jit(solution)/shard_map/while/body/eval_jaxpr/all_to_all | solution.py:104
  181.4 14.0 %all_to_all.41 = f32[16,72,128]{2,1,0:T(8,128)S(1)} all-to-all(f32[16,72,128]{2,1,0:T(8,128)S(1)} %broadcast_in_dim.38), channel_id=1, replica_groups=mesh['mom'=16,'hist'=8] {'mom'}, dimensions={0} | all-to-all | bytes 1179648 | tf_op jit(solution)/shard_map/while/body/eval_jaxpr/all_to_all | solution.py:41
  195.6 1.1 convolution_bitcast_fusion.9
  196.7 1.1 convolution_bitcast_fusion.8
  199.8 0.7 slice_reduce_fusion.2
  200.5 7.9 %eval_jaxpr.5 = f32[8,72,128]{2,1,0:T(8,128)} custom-call(f32[8,8,128]{2,1,0:T(8,128)} %pad_maximum_fusion.26.x_ref, f32[1]{0:T(128)} %bitcast.60.e_ref, f32[2,8,128,1024]{3,2,1,0:T(8,128)} %get-tuple-element.454.p_hbm), custom_call_target="tpu_custom_call" | custom-call | tf_op jit(solution)/shard_map/while/body/eval_jaxpr/pallas_call | solution.py:87
  208.4 5.4 %all-to-all-start.1 = ((f32[8,72,128]{2,1,0:T(8,128)}), f32[8,72,128]{2,1,0:T(8,128)S(1)}, u32[]{:S(2)}, u32[]{:S(2)}) async-start(f32[8,72,128]{2,1,0:T(8,128)} %eval_jaxpr.5), calls=%async_computation.1 | async-start | bytes 589824 | tf_op jit(solution)/shard_map/while/body/eval_jaxpr/all_to_all | solution.py:104
  213.8 6.8 %all-to-all-done.1 = f32[8,72,128]{2,1,0:T(8,128)S(1)} async-done(((f32[8,72,128]{2,1,0:T(8,128)}), f32[8,72,128]{2,1,0:T(8,128)S(1)}, u32[]{:S(2)}, u32[]{:S(2)}) %all-to-all-start.1) | async-done | bytes 294944 | tf_op jit(solution)/shard_map/while/body/eval_jaxpr/all_to_all | solution.py:104
  223.3 14.1 %all_to_all.41 = f32[16,72,128]{2,1,0:T(8,128)S(1)} all-to-all(f32[16,72,128]{2,1,0:T(8,128)S(1)} %broadcast_in_dim.38), channel_id=1, replica_groups=mesh['mom'=16,'hist'=8] {'mom'}, dimensions={0} | all-to-all | bytes 1179648 | tf_op jit(solution)/shard_map/while/body/eval_jaxpr/all_to_all | solution.py:41
  237.5 1.1 convolution_bitcast_fusion.9
  238.6 1.1 convolution_bitcast_fusion.8
  242.4 7.9 %eval_jaxpr.5 = f32[8,72,128]{2,1,0:T(8,128)} custom-call(f32[8,8,128]{2,1,0:T(8,128)} %pad_maximum_fusion.26.x_ref, f32[1]{0:T(128)} %bitcast.60.e_ref, f32[2,8,128,1024]{3,2,1,0:T(8,128)} %get-tuple-element.454.p_hbm), custom_call_target="tpu_custom_call" | custom-call | tf_op jit(solution)/shard_map/while/body/eval_jaxpr/pallas_call | solution.py:87
  250.3 5.4 %all-to-all-start.1 = ((f32[8,72,128]{2,1,0:T(8,128)}), f32[8,72,128]{2,1,0:T(8,128)S(1)}, u32[]{:S(2)}, u32[]{:S(2)}) async-start(f32[8,72,128]{2,1,0:T(8,128)} %eval_jaxpr.5), calls=%async_computation.1 | async-start | bytes 589824 | tf_op jit(solution)/shard_map/while/body/eval_jaxpr/all_to_all | solution.py:104
  255.7 6.8 %all-to-all-done.1 = f32[8,72,128]{2,1,0:T(8,128)S(1)} async-done(((f32[8,72,128]{2,1,0:T(8,128)}), f32[8,72,128]{2,1,0:T(8,128)S(1)}, u32[]{:S(2)}, u32[]{:S(2)}) %all-to-all-start.1) | async-done | bytes 294944 | tf_op jit(solution)/shard_map/while/body/eval_jaxpr/all_to_all | solution.py:104
  265.1 13.9 %all_to_all.40 = f32[128,1,1]{2,1,0:T(1,128)S(1)} all-to-all(f32[128,1,1]{2,1,0:T(1,128)S(1)} %broadcast_in_dim.32), channel_id=1, replica_groups=mesh['mom'=16,'hist'=8] {'mom','hist'}, dimensions={0} | all-to-all | bytes 1024 | tf_op jit(solution)/shard_map/all_to_all | solution.py:175
  279.1 0.7 reduce_sum.68
  (126 shorter events, 25.8 us)
Async XLA Ops:
  2.6 25.3 %all-to-all-start.2 = ((f32[16,136,128]{2,1,0:T(8,128)}), f32[16,136,128]{2,1,0:T(8,128)S(1)}, u32[]{:S(2)}, u32[]{:S(2)}) async-start(f32[16,136,128]{2,1,0:T(8,128)} %broadcast_in_dim.31), calls=%async_computation.2 | async-start | bytes 2228224 | tf_op jit(solution)/shard_map/all_to_all | solution.py:41
  33.6 14.2 %copy-start = (f32[2,8,4,128]{3,2,1,0:T(4,128)S(1)}, f32[2,8,4,128]{3,2,1,0:T(4,128)}, u32[]{:S(2)}) copy-start(f32[2,8,4,128]{3,2,1,0:T(4,128)} %param.8) | copy-start | bytes 98308
  40.8 13.8 %all-to-all-start.3 = ((f32[8,72,128]{2,1,0:T(8,128)}), f32[8,72,128]{2,1,0:T(8,128)S(1)}, u32[]{:S(2)}, u32[]{:S(2)}) async-start(f32[8,72,128]{2,1,0:T(8,128)} %shard_map.50), calls=%async_computation.3 | async-start | bytes 589824 | tf_op jit(solution)/shard_map/all_to_all | solution.py:104
  82.7 12.2 %all-to-all-start.1 = ((f32[8,72,128]{2,1,0:T(8,128)}), f32[8,72,128]{2,1,0:T(8,128)S(1)}, u32[]{:S(2)}, u32[]{:S(2)}) async-start(f32[8,72,128]{2,1,0:T(8,128)} %eval_jaxpr.5), calls=%async_computation.1 | async-start | bytes 589824 | tf_op jit(solution)/shard_map/while/body/eval_jaxpr/all_to_all | solution.py:104
  124.7 12.2 %all-to-all-start.1 = ((f32[8,72,128]{2,1,0:T(8,128)}), f32[8,72,128]{2,1,0:T(8,128)S(1)}, u32[]{:S(2)}, u32[]{:S(2)}) async-start(f32[8,72,128]{2,1,0:T(8,128)} %eval_jaxpr.5), calls=%async_computation.1 | async-start | bytes 589824 | tf_op jit(solution)/shard_map/while/body/eval_jaxpr/all_to_all | solution.py:104
  166.5 12.2 %all-to-all-start.1 = ((f32[8,72,128]{2,1,0:T(8,128)}), f32[8,72,128]{2,1,0:T(8,128)S(1)}, u32[]{:S(2)}, u32[]{:S(2)}) async-start(f32[8,72,128]{2,1,0:T(8,128)} %eval_jaxpr.5), calls=%async_computation.1 | async-start | bytes 589824 | tf_op jit(solution)/shard_map/while/body/eval_jaxpr/all_to_all | solution.py:104
  208.4 12.2 %all-to-all-start.1 = ((f32[8,72,128]{2,1,0:T(8,128)}), f32[8,72,128]{2,1,0:T(8,128)S(1)}, u32[]{:S(2)}, u32[]{:S(2)}) async-start(f32[8,72,128]{2,1,0:T(8,128)} %eval_jaxpr.5), calls=%async_computation.1 | async-start | bytes 589824 | tf_op jit(solution)/shard_map/while/body/eval_jaxpr/all_to_all | solution.py:104
  250.3 12.2 %all-to-all-start.1 = ((f32[8,72,128]{2,1,0:T(8,128)}), f32[8,72,128]{2,1,0:T(8,128)S(1)}, u32[]{:S(2)}, u32[]{:S(2)}) async-start(f32[8,72,128]{2,1,0:T(8,128)} %eval_jaxpr.5), calls=%async_computation.1 | async-start | bytes 589824 | tf_op jit(solution)/shard_map/while/body/eval_jaxpr/all_to_all | solution.py:104
  281.1 0.5 copy-start.1

commit v3 on v1

--- a/solution.py
+++ b/solution.py
@@ -21,14 +21,15 @@
     return (jnp.cos(phase), jnp.sin(phase))
 
 
-def mm(table, field):
-    return jnp.dot(table, field, precision=HIGHEST)
+def mm(table, field, precision=HIGHEST):
+    return jnp.dot(table, field, precision=precision)
 
 
-def dft(cosine, sine, real, imag):
+def dft(cosine, sine, real, imag, precision=HIGHEST):
     both = jnp.concatenate([real, imag], axis=1)
-    cr = mm(cosine, both)
-    sr = mm(sine, both)
+    out = mm(jnp.concatenate([cosine, sine]), both, precision)
+    cr = out[: cosine.shape[0]]
+    sr = out[cosine.shape[0]:]
     n = real.shape[1]
     return (cr[:, :n] + sr[:, n:], cr[:, n:] - sr[:, :n])
 
@@ -72,12 +73,13 @@
     nb = 2 * k_local * R * cols
 
     def sigma_of(full):
-        hr, hi = dft(cosine, sine, full[0], full[1])
+        hr, hi = dft(cosine, sine, full[0], full[1], lax.Precision.HIGH)
         pr = hr * screen_hat[0] - hi * screen_hat[1]
         pi = hr * screen_hat[1] + hi * screen_hat[0]
         both = jnp.concatenate([pr, pi], axis=1)
-        cb = mm(cos_own, both)
-        sb = mm(sin_own, both)
+        out = mm(jnp.concatenate([cos_own, sin_own]), both, lax.Precision.HIGH)
+        cb = out[:k_local]
+        sb = out[k_local:]
         n = pr.shape[1]
         back_real = cb[:, :n] - sb[:, n:]
         back_imag = cb[:, n:] + sb[:, :n]

time: 279 us -> 266 us (0.953)
  matrix products: 59.2 us -> 45.7 us
    dot_general x26 -> x13, matrix products: 21.5 us -> 6.48 us  [mm(): return jnp.dot(table, field, precision=precision)]
where the time goes in v3:
time: 266 us; the launch traced here: 265 us
  blocking collectives  83.9 us (32%)
  waiting for transfers between devices  56.8 us (21%)
  matrix products  45.7 us (17%)
  starting transfers between devices  42.3 us (16%)
  local copies, waits for them, and re-layouts  18.6 us (7%)
  other arithmetic  11.2 us (4%)
  loops' own time  4.39 us (2%)
    all_to_all x5, blocking collectives, gather_rows(): lax.all_to_all(jnp.broadcast_to(packed, (n_mom,) + packed.shape), 'mom',...  69.9 us
    all_to_all x6, waiting for transfers between devices, hist_reduce(): y = lax.all_to_all(x, 'hist', 0, 0, tiled=True)  40.5 us
    all_to_all x6, starting transfers between devices, hist_reduce(): y = lax.all_to_all(x, 'hist', 0, 0, tiled=True)  33.7 us
    dot_general x6, matrix products, contract(): a = jnp.einsum('kxs,kst->kxt', x, hist_panel[0], precision=HIGHEST)  25 us
    all_to_all x1, waiting for transfers between devices, gather_rows(): lax.all_to_all(jnp.broadcast_to(packed, (n_mom,) + packed.shape), 'mom',...  16.3 us
    dot_general x6, matrix products, contract(): b = jnp.einsum('kxs,kst->kxt', x, hist_panel[1], precision=HIGHEST)  14.2 us
    all_to_all x1, blocking collectives, shards(): total = jnp.sum(lax.all_to_all(spread, ('mom', 'hist'), 0, 0, tiled=True))  13.9 us
    all_to_all x1, starting transfers between devices, gather_rows(): lax.all_to_all(jnp.broadcast_to(packed, (n_mom,) + packed.shape), 'mom',...  8.59 us
  transfers between devices with their start and end apart: 7, of which 7 were waited for; matrix products, arithmetic and copies ran while one was open for 0% of the time, Pallas kernels for 0%

profile of v3, /device:TPU:1, one launch (start us, length us, event | category | flops | bytes accessed | tf_op | source)
XLA Modules:
  0.0 264.5 jit_solution(7169084209290886036)
XLA Ops:
  0.7 0.9 maximum_maximum_fusion
  1.5 1.1 broadcast_in_dim.39
  2.6 8.6 %all-to-all-start.2 = ((f32[16,136,128]{2,1,0:T(8,128)}), f32[16,136,128]{2,1,0:T(8,128)S(1)}, u32[]{:S(2)}, u32[]{:S(2)}) async-start(f32[16,136,128]{2,1,0:T(8,128)} %broadcast_in_dim.39), calls=%async_computation.2 | async-start | bytes 2228224 | tf_op jit(solution)/shard_map/all_to_all | solution.py:40
  11.6 16.3 %all-to-all-done.2 = f32[16,136,128]{2,1,0:T(8,128)S(1)} async-done(((f32[16,136,128]{2,1,0:T(8,128)}), f32[16,136,128]{2,1,0:T(8,128)S(1)}, u32[]{:S(2)}, u32[]{:S(2)}) %all-to-all-start.2) | async-done | bytes 1114144 | tf_op jit(solution)/shard_map/all_to_all | solution.py:40
  28.9 1.0 fusion.29
  30.5 3.8 %fusion.21 = f32[8,8,1024]{2,1,0:T(8,128)S(1)} fusion(f32[2,8,128,1024]{3,2,1,0:T(8,128)} %param.7, f32[8,4,128]{2,1,0:T(4,128)S(1)} %copy.49, f32[8,4,128]{2,1,0:T(4,128)S(1)} %copy.48), kind=kOutput, calls=%fused_computation.41 | convolution fusion | flops 100671488 | bytes 4489216 | tf_op jit(solution)/shard_map/kxs,kst->kxt/dot_general | solution.py:90
  34.4 3.8 %fusion.19 = f32[8,8,1024]{2,1,0:T(8,128)S(1)} fusion(f32[2,8,128,1024]{3,2,1,0:T(8,128)} %param.7, f32[8,4,128]{2,1,0:T(4,128)S(1)} %copy.49, f32[8,4,128]{2,1,0:T(4,128)S(1)} %copy.48), kind=kOutput, calls=%fused_computation.39 | convolution fusion | flops 100671488 | bytes 4489216 | tf_op jit(solution)/shard_map/kxs,kst->kxt/dot_general | solution.py:91
  38.5 0.7 concatenate.91
  39.2 7.0 %all-to-all-start.3 = ((f32[8,72,128]{2,1,0:T(8,128)}), f32[8,72,128]{2,1,0:T(8,128)S(1)}, u32[]{:S(2)}, u32[]{:S(2)}) async-start(f32[8,72,128]{2,1,0:T(8,128)} %concatenate.91), calls=%async_computation.3 | async-start | bytes 589824 | tf_op jit(solution)/shard_map/all_to_all | solution.py:57
  46.5 6.5 %all-to-all-done.3 = f32[8,72,128]{2,1,0:T(8,128)S(1)} async-done(((f32[8,72,128]{2,1,0:T(8,128)}), f32[8,72,128]{2,1,0:T(8,128)S(1)}, u32[]{:S(2)}, u32[]{:S(2)}) %all-to-all-start.3) | async-done | bytes 294944 | tf_op jit(solution)/shard_map/all_to_all | solution.py:57
  53.0 193.7 %while.20 = (s32[]{:T(128)}, f32[2,8,4,128]{3,2,1,0:T(4,128)S(1)}, f32[2,8,4,128]{3,2,1,0:T(4,128)S(1)}, f32[6]{0:T(128)S(1)}, f32[2,8,4,128]{3,2,1,0:T(4,128)S(...) while((s32[]{:T(128)}, f32[2,8,4,128]{3,2,1,0:T(4,128)S(1)}, ...), condition=%wide.region_5.6_spmd, body=%wide.region_1.5_spmd.sunk | while | flops 416320512 | bytes 56643948 | solution.py:118
  53.6 0.6 concatenate.94
  54.3 13.7 %all_to_all.41 = f32[16,72,128]{2,1,0:T(8,128)S(1)} all-to-all(f32[16,72,128]{2,1,0:T(8,128)S(1)} %broadcast_in_dim.42), channel_id=1, replica_groups=mesh['mom'=16,'hist'=8] {'mom'}, dimensions={0} | all-to-all | bytes 1179648 | tf_op jit(solution)/shard_map/while/body/eval_jaxpr/all_to_all | solution.py:40
  69.3 4.2 %fusion.79 = f32[8,8,1024]{2,1,0:T(8,128)S(1)} fusion(f32[2,8,128,1024]{3,2,1,0:T(8,128)} %get-tuple-element.515, f32[8,4,128]{2,1,0:T(4,128)S(1)} %copy.59, f32[8,4,128]{2,1,0:T(4,128)S(1)} %copy.60), kind=kOutput, calls=%fused_computation.2.clone.1 | convolution fusion | flops 100671488 | bytes 4489216 | tf_op jit(solution)/shard_map/while/body/eval_jaxpr/kxs,kst->kxt/dot_general | solution.py:90
  73.6 2.1 fusion.78
  76.6 1.4 concatenate.95
  78.0 5.4 %all-to-all-start.1 = ((f32[8,72,128]{2,1,0:T(8,128)}), f32[8,72,128]{2,1,0:T(8,128)S(1)}, u32[]{:S(2)}, u32[]{:S(2)}) async-start(f32[8,72,128]{2,1,0:T(8,128)} %concatenate.95), calls=%async_computation.1 | async-start | bytes 589824 | tf_op jit(solution)/shard_map/while/body/eval_jaxpr/all_to_all | solution.py:57
  83.3 6.8 %all-to-all-done.1 = f32[8,72,128]{2,1,0:T(8,128)S(1)} async-done(((f32[8,72,128]{2,1,0:T(8,128)}), f32[8,72,128]{2,1,0:T(8,128)S(1)}, u32[]{:S(2)}, u32[]{:S(2)}) %all-to-all-start.1) | async-done | bytes 294944 | tf_op jit(solution)/shard_map/while/body/eval_jaxpr/all_to_all | solution.py:57
  92.1 0.6 concatenate.94
  92.8 14.1 %all_to_all.41 = f32[16,72,128]{2,1,0:T(8,128)S(1)} all-to-all(f32[16,72,128]{2,1,0:T(8,128)S(1)} %broadcast_in_dim.42), channel_id=1, replica_groups=mesh['mom'=16,'hist'=8] {'mom'}, dimensions={0} | all-to-all | bytes 1179648 | tf_op jit(solution)/shard_map/while/body/eval_jaxpr/all_to_all | solution.py:40
  108.2 4.2 %fusion.79 = f32[8,8,1024]{2,1,0:T(8,128)S(1)} fusion(f32[2,8,128,1024]{3,2,1,0:T(8,128)} %get-tuple-element.515, f32[8,4,128]{2,1,0:T(4,128)S(1)} %copy.59, f32[8,4,128]{2,1,0:T(4,128)S(1)} %copy.60), kind=kOutput, calls=%fused_computation.2.clone.1 | convolution fusion | flops 100671488 | bytes 4489216 | tf_op jit(solution)/shard_map/while/body/eval_jaxpr/kxs,kst->kxt/dot_general | solution.py:90
  112.4 2.1 fusion.78
  115.4 1.4 concatenate.95
  116.8 5.4 %all-to-all-start.1 = ((f32[8,72,128]{2,1,0:T(8,128)}), f32[8,72,128]{2,1,0:T(8,128)S(1)}, u32[]{:S(2)}, u32[]{:S(2)}) async-start(f32[8,72,128]{2,1,0:T(8,128)} %concatenate.95), calls=%async_computation.1 | async-start | bytes 589824 | tf_op jit(solution)/shard_map/while/body/eval_jaxpr/all_to_all | solution.py:57
  122.2 6.8 %all-to-all-done.1 = f32[8,72,128]{2,1,0:T(8,128)S(1)} async-done(((f32[8,72,128]{2,1,0:T(8,128)}), f32[8,72,128]{2,1,0:T(8,128)S(1)}, u32[]{:S(2)}, u32[]{:S(2)}) %all-to-all-start.1) | async-done | bytes 294944 | tf_op jit(solution)/shard_map/while/body/eval_jaxpr/all_to_all | solution.py:57
  130.9 0.6 concatenate.94
  131.6 14.0 %all_to_all.41 = f32[16,72,128]{2,1,0:T(8,128)S(1)} all-to-all(f32[16,72,128]{2,1,0:T(8,128)S(1)} %broadcast_in_dim.42), channel_id=1, replica_groups=mesh['mom'=16,'hist'=8] {'mom'}, dimensions={0} | all-to-all | bytes 1179648 | tf_op jit(solution)/shard_map/while/body/eval_jaxpr/all_to_all | solution.py:40
  147.0 4.2 %fusion.79 = f32[8,8,1024]{2,1,0:T(8,128)S(1)} fusion(f32[2,8,128,1024]{3,2,1,0:T(8,128)} %get-tuple-element.515, f32[8,4,128]{2,1,0:T(4,128)S(1)} %copy.59, f32[8,4,128]{2,1,0:T(4,128)S(1)} %copy.60), kind=kOutput, calls=%fused_computation.2.clone.1 | convolution fusion | flops 100671488 | bytes 4489216 | tf_op jit(solution)/shard_map/while/body/eval_jaxpr/kxs,kst->kxt/dot_general | solution.py:90
  151.2 2.1 fusion.78
  154.2 1.4 concatenate.95
  155.6 5.4 %all-to-all-start.1 = ((f32[8,72,128]{2,1,0:T(8,128)}), f32[8,72,128]{2,1,0:T(8,128)S(1)}, u32[]{:S(2)}, u32[]{:S(2)}) async-start(f32[8,72,128]{2,1,0:T(8,128)} %concatenate.95), calls=%async_computation.1 | async-start | bytes 589824 | tf_op jit(solution)/shard_map/while/body/eval_jaxpr/all_to_all | solution.py:57
  161.0 6.8 %all-to-all-done.1 = f32[8,72,128]{2,1,0:T(8,128)S(1)} async-done(((f32[8,72,128]{2,1,0:T(8,128)}), f32[8,72,128]{2,1,0:T(8,128)S(1)}, u32[]{:S(2)}, u32[]{:S(2)}) %all-to-all-start.1) | async-done | bytes 294944 | tf_op jit(solution)/shard_map/while/body/eval_jaxpr/all_to_all | solution.py:57
  169.7 0.6 concatenate.94
  170.4 14.0 %all_to_all.41 = f32[16,72,128]{2,1,0:T(8,128)S(1)} all-to-all(f32[16,72,128]{2,1,0:T(8,128)S(1)} %broadcast_in_dim.42), channel_id=1, replica_groups=mesh['mom'=16,'hist'=8] {'mom'}, dimensions={0} | all-to-all | bytes 1179648 | tf_op jit(solution)/shard_map/while/body/eval_jaxpr/all_to_all | solution.py:40
  185.8 4.2 %fusion.79 = f32[8,8,1024]{2,1,0:T(8,128)S(1)} fusion(f32[2,8,128,1024]{3,2,1,0:T(8,128)} %get-tuple-element.515, f32[8,4,128]{2,1,0:T(4,128)S(1)} %copy.59, f32[8,4,128]{2,1,0:T(4,128)S(1)} %copy.60), kind=kOutput, calls=%fused_computation.2.clone.1 | convolution fusion | flops 100671488 | bytes 4489216 | tf_op jit(solution)/shard_map/while/body/eval_jaxpr/kxs,kst->kxt/dot_general | solution.py:90
  190.0 2.1 fusion.78
  193.0 1.4 concatenate.95
  194.4 5.3 %all-to-all-start.1 = ((f32[8,72,128]{2,1,0:T(8,128)}), f32[8,72,128]{2,1,0:T(8,128)S(1)}, u32[]{:S(2)}, u32[]{:S(2)}) async-start(f32[8,72,128]{2,1,0:T(8,128)} %concatenate.95), calls=%async_computation.1 | async-start | bytes 589824 | tf_op jit(solution)/shard_map/while/body/eval_jaxpr/all_to_all | solution.py:57
  199.7 6.8 %all-to-all-done.1 = f32[8,72,128]{2,1,0:T(8,128)S(1)} async-done(((f32[8,72,128]{2,1,0:T(8,128)}), f32[8,72,128]{2,1,0:T(8,128)S(1)}, u32[]{:S(2)}, u32[]{:S(2)}) %all-to-all-start.1) | async-done | bytes 294944 | tf_op jit(solution)/shard_map/while/body/eval_jaxpr/all_to_all | solution.py:57
  209.2 14.1 %all_to_all.41 = f32[16,72,128]{2,1,0:T(8,128)S(1)} all-to-all(f32[16,72,128]{2,1,0:T(8,128)S(1)} %broadcast_in_dim.42), channel_id=1, replica_groups=mesh['mom'=16,'hist'=8] {'mom'}, dimensions={0} | all-to-all | bytes 1179648 | tf_op jit(solution)/shard_map/while/body/eval_jaxpr/all_to_all | solution.py:40
  224.5 4.2 %fusion.79 = f32[8,8,1024]{2,1,0:T(8,128)S(1)} fusion(f32[2,8,128,1024]{3,2,1,0:T(8,128)} %get-tuple-element.515, f32[8,4,128]{2,1,0:T(4,128)S(1)} %copy.59, f32[8,4,128]{2,1,0:T(4,128)S(1)} %copy.60), kind=kOutput, calls=%fused_computation.2.clone.1 | convolution fusion | flops 100671488 | bytes 4489216 | tf_op jit(solution)/shard_map/while/body/eval_jaxpr/kxs,kst->kxt/dot_general | solution.py:90
  228.8 2.1 fusion.78
  231.8 1.4 concatenate.95
  233.2 5.3 %all-to-all-start.1 = ((f32[8,72,128]{2,1,0:T(8,128)}), f32[8,72,128]{2,1,0:T(8,128)S(1)}, u32[]{:S(2)}, u32[]{:S(2)}) async-start(f32[8,72,128]{2,1,0:T(8,128)} %concatenate.95), calls=%async_computation.1 | async-start | bytes 589824 | tf_op jit(solution)/shard_map/while/body/eval_jaxpr/all_to_all | solution.py:57
  238.5 6.8 %all-to-all-done.1 = f32[8,72,128]{2,1,0:T(8,128)S(1)} async-done(((f32[8,72,128]{2,1,0:T(8,128)}), f32[8,72,128]{2,1,0:T(8,128)S(1)}, u32[]{:S(2)}, u32[]{:S(2)}) %all-to-all-start.1) | async-done | bytes 294944 | tf_op jit(solution)/shard_map/while/body/eval_jaxpr/all_to_all | solution.py:57
  247.3 0.7 broadcast_in_dim.40
  248.0 13.9 %all_to_all.40 = f32[128,1,1]{2,1,0:T(1,128)S(1)} all-to-all(f32[128,1,1]{2,1,0:T(1,128)S(1)} %broadcast_in_dim.40), channel_id=1, replica_groups=mesh['mom'=16,'hist'=8] {'mom','hist'}, dimensions={0} | all-to-all | bytes 1024 | tf_op jit(solution)/shard_map/all_to_all | solution.py:123
  261.9 0.7 reduce_sum.74
  (163 shorter events, 21.8 us)
Async XLA Ops:
  2.6 25.3 %all-to-all-start.2 = ((f32[16,136,128]{2,1,0:T(8,128)}), f32[16,136,128]{2,1,0:T(8,128)S(1)}, u32[]{:S(2)}, u32[]{:S(2)}) async-start(f32[16,136,128]{2,1,0:T(8,128)} %broadcast_in_dim.39), calls=%async_computation.2 | async-start | bytes 2228224 | tf_op jit(solution)/shard_map/all_to_all | solution.py:40
  34.3 11.8 %copy-start.1 = (f32[2,8,4,128]{3,2,1,0:T(4,128)S(1)}, f32[2,8,4,128]{3,2,1,0:T(4,128)}, u32[]{:S(2)}) copy-start(f32[2,8,4,128]{3,2,1,0:T(4,128)} %param.8) | copy-start | bytes 98308
  39.2 13.7 %all-to-all-start.3 = ((f32[8,72,128]{2,1,0:T(8,128)}), f32[8,72,128]{2,1,0:T(8,128)S(1)}, u32[]{:S(2)}, u32[]{:S(2)}) async-start(f32[8,72,128]{2,1,0:T(8,128)} %concatenate.91), calls=%async_computation.3 | async-start | bytes 589824 | tf_op jit(solution)/shard_map/all_to_all | solution.py:57
  68.2 5.4 %copy-start = (f32[2,8,128,1024]{3,2,1,0:T(8,128)S(1)}, f32[2,8,128,1024]{3,2,1,0:T(8,128)}, u32[]{:S(2)}) copy-start(f32[2,8,128,1024]{3,2,1,0:T(8,128)} %get-tuple-element.515) | copy-start | bytes 25165828 | tf_op jit(solution)/shard_map/while
  78.0 12.2 %all-to-all-start.1 = ((f32[8,72,128]{2,1,0:T(8,128)}), f32[8,72,128]{2,1,0:T(8,128)S(1)}, u32[]{:S(2)}, u32[]{:S(2)}) async-start(f32[8,72,128]{2,1,0:T(8,128)} %concatenate.95), calls=%async_computation.1 | async-start | bytes 589824 | tf_op jit(solution)/shard_map/while/body/eval_jaxpr/all_to_all | solution.py:57
  107.1 5.3 %copy-start = (f32[2,8,128,1024]{3,2,1,0:T(8,128)S(1)}, f32[2,8,128,1024]{3,2,1,0:T(8,128)}, u32[]{:S(2)}) copy-start(f32[2,8,128,1024]{3,2,1,0:T(8,128)} %get-tuple-element.515) | copy-start | bytes 25165828 | tf_op jit(solution)/shard_map/while
  116.8 12.2 %all-to-all-start.1 = ((f32[8,72,128]{2,1,0:T(8,128)}), f32[8,72,128]{2,1,0:T(8,128)S(1)}, u32[]{:S(2)}, u32[]{:S(2)}) async-start(f32[8,72,128]{2,1,0:T(8,128)} %concatenate.95), calls=%async_computation.1 | async-start | bytes 589824 | tf_op jit(solution)/shard_map/while/body/eval_jaxpr/all_to_all | solution.py:57
  145.9 5.3 %copy-start = (f32[2,8,128,1024]{3,2,1,0:T(8,128)S(1)}, f32[2,8,128,1024]{3,2,1,0:T(8,128)}, u32[]{:S(2)}) copy-start(f32[2,8,128,1024]{3,2,1,0:T(8,128)} %get-tuple-element.515) | copy-start | bytes 25165828 | tf_op jit(solution)/shard_map/while
  155.6 12.2 %all-to-all-start.1 = ((f32[8,72,128]{2,1,0:T(8,128)}), f32[8,72,128]{2,1,0:T(8,128)S(1)}, u32[]{:S(2)}, u32[]{:S(2)}) async-start(f32[8,72,128]{2,1,0:T(8,128)} %concatenate.95), calls=%async_computation.1 | async-start | bytes 589824 | tf_op jit(solution)/shard_map/while/body/eval_jaxpr/all_to_all | solution.py:57
  184.7 5.3 %copy-start = (f32[2,8,128,1024]{3,2,1,0:T(8,128)S(1)}, f32[2,8,128,1024]{3,2,1,0:T(8,128)}, u32[]{:S(2)}) copy-start(f32[2,8,128,1024]{3,2,1,0:T(8,128)} %get-tuple-element.515) | copy-start | bytes 25165828 | tf_op jit(solution)/shard_map/while
  194.4 12.1 %all-to-all-start.1 = ((f32[8,72,128]{2,1,0:T(8,128)}), f32[8,72,128]{2,1,0:T(8,128)S(1)}, u32[]{:S(2)}, u32[]{:S(2)}) async-start(f32[8,72,128]{2,1,0:T(8,128)} %concatenate.95), calls=%async_computation.1 | async-start | bytes 589824 | tf_op jit(solution)/shard_map/while/body/eval_jaxpr/all_to_all | solution.py:57
  223.4 5.4 %copy-start = (f32[2,8,128,1024]{3,2,1,0:T(8,128)S(1)}, f32[2,8,128,1024]{3,2,1,0:T(8,128)}, u32[]{:S(2)}) copy-start(f32[2,8,128,1024]{3,2,1,0:T(8,128)} %get-tuple-element.515) | copy-start | bytes 25165828 | tf_op jit(solution)/shard_map/while
  233.2 12.1 %all-to-all-start.1 = ((f32[8,72,128]{2,1,0:T(8,128)}), f32[8,72,128]{2,1,0:T(8,128)S(1)}, u32[]{:S(2)}, u32[]{:S(2)}) async-start(f32[8,72,128]{2,1,0:T(8,128)} %concatenate.95), calls=%async_computation.1 | async-start | bytes 589824 | tf_op jit(solution)/shard_map/while/body/eval_jaxpr/all_to_all | solution.py:57
  264.0 0.5 copy-start.2

commit v4 on v3

--- a/solution.py
+++ b/solution.py
@@ -87,8 +87,9 @@
 
     def contract(sigma):
         x = jnp.concatenate([sigma[0], sigma[1]], axis=1)
-        a = jnp.einsum("kxs,kst->kxt", x, hist_panel[0], precision=HIGHEST)
-        b = jnp.einsum("kxs,kst->kxt", x, hist_panel[1], precision=HIGHEST)
+        both = jnp.einsum("kxs,ckst->ckxt", x, hist_panel, precision=HIGHEST)
+        a = both[0]
+        b = both[1]
         real = a[:, :R] - b[:, R:]
         imag = b[:, :R] + a[:, R:]
         return jnp.stack([real, imag])

time: 266 us -> 268 us (level)
  local copies, waits for them, and re-layouts: 18.6 us -> 27.3 us
  waiting for transfers between devices: 56.8 us -> 50.3 us
    unnamed x5 -> x6, local copies, waits for them, and re-layouts: 0.52 us -> 8.79 us
    all_to_all x6, waiting for transfers between devices: 40.5 us -> 34 us  [hist_reduce(): y = lax.all_to_all(x, 'hist', 0, 0, tiled=True)]
    dot_general x12 -> x6, matrix products: 39.3 us -> 38.1 us  [contract(): both = jnp.einsum('kxs,ckst->ckxt', x, hist_panel, precision=HIGHEST)]
  transfers between devices with their start and end apart: 7 -> 7, of which waited for: 7 -> 6; matrix products, arithmetic and copies ran while one was open for 0% -> 3% of each run, Pallas kernels for 0% -> 0%
where the time goes in v4:
time: 268 us; the launch traced here: 267 us
  blocking collectives  85 us (32%)
  waiting for transfers between devices  50.3 us (19%)
  matrix products  44.6 us (17%)
  starting transfers between devices  42.3 us (16%)
  local copies, waits for them, and re-layouts  27.3 us (10%)
  other arithmetic  11.2 us (4%)
  loops' own time  4.34 us (2%)
    all_to_all x5, blocking collectives, gather_rows(): lax.all_to_all(jnp.broadcast_to(packed, (n_mom,) + packed.shape), 'mom',...  71 us
    dot_general x6, matrix products, contract(): both = jnp.einsum('kxs,ckst->ckxt', x, hist_panel, precision=HIGHEST)  38.1 us
    all_to_all x6, waiting for transfers between devices, hist_reduce(): y = lax.all_to_all(x, 'hist', 0, 0, tiled=True)  34 us
    all_to_all x6, starting transfers between devices, hist_reduce(): y = lax.all_to_all(x, 'hist', 0, 0, tiled=True)  33.7 us
    all_to_all x1, waiting for transfers between devices, gather_rows(): lax.all_to_all(jnp.broadcast_to(packed, (n_mom,) + packed.shape), 'mom',...  16.3 us
    all_to_all x1, blocking collectives, shards(): total = jnp.sum(lax.all_to_all(spread, ('mom', 'hist'), 0, 0, tiled=True))  13.9 us
    unnamed x6, local copies, waits for them, and re-layouts  8.79 us
    all_to_all x1, starting transfers between devices, gather_rows(): lax.all_to_all(jnp.broadcast_to(packed, (n_mom,) + packed.shape), 'mom',...  8.59 us
  transfers between devices with their start and end apart: 7, of which 6 were waited for; matrix products, arithmetic and copies ran while one was open for 3% of the time, Pallas kernels for 0%

profile of v4, /device:TPU:1, one launch (start us, length us, event | category | flops | bytes accessed | tf_op | source)
XLA Modules:
  0.0 266.6 jit_solution(18027278583759308355)
XLA Ops:
  0.7 0.9 maximum_maximum_fusion
  1.5 1.1 broadcast_in_dim.39
  2.6 8.6 %all-to-all-start.2 = ((f32[16,136,128]{2,1,0:T(8,128)}), f32[16,136,128]{2,1,0:T(8,128)S(1)}, u32[]{:S(2)}, u32[]{:S(2)}) async-start(f32[16,136,128]{2,1,0:T(8,128)} %broadcast_in_dim.39), calls=%async_computation.2 | async-start | bytes 2228224 | tf_op jit(solution)/shard_map/all_to_all | solution.py:40
  11.6 16.3 %all-to-all-done.2 = f32[16,136,128]{2,1,0:T(8,128)S(1)} async-done(((f32[16,136,128]{2,1,0:T(8,128)}), f32[16,136,128]{2,1,0:T(8,128)S(1)}, u32[]{:S(2)}, u32[]{:S(2)}) %all-to-all-start.2) | async-done | bytes 1114144 | tf_op jit(solution)/shard_map/all_to_all | solution.py:40
  28.3 1.0 fusion.18
  30.6 6.4 %convolution_bitcast_fusion.3 = f32[2,8,8,1024]{3,2,0,1:T(8,128)S(1)} fusion(f32[8,4,128]{2,1,0:T(4,128)S(1)} %copy.70, f32[8,4,128]{2,1,0:T(4,128)S(1)} %copy.69, f32[2,8,128,1024]{3,2,1,0:T(8,128)} %param.7), kind=kOutput, calls=%fused_computation.37 | convolution fusion | flops 201334784 | bytes 8945664 | tf_op jit(solution)/shard_map/kxs,ckst->ckxt/dot_general | solution.py:90
  37.3 0.8 concatenate.91
  38.1 7.0 %all-to-all-start.3 = ((f32[8,72,128]{2,1,0:T(8,128)}), f32[8,72,128]{2,1,0:T(8,128)S(1)}, u32[]{:S(2)}, u32[]{:S(2)}) async-start(f32[8,72,128]{2,1,0:T(8,128)} %concatenate.91), calls=%async_computation.3 | async-start | bytes 589824 | tf_op jit(solution)/shard_map/all_to_all | solution.py:57
  45.0 8.3 %copy.71 = f32[2,8,128,1024]{3,2,0,1:T(8,128)} copy(f32[2,8,128,1024]{3,2,1,0:T(8,128)} %param.7) | data formatting | bytes 16777216 | tf_op args[0]
  53.7 195.2 %while.20 = (s32[]{:T(128)}, f32[2,8,4,128]{3,2,1,0:T(4,128)S(1)}, f32[2,8,4,128]{3,2,1,0:T(4,128)S(1)}, f32[6]{0:T(128)S(1)}, f32[2,8,4,128]{3,2,1,0:T(4,128)S(...) while((s32[]{:T(128)}, f32[2,8,4,128]{3,2,1,0:T(4,128)S(1)}, ...), condition=%wide.region_5.6_spmd, body=%wide.region_1.5_spmd.sunk | while | flops 416312320 | bytes 24105296 | solution.py:119
  53.7 0.6 multiply_reduce_fusion.3
  54.3 0.6 concatenate.94
  55.0 14.8 %all_to_all.41 = f32[16,72,128]{2,1,0:T(8,128)S(1)} all-to-all(f32[16,72,128]{2,1,0:T(8,128)S(1)} %broadcast_in_dim.42), channel_id=1, replica_groups=mesh['mom'=16,'hist'=8] {'mom'}, dimensions={0} | all-to-all | bytes 1179648 | tf_op jit(solution)/shard_map/while/body/eval_jaxpr/all_to_all | solution.py:40
  71.1 6.3 %convolution_bitcast_fusion.9 = f32[2,8,8,1024]{3,2,0,1:T(8,128)S(1)} fusion(f32[2,8,128,1024]{3,2,0,1:T(8,128)} %get-tuple-element.523, f32[8,4,128]{2,1,0:T(4,128)S(1)} %copy.89, f32[8,4,128]{2,1,0:T(4,128)S(1)} %copy.90), kind=kOutput, calls=%fused_computation.1.clone.1 | convolution fusion | flops 201334784 | bytes 8945664 | tf_op jit(solution)/shard_map/while/body/eval_jaxpr/kxs,ckst->ckxt/dot_general | solution.py:90
  78.4 1.4 concatenate.95
  79.8 5.4 %all-to-all-start.1 = ((f32[8,72,128]{2,1,0:T(8,128)}), f32[8,72,128]{2,1,0:T(8,128)S(1)}, u32[]{:S(2)}, u32[]{:S(2)}) async-start(f32[8,72,128]{2,1,0:T(8,128)} %concatenate.95), calls=%async_computation.1 | async-start | bytes 589824 | tf_op jit(solution)/shard_map/while/body/eval_jaxpr/all_to_all | solution.py:57
  85.2 6.8 %all-to-all-done.1 = f32[8,72,128]{2,1,0:T(8,128)S(1)} async-done(((f32[8,72,128]{2,1,0:T(8,128)}), f32[8,72,128]{2,1,0:T(8,128)S(1)}, u32[]{:S(2)}, u32[]{:S(2)}) %all-to-all-start.1) | async-done | bytes 294944 | tf_op jit(solution)/shard_map/while/body/eval_jaxpr/all_to_all | solution.py:57
  93.9 0.6 concatenate.94
  94.6 14.1 %all_to_all.41 = f32[16,72,128]{2,1,0:T(8,128)S(1)} all-to-all(f32[16,72,128]{2,1,0:T(8,128)S(1)} %broadcast_in_dim.42), channel_id=1, replica_groups=mesh['mom'=16,'hist'=8] {'mom'}, dimensions={0} | all-to-all | bytes 1179648 | tf_op jit(solution)/shard_map/while/body/eval_jaxpr/all_to_all | solution.py:40
  108.9 0.6 convolution_bitcast_fusion.7
  110.0 6.3 %convolution_bitcast_fusion.9 = f32[2,8,8,1024]{3,2,0,1:T(8,128)S(1)} fusion(f32[2,8,128,1024]{3,2,0,1:T(8,128)} %get-tuple-element.523, f32[8,4,128]{2,1,0:T(4,128)S(1)} %copy.89, f32[8,4,128]{2,1,0:T(4,128)S(1)} %copy.90), kind=kOutput, calls=%fused_computation.1.clone.1 | convolution fusion | flops 201334784 | bytes 8945664 | tf_op jit(solution)/shard_map/while/body/eval_jaxpr/kxs,ckst->ckxt/dot_general | solution.py:90
  117.3 1.4 concatenate.95
  118.7 5.3 %all-to-all-start.1 = ((f32[8,72,128]{2,1,0:T(8,128)}), f32[8,72,128]{2,1,0:T(8,128)S(1)}, u32[]{:S(2)}, u32[]{:S(2)}) async-start(f32[8,72,128]{2,1,0:T(8,128)} %concatenate.95), calls=%async_computation.1 | async-start | bytes 589824 | tf_op jit(solution)/shard_map/while/body/eval_jaxpr/all_to_all | solution.py:57
  124.1 6.8 %all-to-all-done.1 = f32[8,72,128]{2,1,0:T(8,128)S(1)} async-done(((f32[8,72,128]{2,1,0:T(8,128)}), f32[8,72,128]{2,1,0:T(8,128)S(1)}, u32[]{:S(2)}, u32[]{:S(2)}) %all-to-all-start.1) | async-done | bytes 294944 | tf_op jit(solution)/shard_map/while/body/eval_jaxpr/all_to_all | solution.py:57
  132.8 0.6 concatenate.94
  133.5 14.1 %all_to_all.41 = f32[16,72,128]{2,1,0:T(8,128)S(1)} all-to-all(f32[16,72,128]{2,1,0:T(8,128)S(1)} %broadcast_in_dim.42), channel_id=1, replica_groups=mesh['mom'=16,'hist'=8] {'mom'}, dimensions={0} | all-to-all | bytes 1179648 | tf_op jit(solution)/shard_map/while/body/eval_jaxpr/all_to_all | solution.py:40
  148.9 6.3 %convolution_bitcast_fusion.9 = f32[2,8,8,1024]{3,2,0,1:T(8,128)S(1)} fusion(f32[2,8,128,1024]{3,2,0,1:T(8,128)} %get-tuple-element.523, f32[8,4,128]{2,1,0:T(4,128)S(1)} %copy.89, f32[8,4,128]{2,1,0:T(4,128)S(1)} %copy.90), kind=kOutput, calls=%fused_computation.1.clone.1 | convolution fusion | flops 201334784 | bytes 8945664 | tf_op jit(solution)/shard_map/while/body/eval_jaxpr/kxs,ckst->ckxt/dot_general | solution.py:90
  156.2 1.4 concatenate.95
  157.6 5.3 %all-to-all-start.1 = ((f32[8,72,128]{2,1,0:T(8,128)}), f32[8,72,128]{2,1,0:T(8,128)S(1)}, u32[]{:S(2)}, u32[]{:S(2)}) async-start(f32[8,72,128]{2,1,0:T(8,128)} %concatenate.95), calls=%async_computation.1 | async-start | bytes 589824 | tf_op jit(solution)/shard_map/while/body/eval_jaxpr/all_to_all | solution.py:57
  162.9 6.8 %all-to-all-done.1 = f32[8,72,128]{2,1,0:T(8,128)S(1)} async-done(((f32[8,72,128]{2,1,0:T(8,128)}), f32[8,72,128]{2,1,0:T(8,128)S(1)}, u32[]{:S(2)}, u32[]{:S(2)}) %all-to-all-start.1) | async-done | bytes 294944 | tf_op jit(solution)/shard_map/while/body/eval_jaxpr/all_to_all | solution.py:57
  171.1 0.6 multiply_reduce_fusion.3
  171.7 0.6 concatenate.94
  172.4 14.1 %all_to_all.41 = f32[16,72,128]{2,1,0:T(8,128)S(1)} all-to-all(f32[16,72,128]{2,1,0:T(8,128)S(1)} %broadcast_in_dim.42), channel_id=1, replica_groups=mesh['mom'=16,'hist'=8] {'mom'}, dimensions={0} | all-to-all | bytes 1179648 | tf_op jit(solution)/shard_map/while/body/eval_jaxpr/all_to_all | solution.py:40
  186.6 0.6 convolution_bitcast_fusion.7
  187.7 6.3 %convolution_bitcast_fusion.9 = f32[2,8,8,1024]{3,2,0,1:T(8,128)S(1)} fusion(f32[2,8,128,1024]{3,2,0,1:T(8,128)} %get-tuple-element.523, f32[8,4,128]{2,1,0:T(4,128)S(1)} %copy.89, f32[8,4,128]{2,1,0:T(4,128)S(1)} %copy.90), kind=kOutput, calls=%fused_computation.1.clone.1 | convolution fusion | flops 201334784 | bytes 8945664 | tf_op jit(solution)/shard_map/while/body/eval_jaxpr/kxs,ckst->ckxt/dot_general | solution.py:90
  195.0 1.4 concatenate.95
  196.5 5.3 %all-to-all-start.1 = ((f32[8,72,128]{2,1,0:T(8,128)}), f32[8,72,128]{2,1,0:T(8,128)S(1)}, u32[]{:S(2)}, u32[]{:S(2)}) async-start(f32[8,72,128]{2,1,0:T(8,128)} %concatenate.95), calls=%async_computation.1 | async-start | bytes 589824 | tf_op jit(solution)/shard_map/while/body/eval_jaxpr/all_to_all | solution.py:57
  201.8 6.8 %all-to-all-done.1 = f32[8,72,128]{2,1,0:T(8,128)S(1)} async-done(((f32[8,72,128]{2,1,0:T(8,128)}), f32[8,72,128]{2,1,0:T(8,128)S(1)}, u32[]{:S(2)}, u32[]{:S(2)}) %all-to-all-start.1) | async-done | bytes 294944 | tf_op jit(solution)/shard_map/while/body/eval_jaxpr/all_to_all | solution.py:57
  210.6 0.6 concatenate.94
  211.3 14.1 %all_to_all.41 = f32[16,72,128]{2,1,0:T(8,128)S(1)} all-to-all(f32[16,72,128]{2,1,0:T(8,128)S(1)} %broadcast_in_dim.42), channel_id=1, replica_groups=mesh['mom'=16,'hist'=8] {'mom'}, dimensions={0} | all-to-all | bytes 1179648 | tf_op jit(solution)/shard_map/while/body/eval_jaxpr/all_to_all | solution.py:40
  226.6 6.3 %convolution_bitcast_fusion.9 = f32[2,8,8,1024]{3,2,0,1:T(8,128)S(1)} fusion(f32[2,8,128,1024]{3,2,0,1:T(8,128)} %get-tuple-element.523, f32[8,4,128]{2,1,0:T(4,128)S(1)} %copy.89, f32[8,4,128]{2,1,0:T(4,128)S(1)} %copy.90), kind=kOutput, calls=%fused_computation.1.clone.1 | convolution fusion | flops 201334784 | bytes 8945664 | tf_op jit(solution)/shard_map/while/body/eval_jaxpr/kxs,ckst->ckxt/dot_general | solution.py:90
  233.9 1.4 concatenate.95
  235.3 5.4 %all-to-all-start.1 = ((f32[8,72,128]{2,1,0:T(8,128)}), f32[8,72,128]{2,1,0:T(8,128)S(1)}, u32[]{:S(2)}, u32[]{:S(2)}) async-start(f32[8,72,128]{2,1,0:T(8,128)} %concatenate.95), calls=%async_computation.1 | async-start | bytes 589824 | tf_op jit(solution)/shard_map/while/body/eval_jaxpr/all_to_all | solution.py:57
  240.7 6.8 %all-to-all-done.1 = f32[8,72,128]{2,1,0:T(8,128)S(1)} async-done(((f32[8,72,128]{2,1,0:T(8,128)}), f32[8,72,128]{2,1,0:T(8,128)S(1)}, u32[]{:S(2)}, u32[]{:S(2)}) %all-to-all-start.1) | async-done | bytes 294944 | tf_op jit(solution)/shard_map/while/body/eval_jaxpr/all_to_all | solution.py:57
  249.4 0.7 broadcast_in_dim.40
  250.1 13.9 %all_to_all.40 = f32[128,1,1]{2,1,0:T(1,128)S(1)} all-to-all(f32[128,1,1]{2,1,0:T(1,128)S(1)} %broadcast_in_dim.40), channel_id=1, replica_groups=mesh['mom'=16,'hist'=8] {'mom','hist'}, dimensions={0} | all-to-all | bytes 1024 | tf_op jit(solution)/shard_map/all_to_all | solution.py:124
  264.1 0.7 reduce_sum.74
  265.5 0.6 divide_add_fusion.1
  (154 shorter events, 18.2 us)
Async XLA Ops:
  2.6 25.3 %all-to-all-start.2 = ((f32[16,136,128]{2,1,0:T(8,128)}), f32[16,136,128]{2,1,0:T(8,128)S(1)}, u32[]{:S(2)}, u32[]{:S(2)}) async-start(f32[16,136,128]{2,1,0:T(8,128)} %broadcast_in_dim.39), calls=%async_computation.2 | async-start | bytes 2228224 | tf_op jit(solution)/shard_map/all_to_all | solution.py:40
  30.1 14.9 %copy-start = (f32[2,8,4,128]{3,2,1,0:T(4,128)S(1)}, f32[2,8,4,128]{3,2,1,0:T(4,128)}, u32[]{:S(2)}) copy-start(f32[2,8,4,128]{3,2,1,0:T(4,128)} %param.8) | copy-start | bytes 98308
  38.1 15.5 %all-to-all-start.3 = ((f32[8,72,128]{2,1,0:T(8,128)}), f32[8,72,128]{2,1,0:T(8,128)S(1)}, u32[]{:S(2)}, u32[]{:S(2)}) async-start(f32[8,72,128]{2,1,0:T(8,128)} %concatenate.91), calls=%async_computation.3 | async-start | bytes 589824 | tf_op jit(solution)/shard_map/all_to_all | solution.py:57
  79.8 12.2 %all-to-all-start.1 = ((f32[8,72,128]{2,1,0:T(8,128)}), f32[8,72,128]{2,1,0:T(8,128)S(1)}, u32[]{:S(2)}, u32[]{:S(2)}) async-start(f32[8,72,128]{2,1,0:T(8,128)} %concatenate.95), calls=%async_computation.1 | async-start | bytes 589824 | tf_op jit(solution)/shard_map/while/body/eval_jaxpr/all_to_all | solution.py:57
  118.7 12.1 %all-to-all-start.1 = ((f32[8,72,128]{2,1,0:T(8,128)}), f32[8,72,128]{2,1,0:T(8,128)S(1)}, u32[]{:S(2)}, u32[]{:S(2)}) async-start(f32[8,72,128]{2,1,0:T(8,128)} %concatenate.95), calls=%async_computation.1 | async-start | bytes 589824 | tf_op jit(solution)/shard_map/while/body/eval_jaxpr/all_to_all | solution.py:57
  157.6 12.1 %all-to-all-start.1 = ((f32[8,72,128]{2,1,0:T(8,128)}), f32[8,72,128]{2,1,0:T(8,128)S(1)}, u32[]{:S(2)}, u32[]{:S(2)}) async-start(f32[8,72,128]{2,1,0:T(8,128)} %concatenate.95), calls=%async_computation.1 | async-start | bytes 589824 | tf_op jit(solution)/shard_map/while/body/eval_jaxpr/all_to_all | solution.py:57
  196.5 12.1 %all-to-all-start.1 = ((f32[8,72,128]{2,1,0:T(8,128)}), f32[8,72,128]{2,1,0:T(8,128)S(1)}, u32[]{:S(2)}, u32[]{:S(2)}) async-start(f32[8,72,128]{2,1,0:T(8,128)} %concatenate.95), calls=%async_computation.1 | async-start | bytes 589824 | tf_op jit(solution)/shard_map/while/body/eval_jaxpr/all_to_all | solution.py:57
  235.3 12.2 %all-to-all-start.1 = ((f32[8,72,128]{2,1,0:T(8,128)}), f32[8,72,128]{2,1,0:T(8,128)S(1)}, u32[]{:S(2)}, u32[]{:S(2)}) async-start(f32[8,72,128]{2,1,0:T(8,128)} %concatenate.95), calls=%async_computation.1 | async-start | bytes 589824 | tf_op jit(solution)/shard_map/while/body/eval_jaxpr/all_to_all | solution.py:57
  266.1 0.5 copy-start.1

commit v5 on v3

--- a/solution.py
+++ b/solution.py
@@ -39,7 +39,7 @@
     packed = jnp.concatenate([block, jnp.full((8, 128), extra, block.dtype)])
     got = lax.all_to_all(jnp.broadcast_to(packed, (n_mom,) + packed.shape), "mom", 0, 0, tiled=True)
     n = block.shape[0]
-    return got[:, :n], jnp.sum(got[:, n, 0])
+    return got[:, :n], got[:, n, 0]
 
 
 def to_full_k(rows, lead, k_local, cols):
@@ -53,11 +53,12 @@
     cols = h // hist_n
     x = partial.reshape(two, kl, rr, hist_n, cols)
     x = jnp.transpose(x, (3, 0, 1, 2, 4)).reshape(hist_n, two * kl * rr * cols // 128, 128)
-    x = jnp.concatenate([x, jnp.full((hist_n, 8, 128), extra, x.dtype)], axis=1)
+    tile = jnp.pad(extra[None, :], ((0, 7), (0, 128 - extra.shape[0])))
+    x = jnp.concatenate([x, jnp.broadcast_to(tile, (hist_n, 8, 128))], axis=1)
     y = lax.all_to_all(x, "hist", 0, 0, tiled=True)
-    s = jnp.sum(y, axis=0)
     n = two * kl * rr * cols // 128
-    return s[:n].reshape(two, kl, rr, cols), s[n, 0]
+    total = jnp.sum(jnp.sum(y[:, n, : extra.shape[0]], axis=0))
+    return jnp.sum(y[:, :n], axis=0).reshape(two, kl, rr, cols), total
 
 
 def shards(hist_panel, free_rows, screened):
@@ -100,7 +101,7 @@
     green_full = to_full_k(rows[:, half:], 2, k_local, cols)
     screen_hat = dft(cosine, sine, screen_full[0], screen_full[1])
 
-    integral, _ = hist_reduce(contract(sigma_of(green_full)), jnp.float32(0.0), hist_n)
+    integral, _ = hist_reduce(contract(sigma_of(green_full)), jnp.zeros((lax.axis_size("mom"),), jnp.float32), hist_n)
     def correction(turn, carry):
         green, integral, deltas = carry
         change = free_rows + step_size * integral - green

time: 266 us -> 261 us (0.981)
  local copies, waits for them, and re-layouts: 18.6 us -> 9.96 us
  other arithmetic: 11.2 us -> 15.5 us
    concatenate x6 -> x0, local copies, waits for them, and re-layouts: 7.59 us -> none  [hist_reduce(): x = jnp.concatenate([x, jnp.full((hist_n, 8, 128), extra, x.dtype)], axis=1)]
    concatenate x0 -> x6, other arithmetic: none -> 4.35 us  [hist_reduce(): x = jnp.concatenate([x, jnp.broadcast_to(tile, (hist_n, 8, 128))], axis=1)]
where the time goes in v5:
time: 261 us; the launch traced here: 260 us
  blocking collectives  83.9 us (32%)
  waiting for transfers between devices  56.8 us (22%)
  matrix products  45.7 us (18%)
  starting transfers between devices  42.3 us (16%)
  other arithmetic  15.5 us (6%)
  local copies, waits for them, and re-layouts  9.96 us (4%)
  loops' own time  4.31 us (2%)
    all_to_all x5, blocking collectives, gather_rows(): lax.all_to_all(jnp.broadcast_to(packed, (n_mom,) + packed.shape), 'mom',...  69.9 us
    all_to_all x6, waiting for transfers between devices, hist_reduce(): y = lax.all_to_all(x, 'hist', 0, 0, tiled=True)  40.5 us
    all_to_all x6, starting transfers between devices, hist_reduce(): y = lax.all_to_all(x, 'hist', 0, 0, tiled=True)  33.7 us
    dot_general x6, matrix products, contract(): a = jnp.einsum('kxs,kst->kxt', x, hist_panel[0], precision=HIGHEST)  25 us
    all_to_all x1, waiting for transfers between devices, gather_rows(): lax.all_to_all(jnp.broadcast_to(packed, (n_mom,) + packed.shape), 'mom',...  16.3 us
    dot_general x6, matrix products, contract(): b = jnp.einsum('kxs,kst->kxt', x, hist_panel[1], precision=HIGHEST)  14.2 us
    all_to_all x1, blocking collectives, shards(): total = jnp.sum(lax.all_to_all(spread, ('mom', 'hist'), 0, 0, tiled=True))  13.9 us
    all_to_all x1, starting transfers between devices, gather_rows(): lax.all_to_all(jnp.broadcast_to(packed, (n_mom,) + packed.shape), 'mom',...  8.59 us
  transfers between devices with their start and end apart: 7, of which 7 were waited for; matrix products, arithmetic and copies ran while one was open for 0% of the time, Pallas kernels for 0%

profile of v5, /device:TPU:1, one launch (start us, length us, event | category | flops | bytes accessed | tf_op | source)
XLA Modules:
  0.0 260.1 jit_solution(12457146881568654944)
XLA Ops:
  0.7 0.9 maximum_maximum_fusion
  1.5 1.1 broadcast_in_dim.50
  2.6 8.6 %all-to-all-start.2 = ((f32[16,136,128]{2,1,0:T(8,128)}), f32[16,136,128]{2,1,0:T(8,128)S(1)}, u32[]{:S(2)}, u32[]{:S(2)}) async-start(f32[16,136,128]{2,1,0:T(8,128)} %broadcast_in_dim.50), calls=%async_computation.2 | async-start | bytes 2228224 | tf_op jit(solution)/shard_map/all_to_all | solution.py:40
  11.6 16.3 %all-to-all-done.2 = f32[16,136,128]{2,1,0:T(8,128)S(1)} async-done(((f32[16,136,128]{2,1,0:T(8,128)}), f32[16,136,128]{2,1,0:T(8,128)S(1)}, u32[]{:S(2)}, u32[]{:S(2)}) %all-to-all-start.2) | async-done | bytes 1114144 | tf_op jit(solution)/shard_map/all_to_all | solution.py:40
  28.9 1.0 fusion.29
  30.6 3.8 %fusion.21 = f32[8,8,1024]{2,1,0:T(8,128)S(1)} fusion(f32[2,8,128,1024]{3,2,1,0:T(8,128)} %param.7, f32[8,4,128]{2,1,0:T(4,128)S(1)} %copy.52, f32[8,4,128]{2,1,0:T(4,128)S(1)} %copy.51), kind=kOutput, calls=%fused_computation.43 | convolution fusion | flops 100671488 | bytes 4489216 | tf_op jit(solution)/shard_map/kxs,kst->kxt/dot_general | solution.py:91
  34.4 3.8 %fusion.19 = f32[8,8,1024]{2,1,0:T(8,128)S(1)} fusion(f32[2,8,128,1024]{3,2,1,0:T(8,128)} %param.7, f32[8,4,128]{2,1,0:T(4,128)S(1)} %copy.52, f32[8,4,128]{2,1,0:T(4,128)S(1)} %copy.51), kind=kOutput, calls=%fused_computation.41 | convolution fusion | flops 100671488 | bytes 4489216 | tf_op jit(solution)/shard_map/kxs,kst->kxt/dot_general | solution.py:92
  38.5 0.7 pad_maximum_fusion.4
  39.2 7.0 %all-to-all-start.3 = ((f32[8,72,128]{2,1,0:T(8,128)}), f32[8,72,128]{2,1,0:T(8,128)S(1)}, u32[]{:S(2)}, u32[]{:S(2)}) async-start(f32[8,72,128]{2,1,0:T(8,128)} %pad_maximum_fusion.4), calls=%async_computation.3 | async-start | bytes 589824 | tf_op jit(solution)/shard_map/all_to_all | solution.py:58
  46.5 6.5 %all-to-all-done.3 = f32[8,72,128]{2,1,0:T(8,128)S(1)} async-done(((f32[8,72,128]{2,1,0:T(8,128)}), f32[8,72,128]{2,1,0:T(8,128)S(1)}, u32[]{:S(2)}, u32[]{:S(2)}) %all-to-all-start.3) | async-done | bytes 294944 | tf_op jit(solution)/shard_map/all_to_all | solution.py:58
  53.0 189.3 %while.20 = (s32[]{:T(128)}, f32[2,8,4,128]{3,2,1,0:T(4,128)S(1)}, f32[2,8,4,128]{3,2,1,0:T(4,128)S(1)}, f32[6]{0:T(128)S(1)}, f32[2,8,4,128]{3,2,1,0:T(4,128)S(...) while((s32[]{:T(128)}, f32[2,8,4,128]{3,2,1,0:T(4,128)S(1)}, ...), condition=%wide.region_5.6_spmd, body=%wide.region_1.5_spmd.sunk | while | flops 416387200 | bytes 56681420 | solution.py:119
  53.6 0.6 concatenate.102
  54.3 13.7 %all_to_all.43 = f32[16,72,128]{2,1,0:T(8,128)S(1)} all-to-all(f32[16,72,128]{2,1,0:T(8,128)S(1)} %broadcast_in_dim.55), channel_id=1, replica_groups=mesh['mom'=16,'hist'=8] {'mom'}, dimensions={0} | all-to-all | bytes 1179648 | tf_op jit(solution)/shard_map/while/body/eval_jaxpr/all_to_all | solution.py:40
  69.3 4.2 %fusion.79 = f32[8,8,1024]{2,1,0:T(8,128)S(1)} fusion(f32[2,8,128,1024]{3,2,1,0:T(8,128)} %get-tuple-element.538, f32[8,4,128]{2,1,0:T(4,128)S(1)} %copy.61, f32[8,4,128]{2,1,0:T(4,128)S(1)} %copy.62), kind=kOutput, calls=%fused_computation.2.clone.1 | convolution fusion | flops 100671488 | bytes 4489216 | tf_op jit(solution)/shard_map/while/body/eval_jaxpr/kxs,kst->kxt/dot_general | solution.py:91
  73.6 2.1 fusion.78
  76.2 0.7 pad_maximum_fusion.18
  76.9 5.4 %all-to-all-start.1 = ((f32[8,72,128]{2,1,0:T(8,128)}), f32[8,72,128]{2,1,0:T(8,128)S(1)}, u32[]{:S(2)}, u32[]{:S(2)}) async-start(f32[8,72,128]{2,1,0:T(8,128)} %pad_maximum_fusion.18), calls=%async_computation.1 | async-start | bytes 589824 | tf_op jit(solution)/shard_map/while/body/eval_jaxpr/all_to_all | solution.py:58
  82.3 6.8 %all-to-all-done.1 = f32[8,72,128]{2,1,0:T(8,128)S(1)} async-done(((f32[8,72,128]{2,1,0:T(8,128)}), f32[8,72,128]{2,1,0:T(8,128)S(1)}, u32[]{:S(2)}, u32[]{:S(2)}) %all-to-all-start.1) | async-done | bytes 294944 | tf_op jit(solution)/shard_map/while/body/eval_jaxpr/all_to_all | solution.py:58
  91.2 0.6 concatenate.102
  91.9 14.1 %all_to_all.43 = f32[16,72,128]{2,1,0:T(8,128)S(1)} all-to-all(f32[16,72,128]{2,1,0:T(8,128)S(1)} %broadcast_in_dim.55), channel_id=1, replica_groups=mesh['mom'=16,'hist'=8] {'mom'}, dimensions={0} | all-to-all | bytes 1179648 | tf_op jit(solution)/shard_map/while/body/eval_jaxpr/all_to_all | solution.py:40
  107.3 4.2 %fusion.79 = f32[8,8,1024]{2,1,0:T(8,128)S(1)} fusion(f32[2,8,128,1024]{3,2,1,0:T(8,128)} %get-tuple-element.538, f32[8,4,128]{2,1,0:T(4,128)S(1)} %copy.61, f32[8,4,128]{2,1,0:T(4,128)S(1)} %copy.62), kind=kOutput, calls=%fused_computation.2.clone.1 | convolution fusion | flops 100671488 | bytes 4489216 | tf_op jit(solution)/shard_map/while/body/eval_jaxpr/kxs,kst->kxt/dot_general | solution.py:91
  111.5 2.1 fusion.78
  114.1 0.7 pad_maximum_fusion.18
  114.9 5.3 %all-to-all-start.1 = ((f32[8,72,128]{2,1,0:T(8,128)}), f32[8,72,128]{2,1,0:T(8,128)S(1)}, u32[]{:S(2)}, u32[]{:S(2)}) async-start(f32[8,72,128]{2,1,0:T(8,128)} %pad_maximum_fusion.18), calls=%async_computation.1 | async-start | bytes 589824 | tf_op jit(solution)/shard_map/while/body/eval_jaxpr/all_to_all | solution.py:58
  120.2 6.8 %all-to-all-done.1 = f32[8,72,128]{2,1,0:T(8,128)S(1)} async-done(((f32[8,72,128]{2,1,0:T(8,128)}), f32[8,72,128]{2,1,0:T(8,128)S(1)}, u32[]{:S(2)}, u32[]{:S(2)}) %all-to-all-start.1) | async-done | bytes 294944 | tf_op jit(solution)/shard_map/while/body/eval_jaxpr/all_to_all | solution.py:58
  129.1 0.6 concatenate.102
  129.9 14.1 %all_to_all.43 = f32[16,72,128]{2,1,0:T(8,128)S(1)} all-to-all(f32[16,72,128]{2,1,0:T(8,128)S(1)} %broadcast_in_dim.55), channel_id=1, replica_groups=mesh['mom'=16,'hist'=8] {'mom'}, dimensions={0} | all-to-all | bytes 1179648 | tf_op jit(solution)/shard_map/while/body/eval_jaxpr/all_to_all | solution.py:40
  145.2 4.2 %fusion.79 = f32[8,8,1024]{2,1,0:T(8,128)S(1)} fusion(f32[2,8,128,1024]{3,2,1,0:T(8,128)} %get-tuple-element.538, f32[8,4,128]{2,1,0:T(4,128)S(1)} %copy.61, f32[8,4,128]{2,1,0:T(4,128)S(1)} %copy.62), kind=kOutput, calls=%fused_computation.2.clone.1 | convolution fusion | flops 100671488 | bytes 4489216 | tf_op jit(solution)/shard_map/while/body/eval_jaxpr/kxs,kst->kxt/dot_general | solution.py:91
  149.5 2.1 fusion.78
  152.1 0.7 pad_maximum_fusion.18
  152.8 5.3 %all-to-all-start.1 = ((f32[8,72,128]{2,1,0:T(8,128)}), f32[8,72,128]{2,1,0:T(8,128)S(1)}, u32[]{:S(2)}, u32[]{:S(2)}) async-start(f32[8,72,128]{2,1,0:T(8,128)} %pad_maximum_fusion.18), calls=%async_computation.1 | async-start | bytes 589824 | tf_op jit(solution)/shard_map/while/body/eval_jaxpr/all_to_all | solution.py:58
  158.1 6.8 %all-to-all-done.1 = f32[8,72,128]{2,1,0:T(8,128)S(1)} async-done(((f32[8,72,128]{2,1,0:T(8,128)}), f32[8,72,128]{2,1,0:T(8,128)S(1)}, u32[]{:S(2)}, u32[]{:S(2)}) %all-to-all-start.1) | async-done | bytes 294944 | tf_op jit(solution)/shard_map/while/body/eval_jaxpr/all_to_all | solution.py:58
  167.1 0.6 concatenate.102
  167.8 14.1 %all_to_all.43 = f32[16,72,128]{2,1,0:T(8,128)S(1)} all-to-all(f32[16,72,128]{2,1,0:T(8,128)S(1)} %broadcast_in_dim.55), channel_id=1, replica_groups=mesh['mom'=16,'hist'=8] {'mom'}, dimensions={0} | all-to-all | bytes 1179648 | tf_op jit(solution)/shard_map/while/body/eval_jaxpr/all_to_all | solution.py:40
  183.1 4.2 %fusion.79 = f32[8,8,1024]{2,1,0:T(8,128)S(1)} fusion(f32[2,8,128,1024]{3,2,1,0:T(8,128)} %get-tuple-element.538, f32[8,4,128]{2,1,0:T(4,128)S(1)} %copy.61, f32[8,4,128]{2,1,0:T(4,128)S(1)} %copy.62), kind=kOutput, calls=%fused_computation.2.clone.1 | convolution fusion | flops 100671488 | bytes 4489216 | tf_op jit(solution)/shard_map/while/body/eval_jaxpr/kxs,kst->kxt/dot_general | solution.py:91
  187.3 2.1 fusion.78
  190.0 0.7 pad_maximum_fusion.18
  190.7 5.4 %all-to-all-start.1 = ((f32[8,72,128]{2,1,0:T(8,128)}), f32[8,72,128]{2,1,0:T(8,128)S(1)}, u32[]{:S(2)}, u32[]{:S(2)}) async-start(f32[8,72,128]{2,1,0:T(8,128)} %pad_maximum_fusion.18), calls=%async_computation.1 | async-start | bytes 589824 | tf_op jit(solution)/shard_map/while/body/eval_jaxpr/all_to_all | solution.py:58
  196.0 6.8 %all-to-all-done.1 = f32[8,72,128]{2,1,0:T(8,128)S(1)} async-done(((f32[8,72,128]{2,1,0:T(8,128)}), f32[8,72,128]{2,1,0:T(8,128)S(1)}, u32[]{:S(2)}, u32[]{:S(2)}) %all-to-all-start.1) | async-done | bytes 294944 | tf_op jit(solution)/shard_map/while/body/eval_jaxpr/all_to_all | solution.py:58
  205.7 14.0 %all_to_all.43 = f32[16,72,128]{2,1,0:T(8,128)S(1)} all-to-all(f32[16,72,128]{2,1,0:T(8,128)S(1)} %broadcast_in_dim.55), channel_id=1, replica_groups=mesh['mom'=16,'hist'=8] {'mom'}, dimensions={0} | all-to-all | bytes 1179648 | tf_op jit(solution)/shard_map/while/body/eval_jaxpr/all_to_all | solution.py:40
  221.0 4.2 %fusion.79 = f32[8,8,1024]{2,1,0:T(8,128)S(1)} fusion(f32[2,8,128,1024]{3,2,1,0:T(8,128)} %get-tuple-element.538, f32[8,4,128]{2,1,0:T(4,128)S(1)} %copy.61, f32[8,4,128]{2,1,0:T(4,128)S(1)} %copy.62), kind=kOutput, calls=%fused_computation.2.clone.1 | convolution fusion | flops 100671488 | bytes 4489216 | tf_op jit(solution)/shard_map/while/body/eval_jaxpr/kxs,kst->kxt/dot_general | solution.py:91
  225.3 2.1 fusion.78
  227.9 0.7 pad_maximum_fusion.18
  228.6 5.3 %all-to-all-start.1 = ((f32[8,72,128]{2,1,0:T(8,128)}), f32[8,72,128]{2,1,0:T(8,128)S(1)}, u32[]{:S(2)}, u32[]{:S(2)}) async-start(f32[8,72,128]{2,1,0:T(8,128)} %pad_maximum_fusion.18), calls=%async_computation.1 | async-start | bytes 589824 | tf_op jit(solution)/shard_map/while/body/eval_jaxpr/all_to_all | solution.py:58
  233.9 6.8 %all-to-all-done.1 = f32[8,72,128]{2,1,0:T(8,128)S(1)} async-done(((f32[8,72,128]{2,1,0:T(8,128)}), f32[8,72,128]{2,1,0:T(8,128)S(1)}, u32[]{:S(2)}, u32[]{:S(2)}) %all-to-all-start.1) | async-done | bytes 294944 | tf_op jit(solution)/shard_map/while/body/eval_jaxpr/all_to_all | solution.py:58
  242.9 0.7 broadcast_in_dim.52
  243.5 13.9 %all_to_all.42 = f32[128,1,1]{2,1,0:T(1,128)S(1)} all-to-all(f32[128,1,1]{2,1,0:T(1,128)S(1)} %broadcast_in_dim.52), channel_id=1, replica_groups=mesh['mom'=16,'hist'=8] {'mom','hist'}, dimensions={0} | all-to-all | bytes 1024 | tf_op jit(solution)/shard_map/all_to_all | solution.py:124
  257.5 0.7 reduce_sum.83
  (175 shorter events, 20.7 us)
Async XLA Ops:
  2.6 25.3 %all-to-all-start.2 = ((f32[16,136,128]{2,1,0:T(8,128)}), f32[16,136,128]{2,1,0:T(8,128)S(1)}, u32[]{:S(2)}, u32[]{:S(2)}) async-start(f32[16,136,128]{2,1,0:T(8,128)} %broadcast_in_dim.50), calls=%async_computation.2 | async-start | bytes 2228224 | tf_op jit(solution)/shard_map/all_to_all | solution.py:40
  34.4 11.8 %copy-start.1 = (f32[2,8,4,128]{3,2,1,0:T(4,128)S(1)}, f32[2,8,4,128]{3,2,1,0:T(4,128)}, u32[]{:S(2)}) copy-start(f32[2,8,4,128]{3,2,1,0:T(4,128)} %param.8) | copy-start | bytes 98308
  39.2 13.7 %all-to-all-start.3 = ((f32[8,72,128]{2,1,0:T(8,128)}), f32[8,72,128]{2,1,0:T(8,128)S(1)}, u32[]{:S(2)}, u32[]{:S(2)}) async-start(f32[8,72,128]{2,1,0:T(8,128)} %pad_maximum_fusion.4), calls=%async_computation.3 | async-start | bytes 589824 | tf_op jit(solution)/shard_map/all_to_all | solution.py:58
  68.2 5.4 %copy-start = (f32[2,8,128,1024]{3,2,1,0:T(8,128)S(1)}, f32[2,8,128,1024]{3,2,1,0:T(8,128)}, u32[]{:S(2)}) copy-start(f32[2,8,128,1024]{3,2,1,0:T(8,128)} %get-tuple-element.538) | copy-start | bytes 25165828 | tf_op jit(solution)/shard_map/while
  76.9 12.2 %all-to-all-start.1 = ((f32[8,72,128]{2,1,0:T(8,128)}), f32[8,72,128]{2,1,0:T(8,128)S(1)}, u32[]{:S(2)}, u32[]{:S(2)}) async-start(f32[8,72,128]{2,1,0:T(8,128)} %pad_maximum_fusion.18), calls=%async_computation.1 | async-start | bytes 589824 | tf_op jit(solution)/shard_map/while/body/eval_jaxpr/all_to_all | solution.py:58
  106.2 5.3 %copy-start = (f32[2,8,128,1024]{3,2,1,0:T(8,128)S(1)}, f32[2,8,128,1024]{3,2,1,0:T(8,128)}, u32[]{:S(2)}) copy-start(f32[2,8,128,1024]{3,2,1,0:T(8,128)} %get-tuple-element.538) | copy-start | bytes 25165828 | tf_op jit(solution)/shard_map/while
  114.9 12.1 %all-to-all-start.1 = ((f32[8,72,128]{2,1,0:T(8,128)}), f32[8,72,128]{2,1,0:T(8,128)S(1)}, u32[]{:S(2)}, u32[]{:S(2)}) async-start(f32[8,72,128]{2,1,0:T(8,128)} %pad_maximum_fusion.18), calls=%async_computation.1 | async-start | bytes 589824 | tf_op jit(solution)/shard_map/while/body/eval_jaxpr/all_to_all | solution.py:58
  144.1 5.4 %copy-start = (f32[2,8,128,1024]{3,2,1,0:T(8,128)S(1)}, f32[2,8,128,1024]{3,2,1,0:T(8,128)}, u32[]{:S(2)}) copy-start(f32[2,8,128,1024]{3,2,1,0:T(8,128)} %get-tuple-element.538) | copy-start | bytes 25165828 | tf_op jit(solution)/shard_map/while
  152.8 12.1 %all-to-all-start.1 = ((f32[8,72,128]{2,1,0:T(8,128)}), f32[8,72,128]{2,1,0:T(8,128)S(1)}, u32[]{:S(2)}, u32[]{:S(2)}) async-start(f32[8,72,128]{2,1,0:T(8,128)} %pad_maximum_fusion.18), calls=%async_computation.1 | async-start | bytes 589824 | tf_op jit(solution)/shard_map/while/body/eval_jaxpr/all_to_all | solution.py:58
  182.0 5.3 %copy-start = (f32[2,8,128,1024]{3,2,1,0:T(8,128)S(1)}, f32[2,8,128,1024]{3,2,1,0:T(8,128)}, u32[]{:S(2)}) copy-start(f32[2,8,128,1024]{3,2,1,0:T(8,128)} %get-tuple-element.538) | copy-start | bytes 25165828 | tf_op jit(solution)/shard_map/while
  190.7 12.2 %all-to-all-start.1 = ((f32[8,72,128]{2,1,0:T(8,128)}), f32[8,72,128]{2,1,0:T(8,128)S(1)}, u32[]{:S(2)}, u32[]{:S(2)}) async-start(f32[8,72,128]{2,1,0:T(8,128)} %pad_maximum_fusion.18), calls=%async_computation.1 | async-start | bytes 589824 | tf_op jit(solution)/shard_map/while/body/eval_jaxpr/all_to_all | solution.py:58
  219.9 5.4 %copy-start = (f32[2,8,128,1024]{3,2,1,0:T(8,128)S(1)}, f32[2,8,128,1024]{3,2,1,0:T(8,128)}, u32[]{:S(2)}) copy-start(f32[2,8,128,1024]{3,2,1,0:T(8,128)} %get-tuple-element.538) | copy-start | bytes 25165828 | tf_op jit(solution)/shard_map/while
  228.6 12.1 %all-to-all-start.1 = ((f32[8,72,128]{2,1,0:T(8,128)}), f32[8,72,128]{2,1,0:T(8,128)S(1)}, u32[]{:S(2)}, u32[]{:S(2)}) async-start(f32[8,72,128]{2,1,0:T(8,128)} %pad_maximum_fusion.18), calls=%async_computation.1 | async-start | bytes 589824 | tf_op jit(solution)/shard_map/while/body/eval_jaxpr/all_to_all | solution.py:58
  259.6 0.5 copy-start.2

commit v6 on v5

--- a/solution.py
+++ b/solution.py
@@ -34,12 +34,9 @@
     return (cr[:, :n] + sr[:, n:], cr[:, n:] - sr[:, :n])
 
 
-def gather_rows(block, extra):
+def gather_rows(block):
     n_mom = lax.axis_size("mom")
-    packed = jnp.concatenate([block, jnp.full((8, 128), extra, block.dtype)])
-    got = lax.all_to_all(jnp.broadcast_to(packed, (n_mom,) + packed.shape), "mom", 0, 0, tiled=True)
-    n = block.shape[0]
-    return got[:, :n], got[:, n, 0]
+    return lax.all_to_all(jnp.broadcast_to(block, (n_mom,) + block.shape), "mom", 0, 0, tiled=True)
 
 
 def to_full_k(rows, lead, k_local, cols):
@@ -95,7 +92,7 @@
         return jnp.stack([real, imag])
 
     first = jnp.concatenate([screened.reshape(-1, 128), free_rows.reshape(-1, 128)])
-    rows, _ = gather_rows(first, jnp.float32(0.0))
+    rows = gather_rows(first)
     half = nb // 128
     screen_full = to_full_k(rows[:, :half], 2, k_local, cols)
     green_full = to_full_k(rows[:, half:], 2, k_local, cols)
@@ -105,10 +102,10 @@
     def correction(turn, carry):
         green, integral, deltas = carry
         change = free_rows + step_size * integral - green
-        local = jnp.sum(change * change)
-        rows, mom_sum = gather_rows(change.reshape(-1, 128), local)
+        rows = gather_rows(change.reshape(-1, 128))
+        mom_sums = jnp.sum(rows * rows, axis=(1, 2))
         full = to_full_k(rows, 2, k_local, cols)
-        step, total = hist_reduce(contract(sigma_of(full)), mom_sum, hist_n)
+        step, total = hist_reduce(contract(sigma_of(full)), mom_sums, hist_n)
         delta = jnp.sqrt(total / (2.0 * K * R * full_hist))
         deltas = lax.dynamic_update_slice(deltas, delta[None], (turn,))
         green = green + change / (1.0 + delta)

time: 261 us -> 249 us (0.954)
  blocking collectives: 83.9 us -> 78.9 us
  local copies, waits for them, and re-layouts: 9.96 us -> 5.49 us
    all_to_all x5, blocking collectives: 69.9 us -> 65.1 us  [gather_rows(): lax.all_to_all(jnp.broadcast_to(block, (n_mom,) + block.shape), 'mom', 0,...]
    concatenate x6 -> x0, local copies, waits for them, and re-layouts: 3.25 us -> none  [gather_rows(): packed = jnp.concatenate([block, jnp.full((8, 128), extra, block.dtype)])]
where the time goes in v6:
time: 249 us; the launch traced here: 248 us
  blocking collectives  78.9 us (32%)
  waiting for transfers between devices  56.1 us (23%)
  matrix products  45.8 us (18%)
  starting transfers between devices  42.7 us (17%)
  other arithmetic  13.5 us (5%)
  local copies, waits for them, and re-layouts  5.49 us (2%)
  loops' own time  4.23 us (2%)
    all_to_all x5, blocking collectives, gather_rows(): lax.all_to_all(jnp.broadcast_to(block, (n_mom,) + block.shape), 'mom', 0,...  65.1 us
    all_to_all x6, waiting for transfers between devices, hist_reduce(): y = lax.all_to_all(x, 'hist', 0, 0, tiled=True)  40.5 us
    all_to_all x6, starting transfers between devices, hist_reduce(): y = lax.all_to_all(x, 'hist', 0, 0, tiled=True)  34.1 us
    dot_general x6, matrix products, contract(): a = jnp.einsum('kxs,kst->kxt', x, hist_panel[0], precision=HIGHEST)  25.1 us
    all_to_all x1, waiting for transfers between devices, gather_rows(): lax.all_to_all(jnp.broadcast_to(block, (n_mom,) + block.shape), 'mom', 0,...  15.6 us
    dot_general x6, matrix products, contract(): b = jnp.einsum('kxs,kst->kxt', x, hist_panel[1], precision=HIGHEST)  14.2 us
    all_to_all x1, blocking collectives, shards(): total = jnp.sum(lax.all_to_all(spread, ('mom', 'hist'), 0, 0, tiled=True))  13.8 us
    all_to_all x1, starting transfers between devices, gather_rows(): lax.all_to_all(jnp.broadcast_to(block, (n_mom,) + block.shape), 'mom', 0,...  8.59 us
  transfers between devices with their start and end apart: 7, of which 7 were waited for; matrix products, arithmetic and copies ran while one was open for 0% of the time, Pallas kernels for 0%

profile of v6, /device:TPU:1, one launch (start us, length us, event | category | flops | bytes accessed | tf_op | source)
XLA Modules:
  0.0 248.3 jit_solution(9012534777268409329)
XLA Ops:
  0.6 0.8 pad_maximum_fusion.6
  1.4 1.1 broadcast_in_dim.53
  2.5 8.6 %all-to-all-start.2 = ((f32[16,128,128]{2,1,0:T(8,128)}), f32[16,128,128]{2,1,0:T(8,128)S(1)}, u32[]{:S(2)}, u32[]{:S(2)}) async-start(f32[16,128,128]{2,1,0:T(8,128)} %broadcast_in_dim.53), calls=%async_computation.2 | async-start | bytes 2097152 | tf_op jit(solution)/shard_map/all_to_all | solution.py:39
  11.5 15.6 %all-to-all-done.2 = f32[16,128,128]{2,1,0:T(8,128)S(1)} async-done(((f32[16,128,128]{2,1,0:T(8,128)}), f32[16,128,128]{2,1,0:T(8,128)S(1)}, u32[]{:S(2)}, u32[]{:S(2)}) %all-to-all-start.2) | async-done | bytes 1048608 | tf_op jit(solution)/shard_map/all_to_all | solution.py:39
  28.1 1.0 fusion.29
  29.7 3.8 %fusion.21 = f32[8,8,1024]{2,1,0:T(8,128)S(1)} fusion(f32[2,8,128,1024]{3,2,1,0:T(8,128)} %param.7, f32[8,4,128]{2,1,0:T(4,128)S(1)} %copy.31, f32[8,4,128]{2,1,0:T(4,128)S(1)} %copy.30), kind=kOutput, calls=%fused_computation.42 | convolution fusion | flops 100671488 | bytes 4489216 | tf_op jit(solution)/shard_map/kxs,kst->kxt/dot_general | solution.py:88
  33.5 3.8 %fusion.19 = f32[8,8,1024]{2,1,0:T(8,128)S(1)} fusion(f32[2,8,128,1024]{3,2,1,0:T(8,128)} %param.7, f32[8,4,128]{2,1,0:T(4,128)S(1)} %copy.31, f32[8,4,128]{2,1,0:T(4,128)S(1)} %copy.30), kind=kOutput, calls=%fused_computation.40 | convolution fusion | flops 100671488 | bytes 4489216 | tf_op jit(solution)/shard_map/kxs,kst->kxt/dot_general | solution.py:89
  37.6 0.7 pad_maximum_fusion.4
  38.4 6.9 %all-to-all-start.3 = ((f32[8,72,128]{2,1,0:T(8,128)}), f32[8,72,128]{2,1,0:T(8,128)S(1)}, u32[]{:S(2)}, u32[]{:S(2)}) async-start(f32[8,72,128]{2,1,0:T(8,128)} %pad_maximum_fusion.4), calls=%async_computation.3 | async-start | bytes 589824 | tf_op jit(solution)/shard_map/all_to_all | solution.py:55
  45.6 6.5 %all-to-all-done.3 = f32[8,72,128]{2,1,0:T(8,128)S(1)} async-done(((f32[8,72,128]{2,1,0:T(8,128)}), f32[8,72,128]{2,1,0:T(8,128)S(1)}, u32[]{:S(2)}, u32[]{:S(2)}) %all-to-all-start.3) | async-done | bytes 294944 | tf_op jit(solution)/shard_map/all_to_all | solution.py:55
  52.1 178.5 %while.20 = (s32[]{:T(128)}, f32[2,8,4,128]{3,2,1,0:T(4,128)S(1)}, f32[2,8,4,128]{3,2,1,0:T(4,128)S(1)}, f32[6]{0:T(128)S(1)}, f32[2,8,4,128]{3,2,1,0:T(4,128)S(...) while((s32[]{:T(128)}, f32[2,8,4,128]{3,2,1,0:T(4,128)S(1)}, ...), condition=%wide.region_5.6_spmd, body=%wide.region_1.5_spmd.sunk | while | flops 416632960 | bytes 55886724 | solution.py:116
  52.2 13.2 %all_to_all.43 = f32[16,64,128]{2,1,0:T(8,128)S(1)} all-to-all(f32[16,64,128]{2,1,0:T(8,128)S(1)} %broadcast_in_dim.58), channel_id=1, replica_groups=mesh['mom'=16,'hist'=8] {'mom'}, dimensions={0} | all-to-all | bytes 1048576 | tf_op jit(solution)/shard_map/while/body/eval_jaxpr/all_to_all | solution.py:39
  66.6 4.3 %fusion.79 = f32[8,8,1024]{2,1,0:T(8,128)S(1)} fusion(f32[2,8,128,1024]{3,2,1,0:T(8,128)} %get-tuple-element.502, f32[8,4,128]{2,1,0:T(4,128)S(1)} %copy.40, f32[8,4,128]{2,1,0:T(4,128)S(1)} %copy.41), kind=kOutput, calls=%fused_computation.2.clone.1 | convolution fusion | flops 100671488 | bytes 4489216 | tf_op jit(solution)/shard_map/while/body/eval_jaxpr/kxs,kst->kxt/dot_general | solution.py:88
  70.9 2.1 fusion.78
  73.5 0.7 pad_maximum_fusion.19
  74.2 5.2 %all-to-all-start.1 = ((f32[8,72,128]{2,1,0:T(8,128)}), f32[8,72,128]{2,1,0:T(8,128)S(1)}, u32[]{:S(2)}, u32[]{:S(2)}) async-start(f32[8,72,128]{2,1,0:T(8,128)} %pad_maximum_fusion.19), calls=%async_computation.1 | async-start | bytes 589824 | tf_op jit(solution)/shard_map/while/body/eval_jaxpr/all_to_all | solution.py:55
  79.5 6.8 %all-to-all-done.1 = f32[8,72,128]{2,1,0:T(8,128)S(1)} async-done(((f32[8,72,128]{2,1,0:T(8,128)}), f32[8,72,128]{2,1,0:T(8,128)S(1)}, u32[]{:S(2)}, u32[]{:S(2)}) %all-to-all-start.1) | async-done | bytes 294944 | tf_op jit(solution)/shard_map/while/body/eval_jaxpr/all_to_all | solution.py:55
  87.8 13.0 %all_to_all.43 = f32[16,64,128]{2,1,0:T(8,128)S(1)} all-to-all(f32[16,64,128]{2,1,0:T(8,128)S(1)} %broadcast_in_dim.58), channel_id=1, replica_groups=mesh['mom'=16,'hist'=8] {'mom'}, dimensions={0} | all-to-all | bytes 1048576 | tf_op jit(solution)/shard_map/while/body/eval_jaxpr/all_to_all | solution.py:39
  100.9 0.6 convolution_bitcast_fusion.4
  102.0 4.3 %fusion.79 = f32[8,8,1024]{2,1,0:T(8,128)S(1)} fusion(f32[2,8,128,1024]{3,2,1,0:T(8,128)} %get-tuple-element.502, f32[8,4,128]{2,1,0:T(4,128)S(1)} %copy.40, f32[8,4,128]{2,1,0:T(4,128)S(1)} %copy.41), kind=kOutput, calls=%fused_computation.2.clone.1 | convolution fusion | flops 100671488 | bytes 4489216 | tf_op jit(solution)/shard_map/while/body/eval_jaxpr/kxs,kst->kxt/dot_general | solution.py:88
  106.3 2.1 fusion.78
  108.9 0.7 pad_maximum_fusion.19
  109.7 5.5 %all-to-all-start.1 = ((f32[8,72,128]{2,1,0:T(8,128)}), f32[8,72,128]{2,1,0:T(8,128)S(1)}, u32[]{:S(2)}, u32[]{:S(2)}) async-start(f32[8,72,128]{2,1,0:T(8,128)} %pad_maximum_fusion.19), calls=%async_computation.1 | async-start | bytes 589824 | tf_op jit(solution)/shard_map/while/body/eval_jaxpr/all_to_all | solution.py:55
  115.2 6.8 %all-to-all-done.1 = f32[8,72,128]{2,1,0:T(8,128)S(1)} async-done(((f32[8,72,128]{2,1,0:T(8,128)}), f32[8,72,128]{2,1,0:T(8,128)S(1)}, u32[]{:S(2)}, u32[]{:S(2)}) %all-to-all-start.1) | async-done | bytes 294944 | tf_op jit(solution)/shard_map/while/body/eval_jaxpr/all_to_all | solution.py:55
  123.5 13.0 %all_to_all.43 = f32[16,64,128]{2,1,0:T(8,128)S(1)} all-to-all(f32[16,64,128]{2,1,0:T(8,128)S(1)} %broadcast_in_dim.58), channel_id=1, replica_groups=mesh['mom'=16,'hist'=8] {'mom'}, dimensions={0} | all-to-all | bytes 1048576 | tf_op jit(solution)/shard_map/while/body/eval_jaxpr/all_to_all | solution.py:39
  137.7 4.3 %fusion.79 = f32[8,8,1024]{2,1,0:T(8,128)S(1)} fusion(f32[2,8,128,1024]{3,2,1,0:T(8,128)} %get-tuple-element.502, f32[8,4,128]{2,1,0:T(4,128)S(1)} %copy.40, f32[8,4,128]{2,1,0:T(4,128)S(1)} %copy.41), kind=kOutput, calls=%fused_computation.2.clone.1 | convolution fusion | flops 100671488 | bytes 4489216 | tf_op jit(solution)/shard_map/while/body/eval_jaxpr/kxs,kst->kxt/dot_general | solution.py:88
  142.0 2.1 fusion.78
  144.6 0.7 pad_maximum_fusion.19
  145.4 5.5 %all-to-all-start.1 = ((f32[8,72,128]{2,1,0:T(8,128)}), f32[8,72,128]{2,1,0:T(8,128)S(1)}, u32[]{:S(2)}, u32[]{:S(2)}) async-start(f32[8,72,128]{2,1,0:T(8,128)} %pad_maximum_fusion.19), calls=%async_computation.1 | async-start | bytes 589824 | tf_op jit(solution)/shard_map/while/body/eval_jaxpr/all_to_all | solution.py:55
  150.9 6.8 %all-to-all-done.1 = f32[8,72,128]{2,1,0:T(8,128)S(1)} async-done(((f32[8,72,128]{2,1,0:T(8,128)}), f32[8,72,128]{2,1,0:T(8,128)S(1)}, u32[]{:S(2)}, u32[]{:S(2)}) %all-to-all-start.1) | async-done | bytes 294944 | tf_op jit(solution)/shard_map/while/body/eval_jaxpr/all_to_all | solution.py:55
  159.3 13.0 %all_to_all.43 = f32[16,64,128]{2,1,0:T(8,128)S(1)} all-to-all(f32[16,64,128]{2,1,0:T(8,128)S(1)} %broadcast_in_dim.58), channel_id=1, replica_groups=mesh['mom'=16,'hist'=8] {'mom'}, dimensions={0} | all-to-all | bytes 1048576 | tf_op jit(solution)/shard_map/while/body/eval_jaxpr/all_to_all | solution.py:39
  172.4 0.6 convolution_bitcast_fusion.4
  173.5 4.3 %fusion.79 = f32[8,8,1024]{2,1,0:T(8,128)S(1)} fusion(f32[2,8,128,1024]{3,2,1,0:T(8,128)} %get-tuple-element.502, f32[8,4,128]{2,1,0:T(4,128)S(1)} %copy.40, f32[8,4,128]{2,1,0:T(4,128)S(1)} %copy.41), kind=kOutput, calls=%fused_computation.2.clone.1 | convolution fusion | flops 100671488 | bytes 4489216 | tf_op jit(solution)/shard_map/while/body/eval_jaxpr/kxs,kst->kxt/dot_general | solution.py:88
  177.8 2.1 fusion.78
  180.4 0.7 pad_maximum_fusion.19
  181.1 5.5 %all-to-all-start.1 = ((f32[8,72,128]{2,1,0:T(8,128)}), f32[8,72,128]{2,1,0:T(8,128)S(1)}, u32[]{:S(2)}, u32[]{:S(2)}) async-start(f32[8,72,128]{2,1,0:T(8,128)} %pad_maximum_fusion.19), calls=%async_computation.1 | async-start | bytes 589824 | tf_op jit(solution)/shard_map/while/body/eval_jaxpr/all_to_all | solution.py:55
  186.6 6.8 %all-to-all-done.1 = f32[8,72,128]{2,1,0:T(8,128)S(1)} async-done(((f32[8,72,128]{2,1,0:T(8,128)}), f32[8,72,128]{2,1,0:T(8,128)S(1)}, u32[]{:S(2)}, u32[]{:S(2)}) %all-to-all-start.1) | async-done | bytes 294944 | tf_op jit(solution)/shard_map/while/body/eval_jaxpr/all_to_all | solution.py:55
  195.0 13.0 %all_to_all.43 = f32[16,64,128]{2,1,0:T(8,128)S(1)} all-to-all(f32[16,64,128]{2,1,0:T(8,128)S(1)} %broadcast_in_dim.58), channel_id=1, replica_groups=mesh['mom'=16,'hist'=8] {'mom'}, dimensions={0} | all-to-all | bytes 1048576 | tf_op jit(solution)/shard_map/while/body/eval_jaxpr/all_to_all | solution.py:39
  209.2 4.3 %fusion.79 = f32[8,8,1024]{2,1,0:T(8,128)S(1)} fusion(f32[2,8,128,1024]{3,2,1,0:T(8,128)} %get-tuple-element.502, f32[8,4,128]{2,1,0:T(4,128)S(1)} %copy.40, f32[8,4,128]{2,1,0:T(4,128)S(1)} %copy.41), kind=kOutput, calls=%fused_computation.2.clone.1 | convolution fusion | flops 100671488 | bytes 4489216 | tf_op jit(solution)/shard_map/while/body/eval_jaxpr/kxs,kst->kxt/dot_general | solution.py:88
  213.5 2.1 fusion.78
  216.1 0.7 pad_maximum_fusion.19
  216.8 5.5 %all-to-all-start.1 = ((f32[8,72,128]{2,1,0:T(8,128)}), f32[8,72,128]{2,1,0:T(8,128)S(1)}, u32[]{:S(2)}, u32[]{:S(2)}) async-start(f32[8,72,128]{2,1,0:T(8,128)} %pad_maximum_fusion.19), calls=%async_computation.1 | async-start | bytes 589824 | tf_op jit(solution)/shard_map/while/body/eval_jaxpr/all_to_all | solution.py:55
  222.3 6.8 %all-to-all-done.1 = f32[8,72,128]{2,1,0:T(8,128)S(1)} async-done(((f32[8,72,128]{2,1,0:T(8,128)}), f32[8,72,128]{2,1,0:T(8,128)S(1)}, u32[]{:S(2)}, u32[]{:S(2)}) %all-to-all-start.1) | async-done | bytes 294944 | tf_op jit(solution)/shard_map/while/body/eval_jaxpr/all_to_all | solution.py:55
  230.6 0.6 multiply_reduce_fusion.1
  231.2 0.7 broadcast_in_dim.55
  231.9 13.8 %all_to_all.42 = f32[128,1,1]{2,1,0:T(1,128)S(1)} all-to-all(f32[128,1,1]{2,1,0:T(1,128)S(1)} %broadcast_in_dim.55), channel_id=1, replica_groups=mesh['mom'=16,'hist'=8] {'mom','hist'}, dimensions={0} | all-to-all | bytes 1024 | tf_op jit(solution)/shard_map/all_to_all | solution.py:121
  245.7 0.7 reduce_sum.83
  247.1 0.6 divide_add_fusion.1
  (163 shorter events, 14.3 us)
Async XLA Ops:
  2.5 24.6 %all-to-all-start.2 = ((f32[16,128,128]{2,1,0:T(8,128)}), f32[16,128,128]{2,1,0:T(8,128)S(1)}, u32[]{:S(2)}, u32[]{:S(2)}) async-start(f32[16,128,128]{2,1,0:T(8,128)} %broadcast_in_dim.53), calls=%async_computation.2 | async-start | bytes 2097152 | tf_op jit(solution)/shard_map/all_to_all | solution.py:39
  29.0 16.2 %copy-start.1 = (f32[2,8,4,128]{3,2,1,0:T(4,128)S(1)}, f32[2,8,4,128]{3,2,1,0:T(4,128)}, u32[]{:S(2)}) copy-start(f32[2,8,4,128]{3,2,1,0:T(4,128)} %param.8) | copy-start | bytes 98308
  38.4 13.7 %all-to-all-start.3 = ((f32[8,72,128]{2,1,0:T(8,128)}), f32[8,72,128]{2,1,0:T(8,128)S(1)}, u32[]{:S(2)}, u32[]{:S(2)}) async-start(f32[8,72,128]{2,1,0:T(8,128)} %pad_maximum_fusion.4), calls=%async_computation.3 | async-start | bytes 589824 | tf_op jit(solution)/shard_map/all_to_all | solution.py:55
  65.5 5.4 %copy-start = (f32[2,8,128,1024]{3,2,1,0:T(8,128)S(1)}, f32[2,8,128,1024]{3,2,1,0:T(8,128)}, u32[]{:S(2)}) copy-start(f32[2,8,128,1024]{3,2,1,0:T(8,128)} %get-tuple-element.502) | copy-start | bytes 25165828 | tf_op jit(solution)/shard_map/while
  74.2 12.0 %all-to-all-start.1 = ((f32[8,72,128]{2,1,0:T(8,128)}), f32[8,72,128]{2,1,0:T(8,128)S(1)}, u32[]{:S(2)}, u32[]{:S(2)}) async-start(f32[8,72,128]{2,1,0:T(8,128)} %pad_maximum_fusion.19), calls=%async_computation.1 | async-start | bytes 589824 | tf_op jit(solution)/shard_map/while/body/eval_jaxpr/all_to_all | solution.py:55
  100.9 5.4 %copy-start = (f32[2,8,128,1024]{3,2,1,0:T(8,128)S(1)}, f32[2,8,128,1024]{3,2,1,0:T(8,128)}, u32[]{:S(2)}) copy-start(f32[2,8,128,1024]{3,2,1,0:T(8,128)} %get-tuple-element.502) | copy-start | bytes 25165828 | tf_op jit(solution)/shard_map/while
  109.7 12.3 %all-to-all-start.1 = ((f32[8,72,128]{2,1,0:T(8,128)}), f32[8,72,128]{2,1,0:T(8,128)S(1)}, u32[]{:S(2)}, u32[]{:S(2)}) async-start(f32[8,72,128]{2,1,0:T(8,128)} %pad_maximum_fusion.19), calls=%async_computation.1 | async-start | bytes 589824 | tf_op jit(solution)/shard_map/while/body/eval_jaxpr/all_to_all | solution.py:55
  136.6 5.4 %copy-start = (f32[2,8,128,1024]{3,2,1,0:T(8,128)S(1)}, f32[2,8,128,1024]{3,2,1,0:T(8,128)}, u32[]{:S(2)}) copy-start(f32[2,8,128,1024]{3,2,1,0:T(8,128)} %get-tuple-element.502) | copy-start | bytes 25165828 | tf_op jit(solution)/shard_map/while
  145.4 12.3 %all-to-all-start.1 = ((f32[8,72,128]{2,1,0:T(8,128)}), f32[8,72,128]{2,1,0:T(8,128)S(1)}, u32[]{:S(2)}, u32[]{:S(2)}) async-start(f32[8,72,128]{2,1,0:T(8,128)} %pad_maximum_fusion.19), calls=%async_computation.1 | async-start | bytes 589824 | tf_op jit(solution)/shard_map/while/body/eval_jaxpr/all_to_all | solution.py:55
  172.3 5.4 %copy-start = (f32[2,8,128,1024]{3,2,1,0:T(8,128)S(1)}, f32[2,8,128,1024]{3,2,1,0:T(8,128)}, u32[]{:S(2)}) copy-start(f32[2,8,128,1024]{3,2,1,0:T(8,128)} %get-tuple-element.502) | copy-start | bytes 25165828 | tf_op jit(solution)/shard_map/while
  181.1 12.3 %all-to-all-start.1 = ((f32[8,72,128]{2,1,0:T(8,128)}), f32[8,72,128]{2,1,0:T(8,128)S(1)}, u32[]{:S(2)}, u32[]{:S(2)}) async-start(f32[8,72,128]{2,1,0:T(8,128)} %pad_maximum_fusion.19), calls=%async_computation.1 | async-start | bytes 589824 | tf_op jit(solution)/shard_map/while/body/eval_jaxpr/all_to_all | solution.py:55
  208.0 5.4 %copy-start = (f32[2,8,128,1024]{3,2,1,0:T(8,128)S(1)}, f32[2,8,128,1024]{3,2,1,0:T(8,128)}, u32[]{:S(2)}) copy-start(f32[2,8,128,1024]{3,2,1,0:T(8,128)} %get-tuple-element.502) | copy-start | bytes 25165828 | tf_op jit(solution)/shard_map/while
  216.8 12.3 %all-to-all-start.1 = ((f32[8,72,128]{2,1,0:T(8,128)}), f32[8,72,128]{2,1,0:T(8,128)S(1)}, u32[]{:S(2)}, u32[]{:S(2)}) async-start(f32[8,72,128]{2,1,0:T(8,128)} %pad_maximum_fusion.19), calls=%async_computation.1 | async-start | bytes 589824 | tf_op jit(solution)/shard_map/while/body/eval_jaxpr/all_to_all | solution.py:55
  247.8 0.5 copy-start.2

commit v7 on v6

--- a/solution.py
+++ b/solution.py
@@ -70,12 +70,12 @@
     sin_own = sin_own / K
     nb = 2 * k_local * R * cols
 
-    def sigma_of(full):
-        hr, hi = dft(cosine, sine, full[0], full[1], lax.Precision.HIGH)
+    def sigma_of(full, precision=lax.Precision.HIGH):
+        hr, hi = dft(cosine, sine, full[0], full[1], precision)
         pr = hr * screen_hat[0] - hi * screen_hat[1]
         pi = hr * screen_hat[1] + hi * screen_hat[0]
         both = jnp.concatenate([pr, pi], axis=1)
-        out = mm(jnp.concatenate([cos_own, sin_own]), both, lax.Precision.HIGH)
+        out = mm(jnp.concatenate([cos_own, sin_own]), both, precision)
         cb = out[:k_local]
         sb = out[k_local:]
         n = pr.shape[1]
@@ -98,7 +98,7 @@
     green_full = to_full_k(rows[:, half:], 2, k_local, cols)
     screen_hat = dft(cosine, sine, screen_full[0], screen_full[1])
 
-    integral, _ = hist_reduce(contract(sigma_of(green_full)), jnp.zeros((lax.axis_size("mom"),), jnp.float32), hist_n)
+    integral, _ = hist_reduce(contract(sigma_of(green_full, HIGHEST)), jnp.zeros((lax.axis_size("mom"),), jnp.float32), hist_n)
     def correction(turn, carry):
         green, integral, deltas = carry
         change = free_rows + step_size * integral - green

time: 249 us -> 250 us (level)
  no operation moved by 1% of the time
where the time goes in v7:
time: 250 us; the launch traced here: 249 us
  blocking collectives  78.9 us (32%)
  waiting for transfers between devices  56.1 us (22%)
  matrix products  46.4 us (19%)
  starting transfers between devices  42.7 us (17%)
  other arithmetic  13.5 us (5%)
  local copies, waits for them, and re-layouts  5.49 us (2%)
  loops' own time  4.23 us (2%)
    all_to_all x5, blocking collectives, gather_rows(): lax.all_to_all(jnp.broadcast_to(block, (n_mom,) + block.shape), 'mom', 0,...  65.2 us
    all_to_all x6, waiting for transfers between devices, hist_reduce(): y = lax.all_to_all(x, 'hist', 0, 0, tiled=True)  40.5 us
    all_to_all x6, starting transfers between devices, hist_reduce(): y = lax.all_to_all(x, 'hist', 0, 0, tiled=True)  34.1 us
    dot_general x6, matrix products, contract(): a = jnp.einsum('kxs,kst->kxt', x, hist_panel[0], precision=HIGHEST)  25.1 us
    all_to_all x1, waiting for transfers between devices, gather_rows(): lax.all_to_all(jnp.broadcast_to(block, (n_mom,) + block.shape), 'mom', 0,...  15.6 us
    dot_general x6, matrix products, contract(): b = jnp.einsum('kxs,kst->kxt', x, hist_panel[1], precision=HIGHEST)  14.2 us
    all_to_all x1, blocking collectives, shards(): total = jnp.sum(lax.all_to_all(spread, ('mom', 'hist'), 0, 0, tiled=True))  13.8 us
    all_to_all x1, starting transfers between devices, gather_rows(): lax.all_to_all(jnp.broadcast_to(block, (n_mom,) + block.shape), 'mom', 0,...  8.59 us
  transfers between devices with their start and end apart: 7, of which 7 were waited for; matrix products, arithmetic and copies ran while one was open for 0% of the time, Pallas kernels for 0%

profile of v7, /device:TPU:1, one launch (start us, length us, event | category | flops | bytes accessed | tf_op | source)
XLA Modules:
  0.0 248.8 jit_solution(16020883886259150117)
XLA Ops:
  0.6 0.8 pad_maximum_fusion.6
  1.4 1.1 broadcast_in_dim.53
  2.5 8.6 %all-to-all-start.2 = ((f32[16,128,128]{2,1,0:T(8,128)}), f32[16,128,128]{2,1,0:T(8,128)S(1)}, u32[]{:S(2)}, u32[]{:S(2)}) async-start(f32[16,128,128]{2,1,0:T(8,128)} %broadcast_in_dim.53), calls=%async_computation.2 | async-start | bytes 2097152 | tf_op jit(solution)/shard_map/all_to_all | solution.py:39
  11.5 15.6 %all-to-all-done.2 = f32[16,128,128]{2,1,0:T(8,128)S(1)} async-done(((f32[16,128,128]{2,1,0:T(8,128)}), f32[16,128,128]{2,1,0:T(8,128)S(1)}, u32[]{:S(2)}, u32[]{:S(2)}) %all-to-all-start.2) | async-done | bytes 1048608 | tf_op jit(solution)/shard_map/all_to_all | solution.py:39
  27.5 1.0 fusion.25
  28.5 1.0 fusion.29
  30.3 3.8 %fusion.21 = f32[8,8,1024]{2,1,0:T(8,128)S(1)} fusion(f32[2,8,128,1024]{3,2,1,0:T(8,128)} %param.7, f32[8,4,128]{2,1,0:T(4,128)S(1)} %copy.31, f32[8,4,128]{2,1,0:T(4,128)S(1)} %copy.30), kind=kOutput, calls=%fused_computation.42 | convolution fusion | flops 100671488 | bytes 4489216 | tf_op jit(solution)/shard_map/kxs,kst->kxt/dot_general | solution.py:88
  34.1 3.8 %fusion.19 = f32[8,8,1024]{2,1,0:T(8,128)S(1)} fusion(f32[2,8,128,1024]{3,2,1,0:T(8,128)} %param.7, f32[8,4,128]{2,1,0:T(4,128)S(1)} %copy.31, f32[8,4,128]{2,1,0:T(4,128)S(1)} %copy.30), kind=kOutput, calls=%fused_computation.40 | convolution fusion | flops 100671488 | bytes 4489216 | tf_op jit(solution)/shard_map/kxs,kst->kxt/dot_general | solution.py:89
  38.2 0.7 pad_maximum_fusion.4
  38.9 6.9 %all-to-all-start.3 = ((f32[8,72,128]{2,1,0:T(8,128)}), f32[8,72,128]{2,1,0:T(8,128)S(1)}, u32[]{:S(2)}, u32[]{:S(2)}) async-start(f32[8,72,128]{2,1,0:T(8,128)} %pad_maximum_fusion.4), calls=%async_computation.3 | async-start | bytes 589824 | tf_op jit(solution)/shard_map/all_to_all | solution.py:55
  46.1 6.5 %all-to-all-done.3 = f32[8,72,128]{2,1,0:T(8,128)S(1)} async-done(((f32[8,72,128]{2,1,0:T(8,128)}), f32[8,72,128]{2,1,0:T(8,128)S(1)}, u32[]{:S(2)}, u32[]{:S(2)}) %all-to-all-start.3) | async-done | bytes 294944 | tf_op jit(solution)/shard_map/all_to_all | solution.py:55
  52.6 178.6 %while.20 = (s32[]{:T(128)}, f32[2,8,4,128]{3,2,1,0:T(4,128)S(1)}, f32[2,8,4,128]{3,2,1,0:T(4,128)S(1)}, f32[6]{0:T(128)S(1)}, f32[2,8,4,128]{3,2,1,0:T(4,128)S(...) while((s32[]{:T(128)}, f32[2,8,4,128]{3,2,1,0:T(4,128)S(1)}, ...), condition=%wide.region_5.6_spmd, body=%wide.region_1.5_spmd.sunk | while | flops 416632960 | bytes 55886724 | solution.py:116
  52.7 13.2 %all_to_all.43 = f32[16,64,128]{2,1,0:T(8,128)S(1)} all-to-all(f32[16,64,128]{2,1,0:T(8,128)S(1)} %broadcast_in_dim.58), channel_id=1, replica_groups=mesh['mom'=16,'hist'=8] {'mom'}, dimensions={0} | all-to-all | bytes 1048576 | tf_op jit(solution)/shard_map/while/body/eval_jaxpr/all_to_all | solution.py:39
  67.1 4.3 %fusion.79 = f32[8,8,1024]{2,1,0:T(8,128)S(1)} fusion(f32[2,8,128,1024]{3,2,1,0:T(8,128)} %get-tuple-element.502, f32[8,4,128]{2,1,0:T(4,128)S(1)} %copy.40, f32[8,4,128]{2,1,0:T(4,128)S(1)} %copy.41), kind=kOutput, calls=%fused_computation.2.clone.1 | convolution fusion | flops 100671488 | bytes 4489216 | tf_op jit(solution)/shard_map/while/body/eval_jaxpr/kxs,kst->kxt/dot_general | solution.py:88
  71.4 2.1 fusion.78
  74.0 0.7 pad_maximum_fusion.19
  74.8 5.2 %all-to-all-start.1 = ((f32[8,72,128]{2,1,0:T(8,128)}), f32[8,72,128]{2,1,0:T(8,128)S(1)}, u32[]{:S(2)}, u32[]{:S(2)}) async-start(f32[8,72,128]{2,1,0:T(8,128)} %pad_maximum_fusion.19), calls=%async_computation.1 | async-start | bytes 589824 | tf_op jit(solution)/shard_map/while/body/eval_jaxpr/all_to_all | solution.py:55
  80.0 6.8 %all-to-all-done.1 = f32[8,72,128]{2,1,0:T(8,128)S(1)} async-done(((f32[8,72,128]{2,1,0:T(8,128)}), f32[8,72,128]{2,1,0:T(8,128)S(1)}, u32[]{:S(2)}, u32[]{:S(2)}) %all-to-all-start.1) | async-done | bytes 294944 | tf_op jit(solution)/shard_map/while/body/eval_jaxpr/all_to_all | solution.py:55
  88.3 13.0 %all_to_all.43 = f32[16,64,128]{2,1,0:T(8,128)S(1)} all-to-all(f32[16,64,128]{2,1,0:T(8,128)S(1)} %broadcast_in_dim.58), channel_id=1, replica_groups=mesh['mom'=16,'hist'=8] {'mom'}, dimensions={0} | all-to-all | bytes 1048576 | tf_op jit(solution)/shard_map/while/body/eval_jaxpr/all_to_all | solution.py:39
  102.6 4.3 %fusion.79 = f32[8,8,1024]{2,1,0:T(8,128)S(1)} fusion(f32[2,8,128,1024]{3,2,1,0:T(8,128)} %get-tuple-element.502, f32[8,4,128]{2,1,0:T(4,128)S(1)} %copy.40, f32[8,4,128]{2,1,0:T(4,128)S(1)} %copy.41), kind=kOutput, calls=%fused_computation.2.clone.1 | convolution fusion | flops 100671488 | bytes 4489216 | tf_op jit(solution)/shard_map/while/body/eval_jaxpr/kxs,kst->kxt/dot_general | solution.py:88
  106.8 2.1 fusion.78
  109.4 0.7 pad_maximum_fusion.19
  110.2 5.5 %all-to-all-start.1 = ((f32[8,72,128]{2,1,0:T(8,128)}), f32[8,72,128]{2,1,0:T(8,128)S(1)}, u32[]{:S(2)}, u32[]{:S(2)}) async-start(f32[8,72,128]{2,1,0:T(8,128)} %pad_maximum_fusion.19), calls=%async_computation.1 | async-start | bytes 589824 | tf_op jit(solution)/shard_map/while/body/eval_jaxpr/all_to_all | solution.py:55
  115.7 6.8 %all-to-all-done.1 = f32[8,72,128]{2,1,0:T(8,128)S(1)} async-done(((f32[8,72,128]{2,1,0:T(8,128)}), f32[8,72,128]{2,1,0:T(8,128)S(1)}, u32[]{:S(2)}, u32[]{:S(2)}) %all-to-all-start.1) | async-done | bytes 294944 | tf_op jit(solution)/shard_map/while/body/eval_jaxpr/all_to_all | solution.py:55
  124.1 13.0 %all_to_all.43 = f32[16,64,128]{2,1,0:T(8,128)S(1)} all-to-all(f32[16,64,128]{2,1,0:T(8,128)S(1)} %broadcast_in_dim.58), channel_id=1, replica_groups=mesh['mom'=16,'hist'=8] {'mom'}, dimensions={0} | all-to-all | bytes 1048576 | tf_op jit(solution)/shard_map/while/body/eval_jaxpr/all_to_all | solution.py:39
  138.3 4.3 %fusion.79 = f32[8,8,1024]{2,1,0:T(8,128)S(1)} fusion(f32[2,8,128,1024]{3,2,1,0:T(8,128)} %get-tuple-element.502, f32[8,4,128]{2,1,0:T(4,128)S(1)} %copy.40, f32[8,4,128]{2,1,0:T(4,128)S(1)} %copy.41), kind=kOutput, calls=%fused_computation.2.clone.1 | convolution fusion | flops 100671488 | bytes 4489216 | tf_op jit(solution)/shard_map/while/body/eval_jaxpr/kxs,kst->kxt/dot_general | solution.py:88
  142.6 2.1 fusion.78
  145.2 0.7 pad_maximum_fusion.19
  145.9 5.5 %all-to-all-start.1 = ((f32[8,72,128]{2,1,0:T(8,128)}), f32[8,72,128]{2,1,0:T(8,128)S(1)}, u32[]{:S(2)}, u32[]{:S(2)}) async-start(f32[8,72,128]{2,1,0:T(8,128)} %pad_maximum_fusion.19), calls=%async_computation.1 | async-start | bytes 589824 | tf_op jit(solution)/shard_map/while/body/eval_jaxpr/all_to_all | solution.py:55
  151.4 6.8 %all-to-all-done.1 = f32[8,72,128]{2,1,0:T(8,128)S(1)} async-done(((f32[8,72,128]{2,1,0:T(8,128)}), f32[8,72,128]{2,1,0:T(8,128)S(1)}, u32[]{:S(2)}, u32[]{:S(2)}) %all-to-all-start.1) | async-done | bytes 294944 | tf_op jit(solution)/shard_map/while/body/eval_jaxpr/all_to_all | solution.py:55
  159.8 13.0 %all_to_all.43 = f32[16,64,128]{2,1,0:T(8,128)S(1)} all-to-all(f32[16,64,128]{2,1,0:T(8,128)S(1)} %broadcast_in_dim.58), channel_id=1, replica_groups=mesh['mom'=16,'hist'=8] {'mom'}, dimensions={0} | all-to-all | bytes 1048576 | tf_op jit(solution)/shard_map/while/body/eval_jaxpr/all_to_all | solution.py:39
  174.0 4.3 %fusion.79 = f32[8,8,1024]{2,1,0:T(8,128)S(1)} fusion(f32[2,8,128,1024]{3,2,1,0:T(8,128)} %get-tuple-element.502, f32[8,4,128]{2,1,0:T(4,128)S(1)} %copy.40, f32[8,4,128]{2,1,0:T(4,128)S(1)} %copy.41), kind=kOutput, calls=%fused_computation.2.clone.1 | convolution fusion | flops 100671488 | bytes 4489216 | tf_op jit(solution)/shard_map/while/body/eval_jaxpr/kxs,kst->kxt/dot_general | solution.py:88
  178.3 2.1 fusion.78
  180.9 0.7 pad_maximum_fusion.19
  181.6 5.5 %all-to-all-start.1 = ((f32[8,72,128]{2,1,0:T(8,128)}), f32[8,72,128]{2,1,0:T(8,128)S(1)}, u32[]{:S(2)}, u32[]{:S(2)}) async-start(f32[8,72,128]{2,1,0:T(8,128)} %pad_maximum_fusion.19), calls=%async_computation.1 | async-start | bytes 589824 | tf_op jit(solution)/shard_map/while/body/eval_jaxpr/all_to_all | solution.py:55
  187.1 6.8 %all-to-all-done.1 = f32[8,72,128]{2,1,0:T(8,128)S(1)} async-done(((f32[8,72,128]{2,1,0:T(8,128)}), f32[8,72,128]{2,1,0:T(8,128)S(1)}, u32[]{:S(2)}, u32[]{:S(2)}) %all-to-all-start.1) | async-done | bytes 294944 | tf_op jit(solution)/shard_map/while/body/eval_jaxpr/all_to_all | solution.py:55
  195.5 13.0 %all_to_all.43 = f32[16,64,128]{2,1,0:T(8,128)S(1)} all-to-all(f32[16,64,128]{2,1,0:T(8,128)S(1)} %broadcast_in_dim.58), channel_id=1, replica_groups=mesh['mom'=16,'hist'=8] {'mom'}, dimensions={0} | all-to-all | bytes 1048576 | tf_op jit(solution)/shard_map/while/body/eval_jaxpr/all_to_all | solution.py:39
  208.6 0.6 convolution_bitcast_fusion.4
  209.7 4.3 %fusion.79 = f32[8,8,1024]{2,1,0:T(8,128)S(1)} fusion(f32[2,8,128,1024]{3,2,1,0:T(8,128)} %get-tuple-element.502, f32[8,4,128]{2,1,0:T(4,128)S(1)} %copy.40, f32[8,4,128]{2,1,0:T(4,128)S(1)} %copy.41), kind=kOutput, calls=%fused_computation.2.clone.1 | convolution fusion | flops 100671488 | bytes 4489216 | tf_op jit(solution)/shard_map/while/body/eval_jaxpr/kxs,kst->kxt/dot_general | solution.py:88
  214.0 2.1 fusion.78
  216.6 0.7 pad_maximum_fusion.19
  217.4 5.5 %all-to-all-start.1 = ((f32[8,72,128]{2,1,0:T(8,128)}), f32[8,72,128]{2,1,0:T(8,128)S(1)}, u32[]{:S(2)}, u32[]{:S(2)}) async-start(f32[8,72,128]{2,1,0:T(8,128)} %pad_maximum_fusion.19), calls=%async_computation.1 | async-start | bytes 589824 | tf_op jit(solution)/shard_map/while/body/eval_jaxpr/all_to_all | solution.py:55
  222.8 6.8 %all-to-all-done.1 = f32[8,72,128]{2,1,0:T(8,128)S(1)} async-done(((f32[8,72,128]{2,1,0:T(8,128)}), f32[8,72,128]{2,1,0:T(8,128)S(1)}, u32[]{:S(2)}, u32[]{:S(2)}) %all-to-all-start.1) | async-done | bytes 294944 | tf_op jit(solution)/shard_map/while/body/eval_jaxpr/all_to_all | solution.py:55
  231.2 0.6 multiply_reduce_fusion.1
  231.8 0.7 broadcast_in_dim.55
  232.5 13.8 %all_to_all.42 = f32[128,1,1]{2,1,0:T(1,128)S(1)} all-to-all(f32[128,1,1]{2,1,0:T(1,128)S(1)} %broadcast_in_dim.55), channel_id=1, replica_groups=mesh['mom'=16,'hist'=8] {'mom','hist'}, dimensions={0} | all-to-all | bytes 1024 | tf_op jit(solution)/shard_map/all_to_all | solution.py:121
  246.2 0.7 reduce_sum.83
  247.6 0.6 divide_add_fusion.1
  (163 shorter events, 14.5 us)
Async XLA Ops:
  2.5 24.6 %all-to-all-start.2 = ((f32[16,128,128]{2,1,0:T(8,128)}), f32[16,128,128]{2,1,0:T(8,128)S(1)}, u32[]{:S(2)}, u32[]{:S(2)}) async-start(f32[16,128,128]{2,1,0:T(8,128)} %broadcast_in_dim.53), calls=%async_computation.2 | async-start | bytes 2097152 | tf_op jit(solution)/shard_map/all_to_all | solution.py:39
  29.5 16.3 %copy-start.1 = (f32[2,8,4,128]{3,2,1,0:T(4,128)S(1)}, f32[2,8,4,128]{3,2,1,0:T(4,128)}, u32[]{:S(2)}) copy-start(f32[2,8,4,128]{3,2,1,0:T(4,128)} %param.8) | copy-start | bytes 98308
  38.9 13.6 %all-to-all-start.3 = ((f32[8,72,128]{2,1,0:T(8,128)}), f32[8,72,128]{2,1,0:T(8,128)S(1)}, u32[]{:S(2)}, u32[]{:S(2)}) async-start(f32[8,72,128]{2,1,0:T(8,128)} %pad_maximum_fusion.4), calls=%async_computation.3 | async-start | bytes 589824 | tf_op jit(solution)/shard_map/all_to_all | solution.py:55
  66.0 5.4 %copy-start = (f32[2,8,128,1024]{3,2,1,0:T(8,128)S(1)}, f32[2,8,128,1024]{3,2,1,0:T(8,128)}, u32[]{:S(2)}) copy-start(f32[2,8,128,1024]{3,2,1,0:T(8,128)} %get-tuple-element.502) | copy-start | bytes 25165828 | tf_op jit(solution)/shard_map/while
  74.8 12.0 %all-to-all-start.1 = ((f32[8,72,128]{2,1,0:T(8,128)}), f32[8,72,128]{2,1,0:T(8,128)S(1)}, u32[]{:S(2)}, u32[]{:S(2)}) async-start(f32[8,72,128]{2,1,0:T(8,128)} %pad_maximum_fusion.19), calls=%async_computation.1 | async-start | bytes 589824 | tf_op jit(solution)/shard_map/while/body/eval_jaxpr/all_to_all | solution.py:55
  101.4 5.4 %copy-start = (f32[2,8,128,1024]{3,2,1,0:T(8,128)S(1)}, f32[2,8,128,1024]{3,2,1,0:T(8,128)}, u32[]{:S(2)}) copy-start(f32[2,8,128,1024]{3,2,1,0:T(8,128)} %get-tuple-element.502) | copy-start | bytes 25165828 | tf_op jit(solution)/shard_map/while
  110.2 12.3 %all-to-all-start.1 = ((f32[8,72,128]{2,1,0:T(8,128)}), f32[8,72,128]{2,1,0:T(8,128)S(1)}, u32[]{:S(2)}, u32[]{:S(2)}) async-start(f32[8,72,128]{2,1,0:T(8,128)} %pad_maximum_fusion.19), calls=%async_computation.1 | async-start | bytes 589824 | tf_op jit(solution)/shard_map/while/body/eval_jaxpr/all_to_all | solution.py:55
  137.1 5.4 %copy-start = (f32[2,8,128,1024]{3,2,1,0:T(8,128)S(1)}, f32[2,8,128,1024]{3,2,1,0:T(8,128)}, u32[]{:S(2)}) copy-start(f32[2,8,128,1024]{3,2,1,0:T(8,128)} %get-tuple-element.502) | copy-start | bytes 25165828 | tf_op jit(solution)/shard_map/while
  145.9 12.3 %all-to-all-start.1 = ((f32[8,72,128]{2,1,0:T(8,128)}), f32[8,72,128]{2,1,0:T(8,128)S(1)}, u32[]{:S(2)}, u32[]{:S(2)}) async-start(f32[8,72,128]{2,1,0:T(8,128)} %pad_maximum_fusion.19), calls=%async_computation.1 | async-start | bytes 589824 | tf_op jit(solution)/shard_map/while/body/eval_jaxpr/all_to_all | solution.py:55
  172.9 5.4 %copy-start = (f32[2,8,128,1024]{3,2,1,0:T(8,128)S(1)}, f32[2,8,128,1024]{3,2,1,0:T(8,128)}, u32[]{:S(2)}) copy-start(f32[2,8,128,1024]{3,2,1,0:T(8,128)} %get-tuple-element.502) | copy-start | bytes 25165828 | tf_op jit(solution)/shard_map/while
  181.6 12.3 %all-to-all-start.1 = ((f32[8,72,128]{2,1,0:T(8,128)}), f32[8,72,128]{2,1,0:T(8,128)S(1)}, u32[]{:S(2)}, u32[]{:S(2)}) async-start(f32[8,72,128]{2,1,0:T(8,128)} %pad_maximum_fusion.19), calls=%async_computation.1 | async-start | bytes 589824 | tf_op jit(solution)/shard_map/while/body/eval_jaxpr/all_to_all | solution.py:55
  208.6 5.4 %copy-start = (f32[2,8,128,1024]{3,2,1,0:T(8,128)S(1)}, f32[2,8,128,1024]{3,2,1,0:T(8,128)}, u32[]{:S(2)}) copy-start(f32[2,8,128,1024]{3,2,1,0:T(8,128)} %get-tuple-element.502) | copy-start | bytes 25165828 | tf_op jit(solution)/shard_map/while
  217.4 12.3 %all-to-all-start.1 = ((f32[8,72,128]{2,1,0:T(8,128)}), f32[8,72,128]{2,1,0:T(8,128)S(1)}, u32[]{:S(2)}, u32[]{:S(2)}) async-start(f32[8,72,128]{2,1,0:T(8,128)} %pad_maximum_fusion.19), calls=%async_computation.1 | async-start | bytes 589824 | tf_op jit(solution)/shard_map/while/body/eval_jaxpr/all_to_all | solution.py:55
  248.3 0.5 copy-start.2

commit v8 on v7

--- a/solution.py
+++ b/solution.py
@@ -46,10 +46,8 @@
 
 
 def hist_reduce(partial, extra, hist_n):
-    two, kl, rr, h = partial.shape
-    cols = h // hist_n
-    x = partial.reshape(two, kl, rr, hist_n, cols)
-    x = jnp.transpose(x, (3, 0, 1, 2, 4)).reshape(hist_n, two * kl * rr * cols // 128, 128)
+    _, two, kl, rr, cols = partial.shape
+    x = partial.reshape(hist_n, two * kl * rr * cols // 128, 128)
     tile = jnp.pad(extra[None, :], ((0, 7), (0, 128 - extra.shape[0])))
     x = jnp.concatenate([x, jnp.broadcast_to(tile, (hist_n, 8, 128))], axis=1)
     y = lax.all_to_all(x, "hist", 0, 0, tiled=True)
@@ -85,11 +83,12 @@
 
     def contract(sigma):
         x = jnp.concatenate([sigma[0], sigma[1]], axis=1)
-        a = jnp.einsum("kxs,kst->kxt", x, hist_panel[0], precision=HIGHEST)
-        b = jnp.einsum("kxs,kst->kxt", x, hist_panel[1], precision=HIGHEST)
-        real = a[:, :R] - b[:, R:]
-        imag = b[:, :R] + a[:, R:]
-        return jnp.stack([real, imag])
+        panel = hist_panel.reshape(hist_panel.shape[:3] + (hist_n, cols))
+        a = jnp.einsum("kxs,kshu->hkxu", x, panel[0], precision=HIGHEST)
+        b = jnp.einsum("kxs,kshu->hkxu", x, panel[1], precision=HIGHEST)
+        real = a[:, :, :R] - b[:, :, R:]
+        imag = b[:, :, :R] + a[:, :, R:]
+        return jnp.stack([real, imag], axis=1)
 
     first = jnp.concatenate([screened.reshape(-1, 128), free_rows.reshape(-1, 128)])
     rows = gather_rows(first)

time: 250 us -> 275 us (1.10)
  local copies, waits for them, and re-layouts: 5.49 us -> 72.4 us
  blocking collectives: 78.9 us -> 13.9 us
  starting transfers between devices: 42.7 us -> 59.4 us
  waiting for transfers between devices: 56.1 us -> 63.8 us
  other arithmetic: 13.5 us -> 8.77 us
  matrix products: 46.4 us -> 49.7 us
    all_to_all x5 -> x0, blocking collectives: 65.2 us -> none  [gather_rows(): lax.all_to_all(jnp.broadcast_to(block, (n_mom,) + block.shape), 'mom', 0,...]
    slice x0 -> x6, local copies, waits for them, and re-layouts: none -> 45.1 us  [contract(): b = jnp.einsum('kxs,kshu->hkxu', x, panel[1], precision=HIGHEST)]
    all_to_all x1 -> x6, starting transfers between devices: 8.59 us -> 26.4 us  [gather_rows(): lax.all_to_all(jnp.broadcast_to(block, (n_mom,) + block.shape), 'mom', 0,...]
    unnamed x5 -> x12, local copies, waits for them, and re-layouts: 0.52 us -> 9.24 us
    all_to_all x1 -> x6, waiting for transfers between devices: 15.6 us -> 23.3 us  [gather_rows(): lax.all_to_all(jnp.broadcast_to(block, (n_mom,) + block.shape), 'mom', 0,...]
    while x10 -> x20, local copies, waits for them, and re-layouts: 0.03 us -> 5.22 us
    concatenate x0 -> x6, local copies, waits for them, and re-layouts: none -> 4.72 us  [hist_reduce(): x = jnp.concatenate([x, jnp.broadcast_to(tile, (hist_n, 8, 128))], axis=1)]
    concatenate x6, other arithmetic: 4.39 us -> 0.12 us  [hist_reduce(): x = jnp.concatenate([x, jnp.broadcast_to(tile, (hist_n, 8, 128))], axis=1)]
  transfers between devices with their start and end apart: 7 -> 12, of which waited for: 7 -> 12; matrix products, arithmetic and copies ran while one was open for 0% -> 17% of each run, Pallas kernels for 0% -> 0%
where the time goes in v8:
time: 275 us; the launch traced here: 274 us
  local copies, waits for them, and re-layouts  72.4 us (26%)
  waiting for transfers between devices  63.8 us (23%)
  starting transfers between devices  59.4 us (22%)
  matrix products  49.7 us (18%)
  blocking collectives  13.9 us (5%)
  other arithmetic  8.77 us (3%)
  loops' own time  4.18 us (2%)
    slice x6, local copies, waits for them, and re-layouts, contract(): b = jnp.einsum('kxs,kshu->hkxu', x, panel[1], precision=HIGHEST)  45.1 us
    all_to_all x6, waiting for transfers between devices, hist_reduce(): y = lax.all_to_all(x, 'hist', 0, 0, tiled=True)  40.5 us
    all_to_all x6, starting transfers between devices, hist_reduce(): y = lax.all_to_all(x, 'hist', 0, 0, tiled=True)  33 us
    all_to_all x6, starting transfers between devices, gather_rows(): lax.all_to_all(jnp.broadcast_to(block, (n_mom,) + block.shape), 'mom', 0,...  26.4 us
    all_to_all x6, waiting for transfers between devices, gather_rows(): lax.all_to_all(jnp.broadcast_to(block, (n_mom,) + block.shape), 'mom', 0,...  23.3 us
    dot_general x6, matrix products, contract(): a = jnp.einsum('kxs,kshu->hkxu', x, panel[0], precision=HIGHEST)  21.4 us
    dot_general x6, matrix products, contract(): b = jnp.einsum('kxs,kshu->hkxu', x, panel[1], precision=HIGHEST)  21.3 us
    all_to_all x1, blocking collectives, shards(): total = jnp.sum(lax.all_to_all(spread, ('mom', 'hist'), 0, 0, tiled=True))  13.9 us
  transfers between devices with their start and end apart: 12, of which 12 were waited for; matrix products, arithmetic and copies ran while one was open for 17% of the time, Pallas kernels for 0%

profile of v8, /device:TPU:1, one launch (start us, length us, event | category | flops | bytes accessed | tf_op | source)
XLA Modules:
  0.0 273.8 jit_solution(13968703780013575869)
XLA Ops:
  0.7 8.7 %copy.68 = f32[2,8,128,1024]{2,3,1,0:T(8,128)} copy(f32[2,8,128,1024]{3,2,1,0:T(8,128)} %param.7) | data formatting | bytes 16777216 | tf_op args[0]
  9.4 1.1 broadcast_in_dim.53
  10.5 8.6 %all-to-all-start.2 = ((f32[16,128,128]{2,1,0:T(8,128)}), f32[16,128,128]{2,1,0:T(8,128)S(1)}, u32[]{:S(2)}, u32[]{:S(2)}) async-start(f32[16,128,128]{2,1,0:T(8,128)} %broadcast_in_dim.53), calls=%async_computation.2 | async-start | bytes 2097152 | tf_op jit(solution)/shard_map/all_to_all | solution.py:39
  19.5 7.5 %fusion.52 = (f32[1,8,128,1024]{2,3,1,0:T(8,128)}, f32[1,8,128,1024]{2,3,1,0:T(8,128)}) fusion(f32[2,8,128,1024]{2,3,1,0:T(8,128)} %copy.68), kind=kLoop, calls=%fused_computation.111 | loop fusion | bytes 16777216 | tf_op jit(solution)/shard_map/slice | solution.py:88
  27.0 8.1 %all-to-all-done.2 = f32[16,128,128]{2,1,0:T(8,128)S(1)} async-done(((f32[16,128,128]{2,1,0:T(8,128)}), f32[16,128,128]{2,1,0:T(8,128)S(1)}, u32[]{:S(2)}, u32[]{:S(2)}) %all-to-all-start.2) | async-done | bytes 1048608 | tf_op jit(solution)/shard_map/all_to_all | solution.py:39
  38.3 3.6 %convolution_bitcast_fusion.4 = f32[8,8,8,128]{3,2,0,1:T(8,128)S(1)} fusion(f32[8,128,8,128]{1,3,2,0:T(8,128)S(1)} %bitcast.131, f32[8,4,128]{2,1,0:T(4,128)S(1)} %copy.67, f32[8,4,128]{2,1,0:T(4,128)S(1)} %copy.66), kind=kOutput, calls=%fused_computation.38 | convolution fusion | flops 100671488 | bytes 4489216 | tf_op jit(solution)/shard_map/kxs,kshu->hkxu/dot_general | solution.py:88
  41.8 3.6 %convolution_bitcast_fusion.5 = f32[8,8,8,128]{3,2,0,1:T(8,128)S(1)} fusion(f32[8,128,8,128]{1,3,2,0:T(8,128)S(1)} %bitcast.130, f32[8,4,128]{2,1,0:T(4,128)S(1)} %copy.67, f32[8,4,128]{2,1,0:T(4,128)S(1)} %copy.66), kind=kOutput, calls=%fused_computation.39 | convolution fusion | flops 100671488 | bytes 4489216 | tf_op jit(solution)/shard_map/kxs,kshu->hkxu/dot_general | solution.py:87
  46.4 6.9 %all-to-all-start.3 = ((f32[8,72,128]{2,1,0:T(8,128)}), f32[8,72,128]{2,1,0:T(8,128)S(1)}, u32[]{:S(2)}, u32[]{:S(2)}) async-start(f32[8,72,128]{2,1,0:T(8,128)} %copy.73), calls=%async_computation.3 | async-start | bytes 589824 | tf_op jit(solution)/shard_map/all_to_all | solution.py:53
  53.6 6.5 %all-to-all-done.3 = f32[8,72,128]{2,1,0:T(8,128)S(1)} async-done(((f32[8,72,128]{2,1,0:T(8,128)}), f32[8,72,128]{2,1,0:T(8,128)S(1)}, u32[]{:S(2)}, u32[]{:S(2)}) %all-to-all-start.3) | async-done | bytes 294944 | tf_op jit(solution)/shard_map/all_to_all | solution.py:53
  60.1 195.8 %while.20 = (s32[]{:T(128)}, f32[2,8,4,128]{3,2,1,0:T(4,128)S(1)}, f32[2,8,4,128]{3,2,1,0:T(4,128)S(1)}, f32[6]{0:T(128)S(1)}, f32[2,8,4,128]{3,2,1,0:T(4,128)S(...) while((s32[]{:T(128)}, f32[2,8,4,128]{3,2,1,0:T(4,128)S(1)}, ...), condition=%wide.region_5.6_spmd, body=%wide.region_1.5_spmd.sunk | while | flops 416632960 | bytes 73253816 | solution.py:115
  61.0 3.6 %all-to-all-start = ((f32[16,64,128]{2,1,0:T(8,128)}), f32[16,64,128]{2,1,0:T(8,128)S(1)}, u32[]{:S(2)}, u32[]{:S(2)}) async-start(f32[16,64,128]{2,1,0:T(8,128)} %broadcast_in_dim.58), calls=%async_computation | async-start | bytes 1048576 | tf_op jit(solution)/shard_map/while/body/eval_jaxpr/all_to_all | solution.py:39
  64.6 7.5 %fusion.75 = (f32[1,8,128,1024]{2,3,1,0:T(8,128)}, f32[1,8,128,1024]{2,3,1,0:T(8,128)}) fusion(f32[2,8,128,1024]{2,3,1,0:T(8,128)} %get-tuple-element.520), kind=kLoop, calls=%fused_computation.110.clone.1 | loop fusion | bytes 16777216 | tf_op jit(solution)/shard_map/while/body/eval_jaxpr/slice | solution.py:88
  72.1 3.0 %all-to-all-done = f32[16,64,128]{2,1,0:T(8,128)S(1)} async-done(((f32[16,64,128]{2,1,0:T(8,128)}), f32[16,64,128]{2,1,0:T(8,128)S(1)}, u32[]{:S(2)}, u32[]{:S(2)}) %all-to-all-start) | async-done | bytes 524320 | tf_op jit(solution)/shard_map/while/body/eval_jaxpr/all_to_all | solution.py:39
  77.4 3.5 %convolution_bitcast_fusion.12 = f32[8,8,8,128]{3,2,0,1:T(8,128)S(1)} fusion(f32[8,128,8,128]{1,3,2,0:T(8,128)S(1)} %bitcast.127, f32[8,4,128]{2,1,0:T(4,128)S(1)} %copy.89, f32[8,4,128]{2,1,0:T(4,128)S(1)} %copy.90), kind=kOutput, calls=%fused_computation.1.clone.1 | convolution fusion | flops 100671488 | bytes 4489216 | tf_op jit(solution)/shard_map/while/body/eval_jaxpr/kxs,kshu->hkxu/dot_general | solution.py:88
  81.0 3.6 %convolution_bitcast_fusion.13 = f32[8,8,8,128]{3,2,0,1:T(8,128)S(1)} fusion(f32[8,128,8,128]{1,3,2,0:T(8,128)S(1)} %bitcast.126, f32[8,4,128]{2,1,0:T(4,128)S(1)} %copy.89, f32[8,4,128]{2,1,0:T(4,128)S(1)} %copy.90), kind=kOutput, calls=%fused_computation.2.clone.1 | convolution fusion | flops 100671488 | bytes 4489216 | tf_op jit(solution)/shard_map/while/body/eval_jaxpr/kxs,kshu->hkxu/dot_general | solution.py:87
  85.8 5.2 %all-to-all-start.1 = ((f32[8,72,128]{2,1,0:T(8,128)}), f32[8,72,128]{2,1,0:T(8,128)S(1)}, u32[]{:S(2)}, u32[]{:S(2)}) async-start(f32[8,72,128]{2,1,0:T(8,128)} %copy.92), calls=%async_computation.1 | async-start | bytes 589824 | tf_op jit(solution)/shard_map/while/body/eval_jaxpr/all_to_all | solution.py:53
  91.0 6.8 %all-to-all-done.1 = f32[8,72,128]{2,1,0:T(8,128)S(1)} async-done(((f32[8,72,128]{2,1,0:T(8,128)}), f32[8,72,128]{2,1,0:T(8,128)S(1)}, u32[]{:S(2)}, u32[]{:S(2)}) %all-to-all-start.1) | async-done | bytes 294944 | tf_op jit(solution)/shard_map/while/body/eval_jaxpr/all_to_all | solution.py:53
  100.2 3.6 %all-to-all-start = ((f32[16,64,128]{2,1,0:T(8,128)}), f32[16,64,128]{2,1,0:T(8,128)S(1)}, u32[]{:S(2)}, u32[]{:S(2)}) async-start(f32[16,64,128]{2,1,0:T(8,128)} %broadcast_in_dim.58), calls=%async_computation | async-start | bytes 1048576 | tf_op jit(solution)/shard_map/while/body/eval_jaxpr/all_to_all | solution.py:39
  103.8 7.5 %fusion.75 = (f32[1,8,128,1024]{2,3,1,0:T(8,128)}, f32[1,8,128,1024]{2,3,1,0:T(8,128)}) fusion(f32[2,8,128,1024]{2,3,1,0:T(8,128)} %get-tuple-element.520), kind=kLoop, calls=%fused_computation.110.clone.1 | loop fusion | bytes 16777216 | tf_op jit(solution)/shard_map/while/body/eval_jaxpr/slice | solution.py:88
  111.3 3.0 %all-to-all-done = f32[16,64,128]{2,1,0:T(8,128)S(1)} async-done(((f32[16,64,128]{2,1,0:T(8,128)}), f32[16,64,128]{2,1,0:T(8,128)S(1)}, u32[]{:S(2)}, u32[]{:S(2)}) %all-to-all-start) | async-done | bytes 524320 | tf_op jit(solution)/shard_map/while/body/eval_jaxpr/all_to_all | solution.py:39
  116.6 3.5 %convolution_bitcast_fusion.12 = f32[8,8,8,128]{3,2,0,1:T(8,128)S(1)} fusion(f32[8,128,8,128]{1,3,2,0:T(8,128)S(1)} %bitcast.127, f32[8,4,128]{2,1,0:T(4,128)S(1)} %copy.89, f32[8,4,128]{2,1,0:T(4,128)S(1)} %copy.90), kind=kOutput, calls=%fused_computation.1.clone.1 | convolution fusion | flops 100671488 | bytes 4489216 | tf_op jit(solution)/shard_map/while/body/eval_jaxpr/kxs,kshu->hkxu/dot_general | solution.py:88
  120.2 3.6 %convolution_bitcast_fusion.13 = f32[8,8,8,128]{3,2,0,1:T(8,128)S(1)} fusion(f32[8,128,8,128]{1,3,2,0:T(8,128)S(1)} %bitcast.126, f32[8,4,128]{2,1,0:T(4,128)S(1)} %copy.89, f32[8,4,128]{2,1,0:T(4,128)S(1)} %copy.90), kind=kOutput, calls=%fused_computation.2.clone.1 | convolution fusion | flops 100671488 | bytes 4489216 | tf_op jit(solution)/shard_map/while/body/eval_jaxpr/kxs,kshu->hkxu/dot_general | solution.py:87
  124.9 5.2 %all-to-all-start.1 = ((f32[8,72,128]{2,1,0:T(8,128)}), f32[8,72,128]{2,1,0:T(8,128)S(1)}, u32[]{:S(2)}, u32[]{:S(2)}) async-start(f32[8,72,128]{2,1,0:T(8,128)} %copy.92), calls=%async_computation.1 | async-start | bytes 589824 | tf_op jit(solution)/shard_map/while/body/eval_jaxpr/all_to_all | solution.py:53
  130.2 6.8 %all-to-all-done.1 = f32[8,72,128]{2,1,0:T(8,128)S(1)} async-done(((f32[8,72,128]{2,1,0:T(8,128)}), f32[8,72,128]{2,1,0:T(8,128)S(1)}, u32[]{:S(2)}, u32[]{:S(2)}) %all-to-all-start.1) | async-done | bytes 294944 | tf_op jit(solution)/shard_map/while/body/eval_jaxpr/all_to_all | solution.py:53
  139.4 3.6 %all-to-all-start = ((f32[16,64,128]{2,1,0:T(8,128)}), f32[16,64,128]{2,1,0:T(8,128)S(1)}, u32[]{:S(2)}, u32[]{:S(2)}) async-start(f32[16,64,128]{2,1,0:T(8,128)} %broadcast_in_dim.58), calls=%async_computation | async-start | bytes 1048576 | tf_op jit(solution)/shard_map/while/body/eval_jaxpr/all_to_all | solution.py:39
  142.9 7.5 %fusion.75 = (f32[1,8,128,1024]{2,3,1,0:T(8,128)}, f32[1,8,128,1024]{2,3,1,0:T(8,128)}) fusion(f32[2,8,128,1024]{2,3,1,0:T(8,128)} %get-tuple-element.520), kind=kLoop, calls=%fused_computation.110.clone.1 | loop fusion | bytes 16777216 | tf_op jit(solution)/shard_map/while/body/eval_jaxpr/slice | solution.py:88
  150.5 3.0 %all-to-all-done = f32[16,64,128]{2,1,0:T(8,128)S(1)} async-done(((f32[16,64,128]{2,1,0:T(8,128)}), f32[16,64,128]{2,1,0:T(8,128)S(1)}, u32[]{:S(2)}, u32[]{:S(2)}) %all-to-all-start) | async-done | bytes 524320 | tf_op jit(solution)/shard_map/while/body/eval_jaxpr/all_to_all | solution.py:39
  154.7 1.0 copy-done.1
  155.8 3.5 %convolution_bitcast_fusion.12 = f32[8,8,8,128]{3,2,0,1:T(8,128)S(1)} fusion(f32[8,128,8,128]{1,3,2,0:T(8,128)S(1)} %bitcast.127, f32[8,4,128]{2,1,0:T(4,128)S(1)} %copy.89, f32[8,4,128]{2,1,0:T(4,128)S(1)} %copy.90), kind=kOutput, calls=%fused_computation.1.clone.1 | convolution fusion | flops 100671488 | bytes 4489216 | tf_op jit(solution)/shard_map/while/body/eval_jaxpr/kxs,kshu->hkxu/dot_general | solution.py:88
  159.3 3.6 %convolution_bitcast_fusion.13 = f32[8,8,8,128]{3,2,0,1:T(8,128)S(1)} fusion(f32[8,128,8,128]{1,3,2,0:T(8,128)S(1)} %bitcast.126, f32[8,4,128]{2,1,0:T(4,128)S(1)} %copy.89, f32[8,4,128]{2,1,0:T(4,128)S(1)} %copy.90), kind=kOutput, calls=%fused_computation.2.clone.1 | convolution fusion | flops 100671488 | bytes 4489216 | tf_op jit(solution)/shard_map/while/body/eval_jaxpr/kxs,kshu->hkxu/dot_general | solution.py:87
  164.1 5.2 %all-to-all-start.1 = ((f32[8,72,128]{2,1,0:T(8,128)}), f32[8,72,128]{2,1,0:T(8,128)S(1)}, u32[]{:S(2)}, u32[]{:S(2)}) async-start(f32[8,72,128]{2,1,0:T(8,128)} %copy.92), calls=%async_computation.1 | async-start | bytes 589824 | tf_op jit(solution)/shard_map/while/body/eval_jaxpr/all_to_all | solution.py:53
  169.3 6.8 %all-to-all-done.1 = f32[8,72,128]{2,1,0:T(8,128)S(1)} async-done(((f32[8,72,128]{2,1,0:T(8,128)}), f32[8,72,128]{2,1,0:T(8,128)S(1)}, u32[]{:S(2)}, u32[]{:S(2)}) %all-to-all-start.1) | async-done | bytes 294944 | tf_op jit(solution)/shard_map/while/body/eval_jaxpr/all_to_all | solution.py:53
  178.5 3.6 %all-to-all-start = ((f32[16,64,128]{2,1,0:T(8,128)}), f32[16,64,128]{2,1,0:T(8,128)S(1)}, u32[]{:S(2)}, u32[]{:S(2)}) async-start(f32[16,64,128]{2,1,0:T(8,128)} %broadcast_in_dim.58), calls=%async_computation | async-start | bytes 1048576 | tf_op jit(solution)/shard_map/while/body/eval_jaxpr/all_to_all | solution.py:39
  182.1 7.5 %fusion.75 = (f32[1,8,128,1024]{2,3,1,0:T(8,128)}, f32[1,8,128,1024]{2,3,1,0:T(8,128)}) fusion(f32[2,8,128,1024]{2,3,1,0:T(8,128)} %get-tuple-element.520), kind=kLoop, calls=%fused_computation.110.clone.1 | loop fusion | bytes 16777216 | tf_op jit(solution)/shard_map/while/body/eval_jaxpr/slice | solution.py:88
  189.6 3.0 %all-to-all-done = f32[16,64,128]{2,1,0:T(8,128)S(1)} async-done(((f32[16,64,128]{2,1,0:T(8,128)}), f32[16,64,128]{2,1,0:T(8,128)S(1)}, u32[]{:S(2)}, u32[]{:S(2)}) %all-to-all-start) | async-done | bytes 524320 | tf_op jit(solution)/shard_map/while/body/eval_jaxpr/all_to_all | solution.py:39
  194.9 3.5 %convolution_bitcast_fusion.12 = f32[8,8,8,128]{3,2,0,1:T(8,128)S(1)} fusion(f32[8,128,8,128]{1,3,2,0:T(8,128)S(1)} %bitcast.127, f32[8,4,128]{2,1,0:T(4,128)S(1)} %copy.89, f32[8,4,128]{2,1,0:T(4,128)S(1)} %copy.90), kind=kOutput, calls=%fused_computation.1.clone.1 | convolution fusion | flops 100671488 | bytes 4489216 | tf_op jit(solution)/shard_map/while/body/eval_jaxpr/kxs,kshu->hkxu/dot_general | solution.py:88
  198.5 3.6 %convolution_bitcast_fusion.13 = f32[8,8,8,128]{3,2,0,1:T(8,128)S(1)} fusion(f32[8,128,8,128]{1,3,2,0:T(8,128)S(1)} %bitcast.126, f32[8,4,128]{2,1,0:T(4,128)S(1)} %copy.89, f32[8,4,128]{2,1,0:T(4,128)S(1)} %copy.90), kind=kOutput, calls=%fused_computation.2.clone.1 | convolution fusion | flops 100671488 | bytes 4489216 | tf_op jit(solution)/shard_map/while/body/eval_jaxpr/kxs,kshu->hkxu/dot_general | solution.py:87
  203.3 5.2 %all-to-all-start.1 = ((f32[8,72,128]{2,1,0:T(8,128)}), f32[8,72,128]{2,1,0:T(8,128)S(1)}, u32[]{:S(2)}, u32[]{:S(2)}) async-start(f32[8,72,128]{2,1,0:T(8,128)} %copy.92), calls=%async_computation.1 | async-start | bytes 589824 | tf_op jit(solution)/shard_map/while/body/eval_jaxpr/all_to_all | solution.py:53
  208.5 6.8 %all-to-all-done.1 = f32[8,72,128]{2,1,0:T(8,128)S(1)} async-done(((f32[8,72,128]{2,1,0:T(8,128)}), f32[8,72,128]{2,1,0:T(8,128)S(1)}, u32[]{:S(2)}, u32[]{:S(2)}) %all-to-all-start.1) | async-done | bytes 294944 | tf_op jit(solution)/shard_map/while/body/eval_jaxpr/all_to_all | solution.py:53
  217.7 3.6 %all-to-all-start = ((f32[16,64,128]{2,1,0:T(8,128)}), f32[16,64,128]{2,1,0:T(8,128)S(1)}, u32[]{:S(2)}, u32[]{:S(2)}) async-start(f32[16,64,128]{2,1,0:T(8,128)} %broadcast_in_dim.58), calls=%async_computation | async-start | bytes 1048576 | tf_op jit(solution)/shard_map/while/body/eval_jaxpr/all_to_all | solution.py:39
  221.3 7.5 %fusion.75 = (f32[1,8,128,1024]{2,3,1,0:T(8,128)}, f32[1,8,128,1024]{2,3,1,0:T(8,128)}) fusion(f32[2,8,128,1024]{2,3,1,0:T(8,128)} %get-tuple-element.520), kind=kLoop, calls=%fused_computation.110.clone.1 | loop fusion | bytes 16777216 | tf_op jit(solution)/shard_map/while/body/eval_jaxpr/slice | solution.py:88
  228.8 3.0 %all-to-all-done = f32[16,64,128]{2,1,0:T(8,128)S(1)} async-done(((f32[16,64,128]{2,1,0:T(8,128)}), f32[16,64,128]{2,1,0:T(8,128)S(1)}, u32[]{:S(2)}, u32[]{:S(2)}) %all-to-all-start) | async-done | bytes 524320 | tf_op jit(solution)/shard_map/while/body/eval_jaxpr/all_to_all | solution.py:39
  233.1 1.0 copy-done.1
  234.1 3.5 %convolution_bitcast_fusion.12 = f32[8,8,8,128]{3,2,0,1:T(8,128)S(1)} fusion(f32[8,128,8,128]{1,3,2,0:T(8,128)S(1)} %bitcast.127, f32[8,4,128]{2,1,0:T(4,128)S(1)} %copy.89, f32[8,4,128]{2,1,0:T(4,128)S(1)} %copy.90), kind=kOutput, calls=%fused_computation.1.clone.1 | convolution fusion | flops 100671488 | bytes 4489216 | tf_op jit(solution)/shard_map/while/body/eval_jaxpr/kxs,kshu->hkxu/dot_general | solution.py:88
  237.6 3.6 %convolution_bitcast_fusion.13 = f32[8,8,8,128]{3,2,0,1:T(8,128)S(1)} fusion(f32[8,128,8,128]{1,3,2,0:T(8,128)S(1)} %bitcast.126, f32[8,4,128]{2,1,0:T(4,128)S(1)} %copy.89, f32[8,4,128]{2,1,0:T(4,128)S(1)} %copy.90), kind=kOutput, calls=%fused_computation.2.clone.1 | convolution fusion | flops 100671488 | bytes 4489216 | tf_op jit(solution)/shard_map/while/body/eval_jaxpr/kxs,kshu->hkxu/dot_general | solution.py:87
  242.4 5.2 %all-to-all-start.1 = ((f32[8,72,128]{2,1,0:T(8,128)}), f32[8,72,128]{2,1,0:T(8,128)S(1)}, u32[]{:S(2)}, u32[]{:S(2)}) async-start(f32[8,72,128]{2,1,0:T(8,128)} %copy.92), calls=%async_computation.1 | async-start | bytes 589824 | tf_op jit(solution)/shard_map/while/body/eval_jaxpr/all_to_all | solution.py:53
  247.7 6.8 %all-to-all-done.1 = f32[8,72,128]{2,1,0:T(8,128)S(1)} async-done(((f32[8,72,128]{2,1,0:T(8,128)}), f32[8,72,128]{2,1,0:T(8,128)S(1)}, u32[]{:S(2)}, u32[]{:S(2)}) %all-to-all-start.1) | async-done | bytes 294944 | tf_op jit(solution)/shard_map/while/body/eval_jaxpr/all_to_all | solution.py:53
  257.3 13.9 %all_to_all.42 = f32[128,1,1]{2,1,0:T(1,128)S(1)} all-to-all(f32[128,1,1]{2,1,0:T(1,128)S(1)} %broadcast_in_dim.55), channel_id=1, replica_groups=mesh['mom'=16,'hist'=8] {'mom','hist'}, dimensions={0} | all-to-all | bytes 1024 | tf_op jit(solution)/shard_map/all_to_all | solution.py:120
  (185 shorter events, 31.2 us)
Async XLA Ops:
  0.7 8.7 %copy-start.4 = (f32[2,8,4,128]{3,2,1,0:T(4,128)S(1)}, f32[2,8,4,128]{3,2,1,0:T(4,128)}, u32[]{:S(2)}) copy-start(f32[2,8,4,128]{3,2,1,0:T(4,128)} %param.8) | copy-start | bytes 98308
  0.7 8.7 %copy-start.5 = (f32[2,8,4,128]{3,2,1,0:T(4,128)S(1)}, f32[2,8,4,128]{3,2,1,0:T(4,128)}, u32[]{:S(2)}) copy-start(f32[2,8,4,128]{3,2,1,0:T(4,128)} %param.9) | copy-start | bytes 98308
  10.5 24.6 %all-to-all-start.2 = ((f32[16,128,128]{2,1,0:T(8,128)}), f32[16,128,128]{2,1,0:T(8,128)S(1)}, u32[]{:S(2)}, u32[]{:S(2)}) async-start(f32[16,128,128]{2,1,0:T(8,128)} %broadcast_in_dim.53), calls=%async_computation.2 | async-start | bytes 2097152 | tf_op jit(solution)/shard_map/all_to_all | solution.py:39
  35.5 2.8 %copy-start.3 = (f32[1,8,128,1024]{2,3,1,0:T(8,128)S(1)}, f32[1,8,128,1024]{2,3,1,0:T(8,128)}, u32[]{:S(2)}) copy-start(f32[1,8,128,1024]{2,3,1,0:T(8,128)} %get-tuple-element.386) | copy-start | bytes 12582916
  37.7 4.1 %copy-start.2 = (f32[1,8,128,1024]{2,3,1,0:T(8,128)S(1)}, f32[1,8,128,1024]{2,3,1,0:T(8,128)}, u32[]{:S(2)}) copy-start(f32[1,8,128,1024]{2,3,1,0:T(8,128)} %get-tuple-element.387) | copy-start | bytes 12582916
  46.4 13.7 %all-to-all-start.3 = ((f32[8,72,128]{2,1,0:T(8,128)}), f32[8,72,128]{2,1,0:T(8,128)S(1)}, u32[]{:S(2)}, u32[]{:S(2)}) async-start(f32[8,72,128]{2,1,0:T(8,128)} %copy.73), calls=%async_computation.3 | async-start | bytes 589824 | tf_op jit(solution)/shard_map/all_to_all | solution.py:53
  61.0 14.1 %all-to-all-start = ((f32[16,64,128]{2,1,0:T(8,128)}), f32[16,64,128]{2,1,0:T(8,128)S(1)}, u32[]{:S(2)}, u32[]{:S(2)}) async-start(f32[16,64,128]{2,1,0:T(8,128)} %broadcast_in_dim.58), calls=%async_computation | async-start | bytes 1048576 | tf_op jit(solution)/shard_map/while/body/eval_jaxpr/all_to_all | solution.py:39
  75.3 2.2 copy-start.1
  75.3 5.7 %copy-start = (f32[1,8,128,1024]{2,3,1,0:T(8,128)S(1)}, f32[1,8,128,1024]{2,3,1,0:T(8,128)}, u32[]{:S(2)}) copy-start(f32[1,8,128,1024]{2,3,1,0:T(8,128)} %get-tuple-element.480) | copy-start | bytes 12582916 | tf_op jit(solution)/shard_map/while
  85.8 12.0 %all-to-all-start.1 = ((f32[8,72,128]{2,1,0:T(8,128)}), f32[8,72,128]{2,1,0:T(8,128)S(1)}, u32[]{:S(2)}, u32[]{:S(2)}) async-start(f32[8,72,128]{2,1,0:T(8,128)} %copy.92), calls=%async_computation.1 | async-start | bytes 589824 | tf_op jit(solution)/shard_map/while/body/eval_jaxpr/all_to_all | solution.py:53
  100.2 14.1 %all-to-all-start = ((f32[16,64,128]{2,1,0:T(8,128)}), f32[16,64,128]{2,1,0:T(8,128)S(1)}, u32[]{:S(2)}, u32[]{:S(2)}) async-start(f32[16,64,128]{2,1,0:T(8,128)} %broadcast_in_dim.58), calls=%async_computation | async-start | bytes 1048576 | tf_op jit(solution)/shard_map/while/body/eval_jaxpr/all_to_all | solution.py:39
  114.4 2.2 copy-start.1
  114.5 5.7 %copy-start = (f32[1,8,128,1024]{2,3,1,0:T(8,128)S(1)}, f32[1,8,128,1024]{2,3,1,0:T(8,128)}, u32[]{:S(2)}) copy-start(f32[1,8,128,1024]{2,3,1,0:T(8,128)} %get-tuple-element.480) | copy-start | bytes 12582916 | tf_op jit(solution)/shard_map/while
  124.9 12.0 %all-to-all-start.1 = ((f32[8,72,128]{2,1,0:T(8,128)}), f32[8,72,128]{2,1,0:T(8,128)S(1)}, u32[]{:S(2)}, u32[]{:S(2)}) async-start(f32[8,72,128]{2,1,0:T(8,128)} %copy.92), calls=%async_computation.1 | async-start | bytes 589824 | tf_op jit(solution)/shard_map/while/body/eval_jaxpr/all_to_all | solution.py:53
  139.4 14.1 %all-to-all-start = ((f32[16,64,128]{2,1,0:T(8,128)}), f32[16,64,128]{2,1,0:T(8,128)S(1)}, u32[]{:S(2)}, u32[]{:S(2)}) async-start(f32[16,64,128]{2,1,0:T(8,128)} %broadcast_in_dim.58), calls=%async_computation | async-start | bytes 1048576 | tf_op jit(solution)/shard_map/while/body/eval_jaxpr/all_to_all | solution.py:39
  153.6 2.2 copy-start.1
  153.6 5.7 %copy-start = (f32[1,8,128,1024]{2,3,1,0:T(8,128)S(1)}, f32[1,8,128,1024]{2,3,1,0:T(8,128)}, u32[]{:S(2)}) copy-start(f32[1,8,128,1024]{2,3,1,0:T(8,128)} %get-tuple-element.480) | copy-start | bytes 12582916 | tf_op jit(solution)/shard_map/while
  164.1 12.0 %all-to-all-start.1 = ((f32[8,72,128]{2,1,0:T(8,128)}), f32[8,72,128]{2,1,0:T(8,128)S(1)}, u32[]{:S(2)}, u32[]{:S(2)}) async-start(f32[8,72,128]{2,1,0:T(8,128)} %copy.92), calls=%async_computation.1 | async-start | bytes 589824 | tf_op jit(solution)/shard_map/while/body/eval_jaxpr/all_to_all | solution.py:53
  178.5 14.1 %all-to-all-start = ((f32[16,64,128]{2,1,0:T(8,128)}), f32[16,64,128]{2,1,0:T(8,128)S(1)}, u32[]{:S(2)}, u32[]{:S(2)}) async-start(f32[16,64,128]{2,1,0:T(8,128)} %broadcast_in_dim.58), calls=%async_computation | async-start | bytes 1048576 | tf_op jit(solution)/shard_map/while/body/eval_jaxpr/all_to_all | solution.py:39
  192.7 2.2 copy-start.1
  192.8 5.7 %copy-start = (f32[1,8,128,1024]{2,3,1,0:T(8,128)S(1)}, f32[1,8,128,1024]{2,3,1,0:T(8,128)}, u32[]{:S(2)}) copy-start(f32[1,8,128,1024]{2,3,1,0:T(8,128)} %get-tuple-element.480) | copy-start | bytes 12582916 | tf_op jit(solution)/shard_map/while
  203.3 12.0 %all-to-all-start.1 = ((f32[8,72,128]{2,1,0:T(8,128)}), f32[8,72,128]{2,1,0:T(8,128)S(1)}, u32[]{:S(2)}, u32[]{:S(2)}) async-start(f32[8,72,128]{2,1,0:T(8,128)} %copy.92), calls=%async_computation.1 | async-start | bytes 589824 | tf_op jit(solution)/shard_map/while/body/eval_jaxpr/all_to_all | solution.py:53
  217.7 14.1 %all-to-all-start = ((f32[16,64,128]{2,1,0:T(8,128)}), f32[16,64,128]{2,1,0:T(8,128)S(1)}, u32[]{:S(2)}, u32[]{:S(2)}) async-start(f32[16,64,128]{2,1,0:T(8,128)} %broadcast_in_dim.58), calls=%async_computation | async-start | bytes 1048576 | tf_op jit(solution)/shard_map/while/body/eval_jaxpr/all_to_all | solution.py:39
  231.9 2.2 copy-start.1
  232.0 5.7 %copy-start = (f32[1,8,128,1024]{2,3,1,0:T(8,128)S(1)}, f32[1,8,128,1024]{2,3,1,0:T(8,128)}, u32[]{:S(2)}) copy-start(f32[1,8,128,1024]{2,3,1,0:T(8,128)} %get-tuple-element.480) | copy-start | bytes 12582916 | tf_op jit(solution)/shard_map/while
  242.4 12.0 %all-to-all-start.1 = ((f32[8,72,128]{2,1,0:T(8,128)}), f32[8,72,128]{2,1,0:T(8,128)S(1)}, u32[]{:S(2)}, u32[]{:S(2)}) async-start(f32[8,72,128]{2,1,0:T(8,128)} %copy.92), calls=%async_computation.1 | async-start | bytes 589824 | tf_op jit(solution)/shard_map/while/body/eval_jaxpr/all_to_all | solution.py:53
  273.3 0.5 copy-start.6

commit v9 on v7

--- a/solution.py
+++ b/solution.py
@@ -83,10 +83,10 @@
         back_imag = cb[:, n:] + sb[:, :n]
         return jnp.stack([-back_imag, back_real]).reshape(2, k_local, R, cols)
 
-    def contract(sigma):
+    def contract(sigma, precision=lax.Precision.HIGH):
         x = jnp.concatenate([sigma[0], sigma[1]], axis=1)
-        a = jnp.einsum("kxs,kst->kxt", x, hist_panel[0], precision=HIGHEST)
-        b = jnp.einsum("kxs,kst->kxt", x, hist_panel[1], precision=HIGHEST)
+        a = jnp.einsum("kxs,kst->kxt", x, hist_panel[0], precision=precision)
+        b = jnp.einsum("kxs,kst->kxt", x, hist_panel[1], precision=precision)
         real = a[:, :R] - b[:, R:]
         imag = b[:, :R] + a[:, R:]
         return jnp.stack([real, imag])
@@ -98,7 +98,7 @@
     green_full = to_full_k(rows[:, half:], 2, k_local, cols)
     screen_hat = dft(cosine, sine, screen_full[0], screen_full[1])
 
-    integral, _ = hist_reduce(contract(sigma_of(green_full, HIGHEST)), jnp.zeros((lax.axis_size("mom"),), jnp.float32), hist_n)
+    integral, _ = hist_reduce(contract(sigma_of(green_full, HIGHEST), HIGHEST), jnp.zeros((lax.axis_size("mom"),), jnp.float32), hist_n)
     def correction(turn, carry):
         green, integral, deltas = carry
         change = free_rows + step_size * integral - green

time: 250 us -> 244 us (0.976)
  matrix products: 46.4 us -> 40.3 us
    dot_general x12, matrix products: 39.4 us -> 33.2 us  [the longest x6 22.8 us: contract(): a = jnp.einsum('kxs,kst->kxt', x, hist_panel[0], precision=precision)]
where the time goes in v9:
time: 244 us; the launch traced here: 243 us
  blocking collectives  78.9 us (32%)
  waiting for transfers between devices  56.1 us (23%)
  starting transfers between devices  42.6 us (17%)
  matrix products  40.3 us (17%)
  other arithmetic  13.5 us (6%)
  local copies, waits for them, and re-layouts  5.49 us (2%)
  loops' own time  4.19 us (2%)
    all_to_all x5, blocking collectives, gather_rows(): lax.all_to_all(jnp.broadcast_to(block, (n_mom,) + block.shape), 'mom', 0,...  65.1 us
    all_to_all x6, waiting for transfers between devices, hist_reduce(): y = lax.all_to_all(x, 'hist', 0, 0, tiled=True)  40.5 us
    all_to_all x6, starting transfers between devices, hist_reduce(): y = lax.all_to_all(x, 'hist', 0, 0, tiled=True)  34 us
    dot_general x6, matrix products, contract(): a = jnp.einsum('kxs,kst->kxt', x, hist_panel[0], precision=precision)  22.8 us
    all_to_all x1, waiting for transfers between devices, gather_rows(): lax.all_to_all(jnp.broadcast_to(block, (n_mom,) + block.shape), 'mom', 0,...  15.6 us
    all_to_all x1, blocking collectives, shards(): total = jnp.sum(lax.all_to_all(spread, ('mom', 'hist'), 0, 0, tiled=True))  13.7 us
    dot_general x6, matrix products, contract(): b = jnp.einsum('kxs,kst->kxt', x, hist_panel[1], precision=precision)  10.4 us
    all_to_all x1, starting transfers between devices, gather_rows(): lax.all_to_all(jnp.broadcast_to(block, (n_mom,) + block.shape), 'mom', 0,...  8.59 us
  transfers between devices with their start and end apart: 7, of which 7 were waited for; matrix products, arithmetic and copies ran while one was open for 0% of the time, Pallas kernels for 0%

profile of v9, /device:TPU:1, one launch (start us, length us, event | category | flops | bytes accessed | tf_op | source)
XLA Modules:
  0.0 242.6 jit_solution(11252676485314210751)
XLA Ops:
  0.6 0.8 pad_maximum_fusion.6
  1.4 1.1 broadcast_in_dim.53
  2.5 8.6 %all-to-all-start.2 = ((f32[16,128,128]{2,1,0:T(8,128)}), f32[16,128,128]{2,1,0:T(8,128)S(1)}, u32[]{:S(2)}, u32[]{:S(2)}) async-start(f32[16,128,128]{2,1,0:T(8,128)} %broadcast_in_dim.53), calls=%async_computation.2 | async-start | bytes 2097152 | tf_op jit(solution)/shard_map/all_to_all | solution.py:39
  11.5 15.6 %all-to-all-done.2 = f32[16,128,128]{2,1,0:T(8,128)S(1)} async-done(((f32[16,128,128]{2,1,0:T(8,128)}), f32[16,128,128]{2,1,0:T(8,128)S(1)}, u32[]{:S(2)}, u32[]{:S(2)}) %all-to-all-start.2) | async-done | bytes 1048608 | tf_op jit(solution)/shard_map/all_to_all | solution.py:39
  27.5 1.0 fusion.25
  28.5 1.0 fusion.29
  30.3 3.8 %fusion.21 = f32[8,8,1024]{2,1,0:T(8,128)S(1)} fusion(f32[2,8,128,1024]{3,2,1,0:T(8,128)} %param.7, f32[8,4,128]{2,1,0:T(4,128)S(1)} %copy.31, f32[8,4,128]{2,1,0:T(4,128)S(1)} %copy.30), kind=kOutput, calls=%fused_computation.42 | convolution fusion | flops 100671488 | bytes 4489216 | tf_op jit(solution)/shard_map/kxs,kst->kxt/dot_general | solution.py:88
  34.1 3.8 %fusion.19 = f32[8,8,1024]{2,1,0:T(8,128)S(1)} fusion(f32[2,8,128,1024]{3,2,1,0:T(8,128)} %param.7, f32[8,4,128]{2,1,0:T(4,128)S(1)} %copy.31, f32[8,4,128]{2,1,0:T(4,128)S(1)} %copy.30), kind=kOutput, calls=%fused_computation.40 | convolution fusion | flops 100671488 | bytes 4489216 | tf_op jit(solution)/shard_map/kxs,kst->kxt/dot_general | solution.py:89
  38.2 0.7 pad_maximum_fusion.4
  38.9 6.9 %all-to-all-start.3 = ((f32[8,72,128]{2,1,0:T(8,128)}), f32[8,72,128]{2,1,0:T(8,128)S(1)}, u32[]{:S(2)}, u32[]{:S(2)}) async-start(f32[8,72,128]{2,1,0:T(8,128)} %pad_maximum_fusion.4), calls=%async_computation.3 | async-start | bytes 589824 | tf_op jit(solution)/shard_map/all_to_all | solution.py:55
  46.1 6.5 %all-to-all-done.3 = f32[8,72,128]{2,1,0:T(8,128)S(1)} async-done(((f32[8,72,128]{2,1,0:T(8,128)}), f32[8,72,128]{2,1,0:T(8,128)S(1)}, u32[]{:S(2)}, u32[]{:S(2)}) %all-to-all-start.3) | async-done | bytes 294944 | tf_op jit(solution)/shard_map/all_to_all | solution.py:55
  52.6 172.4 %while.20 = (s32[]{:T(128)}, f32[2,8,4,128]{3,2,1,0:T(4,128)S(1)}, f32[2,8,4,128]{3,2,1,0:T(4,128)S(1)}, f32[6]{0:T(128)S(1)}, f32[2,8,4,128]{3,2,1,0:T(4,128)S(...) while((s32[]{:T(128)}, f32[2,8,4,128]{3,2,1,0:T(4,128)S(1)}, ...), condition=%wide.region_5.6_spmd, body=%wide.region_1.5_spmd.sunk | while | flops 315969664 | bytes 55886724 | solution.py:116
  52.7 13.2 %all_to_all.43 = f32[16,64,128]{2,1,0:T(8,128)S(1)} all-to-all(f32[16,64,128]{2,1,0:T(8,128)S(1)} %broadcast_in_dim.58), channel_id=1, replica_groups=mesh['mom'=16,'hist'=8] {'mom'}, dimensions={0} | all-to-all | bytes 1048576 | tf_op jit(solution)/shard_map/while/body/eval_jaxpr/all_to_all | solution.py:39
  67.1 3.8 %fusion.79 = f32[8,8,1024]{2,1,0:T(8,128)S(1)} fusion(f32[2,8,128,1024]{3,2,1,0:T(8,128)} %get-tuple-element.502, f32[8,4,128]{2,1,0:T(4,128)S(1)} %copy.40, f32[8,4,128]{2,1,0:T(4,128)S(1)} %copy.41), kind=kOutput, calls=%fused_computation.2.clone.1 | convolution fusion | flops 50339840 | bytes 4489216 | tf_op jit(solution)/shard_map/while/body/eval_jaxpr/kxs,kst->kxt/dot_general | solution.py:88
  70.9 1.3 fusion.78
  72.8 0.7 pad_maximum_fusion.19
  73.5 5.2 %all-to-all-start.1 = ((f32[8,72,128]{2,1,0:T(8,128)}), f32[8,72,128]{2,1,0:T(8,128)S(1)}, u32[]{:S(2)}, u32[]{:S(2)}) async-start(f32[8,72,128]{2,1,0:T(8,128)} %pad_maximum_fusion.19), calls=%async_computation.1 | async-start | bytes 589824 | tf_op jit(solution)/shard_map/while/body/eval_jaxpr/all_to_all | solution.py:55
  78.7 6.8 %all-to-all-done.1 = f32[8,72,128]{2,1,0:T(8,128)S(1)} async-done(((f32[8,72,128]{2,1,0:T(8,128)}), f32[8,72,128]{2,1,0:T(8,128)S(1)}, u32[]{:S(2)}, u32[]{:S(2)}) %all-to-all-start.1) | async-done | bytes 294944 | tf_op jit(solution)/shard_map/while/body/eval_jaxpr/all_to_all | solution.py:55
  87.1 13.0 %all_to_all.43 = f32[16,64,128]{2,1,0:T(8,128)S(1)} all-to-all(f32[16,64,128]{2,1,0:T(8,128)S(1)} %broadcast_in_dim.58), channel_id=1, replica_groups=mesh['mom'=16,'hist'=8] {'mom'}, dimensions={0} | all-to-all | bytes 1048576 | tf_op jit(solution)/shard_map/while/body/eval_jaxpr/all_to_all | solution.py:39
  100.2 0.6 convolution_bitcast_fusion.4
  101.3 3.8 %fusion.79 = f32[8,8,1024]{2,1,0:T(8,128)S(1)} fusion(f32[2,8,128,1024]{3,2,1,0:T(8,128)} %get-tuple-element.502, f32[8,4,128]{2,1,0:T(4,128)S(1)} %copy.40, f32[8,4,128]{2,1,0:T(4,128)S(1)} %copy.41), kind=kOutput, calls=%fused_computation.2.clone.1 | convolution fusion | flops 50339840 | bytes 4489216 | tf_op jit(solution)/shard_map/while/body/eval_jaxpr/kxs,kst->kxt/dot_general | solution.py:88
  105.1 1.3 fusion.78
  107.0 0.7 pad_maximum_fusion.19
  107.7 5.5 %all-to-all-start.1 = ((f32[8,72,128]{2,1,0:T(8,128)}), f32[8,72,128]{2,1,0:T(8,128)S(1)}, u32[]{:S(2)}, u32[]{:S(2)}) async-start(f32[8,72,128]{2,1,0:T(8,128)} %pad_maximum_fusion.19), calls=%async_computation.1 | async-start | bytes 589824 | tf_op jit(solution)/shard_map/while/body/eval_jaxpr/all_to_all | solution.py:55
  113.2 6.8 %all-to-all-done.1 = f32[8,72,128]{2,1,0:T(8,128)S(1)} async-done(((f32[8,72,128]{2,1,0:T(8,128)}), f32[8,72,128]{2,1,0:T(8,128)S(1)}, u32[]{:S(2)}, u32[]{:S(2)}) %all-to-all-start.1) | async-done | bytes 294944 | tf_op jit(solution)/shard_map/while/body/eval_jaxpr/all_to_all | solution.py:55
  121.6 13.0 %all_to_all.43 = f32[16,64,128]{2,1,0:T(8,128)S(1)} all-to-all(f32[16,64,128]{2,1,0:T(8,128)S(1)} %broadcast_in_dim.58), channel_id=1, replica_groups=mesh['mom'=16,'hist'=8] {'mom'}, dimensions={0} | all-to-all | bytes 1048576 | tf_op jit(solution)/shard_map/while/body/eval_jaxpr/all_to_all | solution.py:39
  135.8 3.8 %fusion.79 = f32[8,8,1024]{2,1,0:T(8,128)S(1)} fusion(f32[2,8,128,1024]{3,2,1,0:T(8,128)} %get-tuple-element.502, f32[8,4,128]{2,1,0:T(4,128)S(1)} %copy.40, f32[8,4,128]{2,1,0:T(4,128)S(1)} %copy.41), kind=kOutput, calls=%fused_computation.2.clone.1 | convolution fusion | flops 50339840 | bytes 4489216 | tf_op jit(solution)/shard_map/while/body/eval_jaxpr/kxs,kst->kxt/dot_general | solution.py:88
  139.6 1.3 fusion.78
  141.5 0.7 pad_maximum_fusion.19
  142.2 5.5 %all-to-all-start.1 = ((f32[8,72,128]{2,1,0:T(8,128)}), f32[8,72,128]{2,1,0:T(8,128)S(1)}, u32[]{:S(2)}, u32[]{:S(2)}) async-start(f32[8,72,128]{2,1,0:T(8,128)} %pad_maximum_fusion.19), calls=%async_computation.1 | async-start | bytes 589824 | tf_op jit(solution)/shard_map/while/body/eval_jaxpr/all_to_all | solution.py:55
  147.7 6.8 %all-to-all-done.1 = f32[8,72,128]{2,1,0:T(8,128)S(1)} async-done(((f32[8,72,128]{2,1,0:T(8,128)}), f32[8,72,128]{2,1,0:T(8,128)S(1)}, u32[]{:S(2)}, u32[]{:S(2)}) %all-to-all-start.1) | async-done | bytes 294944 | tf_op jit(solution)/shard_map/while/body/eval_jaxpr/all_to_all | solution.py:55
  156.1 13.0 %all_to_all.43 = f32[16,64,128]{2,1,0:T(8,128)S(1)} all-to-all(f32[16,64,128]{2,1,0:T(8,128)S(1)} %broadcast_in_dim.58), channel_id=1, replica_groups=mesh['mom'=16,'hist'=8] {'mom'}, dimensions={0} | all-to-all | bytes 1048576 | tf_op jit(solution)/shard_map/while/body/eval_jaxpr/all_to_all | solution.py:39
  170.3 3.8 %fusion.79 = f32[8,8,1024]{2,1,0:T(8,128)S(1)} fusion(f32[2,8,128,1024]{3,2,1,0:T(8,128)} %get-tuple-element.502, f32[8,4,128]{2,1,0:T(4,128)S(1)} %copy.40, f32[8,4,128]{2,1,0:T(4,128)S(1)} %copy.41), kind=kOutput, calls=%fused_computation.2.clone.1 | convolution fusion | flops 50339840 | bytes 4489216 | tf_op jit(solution)/shard_map/while/body/eval_jaxpr/kxs,kst->kxt/dot_general | solution.py:88
  174.1 1.3 fusion.78
  175.9 0.7 pad_maximum_fusion.19
  176.7 5.5 %all-to-all-start.1 = ((f32[8,72,128]{2,1,0:T(8,128)}), f32[8,72,128]{2,1,0:T(8,128)S(1)}, u32[]{:S(2)}, u32[]{:S(2)}) async-start(f32[8,72,128]{2,1,0:T(8,128)} %pad_maximum_fusion.19), calls=%async_computation.1 | async-start | bytes 589824 | tf_op jit(solution)/shard_map/while/body/eval_jaxpr/all_to_all | solution.py:55
  182.2 6.8 %all-to-all-done.1 = f32[8,72,128]{2,1,0:T(8,128)S(1)} async-done(((f32[8,72,128]{2,1,0:T(8,128)}), f32[8,72,128]{2,1,0:T(8,128)S(1)}, u32[]{:S(2)}, u32[]{:S(2)}) %all-to-all-start.1) | async-done | bytes 294944 | tf_op jit(solution)/shard_map/while/body/eval_jaxpr/all_to_all | solution.py:55
  190.5 13.0 %all_to_all.43 = f32[16,64,128]{2,1,0:T(8,128)S(1)} all-to-all(f32[16,64,128]{2,1,0:T(8,128)S(1)} %broadcast_in_dim.58), channel_id=1, replica_groups=mesh['mom'=16,'hist'=8] {'mom'}, dimensions={0} | all-to-all | bytes 1048576 | tf_op jit(solution)/shard_map/while/body/eval_jaxpr/all_to_all | solution.py:39
  203.7 0.6 convolution_bitcast_fusion.4
  204.8 3.8 %fusion.79 = f32[8,8,1024]{2,1,0:T(8,128)S(1)} fusion(f32[2,8,128,1024]{3,2,1,0:T(8,128)} %get-tuple-element.502, f32[8,4,128]{2,1,0:T(4,128)S(1)} %copy.40, f32[8,4,128]{2,1,0:T(4,128)S(1)} %copy.41), kind=kOutput, calls=%fused_computation.2.clone.1 | convolution fusion | flops 50339840 | bytes 4489216 | tf_op jit(solution)/shard_map/while/body/eval_jaxpr/kxs,kst->kxt/dot_general | solution.py:88
  208.6 1.3 fusion.78
  210.4 0.7 pad_maximum_fusion.19
  211.1 5.5 %all-to-all-start.1 = ((f32[8,72,128]{2,1,0:T(8,128)}), f32[8,72,128]{2,1,0:T(8,128)S(1)}, u32[]{:S(2)}, u32[]{:S(2)}) async-start(f32[8,72,128]{2,1,0:T(8,128)} %pad_maximum_fusion.19), calls=%async_computation.1 | async-start | bytes 589824 | tf_op jit(solution)/shard_map/while/body/eval_jaxpr/all_to_all | solution.py:55
  216.6 6.8 %all-to-all-done.1 = f32[8,72,128]{2,1,0:T(8,128)S(1)} async-done(((f32[8,72,128]{2,1,0:T(8,128)}), f32[8,72,128]{2,1,0:T(8,128)S(1)}, u32[]{:S(2)}, u32[]{:S(2)}) %all-to-all-start.1) | async-done | bytes 294944 | tf_op jit(solution)/shard_map/while/body/eval_jaxpr/all_to_all | solution.py:55
  225.6 0.7 broadcast_in_dim.55
  226.3 13.7 %all_to_all.42 = f32[128,1,1]{2,1,0:T(1,128)S(1)} all-to-all(f32[128,1,1]{2,1,0:T(1,128)S(1)} %broadcast_in_dim.55), channel_id=1, replica_groups=mesh['mom'=16,'hist'=8] {'mom','hist'}, dimensions={0} | all-to-all | bytes 1024 | tf_op jit(solution)/shard_map/all_to_all | solution.py:121
  240.0 0.7 reduce_sum.83
  241.4 0.6 divide_add_fusion.1
  (163 shorter events, 14.5 us)
Async XLA Ops:
  2.5 24.6 %all-to-all-start.2 = ((f32[16,128,128]{2,1,0:T(8,128)}), f32[16,128,128]{2,1,0:T(8,128)S(1)}, u32[]{:S(2)}, u32[]{:S(2)}) async-start(f32[16,128,128]{2,1,0:T(8,128)} %broadcast_in_dim.53), calls=%async_computation.2 | async-start | bytes 2097152 | tf_op jit(solution)/shard_map/all_to_all | solution.py:39
  29.5 16.3 %copy-start.1 = (f32[2,8,4,128]{3,2,1,0:T(4,128)S(1)}, f32[2,8,4,128]{3,2,1,0:T(4,128)}, u32[]{:S(2)}) copy-start(f32[2,8,4,128]{3,2,1,0:T(4,128)} %param.8) | copy-start | bytes 98308
  38.9 13.6 %all-to-all-start.3 = ((f32[8,72,128]{2,1,0:T(8,128)}), f32[8,72,128]{2,1,0:T(8,128)S(1)}, u32[]{:S(2)}, u32[]{:S(2)}) async-start(f32[8,72,128]{2,1,0:T(8,128)} %pad_maximum_fusion.4), calls=%async_computation.3 | async-start | bytes 589824 | tf_op jit(solution)/shard_map/all_to_all | solution.py:55
  66.0 4.9 %copy-start = (f32[2,8,128,1024]{3,2,1,0:T(8,128)S(1)}, f32[2,8,128,1024]{3,2,1,0:T(8,128)}, u32[]{:S(2)}) copy-start(f32[2,8,128,1024]{3,2,1,0:T(8,128)} %get-tuple-element.502) | copy-start | bytes 25165828 | tf_op jit(solution)/shard_map/while
  73.5 12.0 %all-to-all-start.1 = ((f32[8,72,128]{2,1,0:T(8,128)}), f32[8,72,128]{2,1,0:T(8,128)S(1)}, u32[]{:S(2)}, u32[]{:S(2)}) async-start(f32[8,72,128]{2,1,0:T(8,128)} %pad_maximum_fusion.19), calls=%async_computation.1 | async-start | bytes 589824 | tf_op jit(solution)/shard_map/while/body/eval_jaxpr/all_to_all | solution.py:55
  100.2 4.9 %copy-start = (f32[2,8,128,1024]{3,2,1,0:T(8,128)S(1)}, f32[2,8,128,1024]{3,2,1,0:T(8,128)}, u32[]{:S(2)}) copy-start(f32[2,8,128,1024]{3,2,1,0:T(8,128)} %get-tuple-element.502) | copy-start | bytes 25165828 | tf_op jit(solution)/shard_map/while
  107.7 12.3 %all-to-all-start.1 = ((f32[8,72,128]{2,1,0:T(8,128)}), f32[8,72,128]{2,1,0:T(8,128)S(1)}, u32[]{:S(2)}, u32[]{:S(2)}) async-start(f32[8,72,128]{2,1,0:T(8,128)} %pad_maximum_fusion.19), calls=%async_computation.1 | async-start | bytes 589824 | tf_op jit(solution)/shard_map/while/body/eval_jaxpr/all_to_all | solution.py:55
  134.7 4.9 %copy-start = (f32[2,8,128,1024]{3,2,1,0:T(8,128)S(1)}, f32[2,8,128,1024]{3,2,1,0:T(8,128)}, u32[]{:S(2)}) copy-start(f32[2,8,128,1024]{3,2,1,0:T(8,128)} %get-tuple-element.502) | copy-start | bytes 25165828 | tf_op jit(solution)/shard_map/while
  142.2 12.3 %all-to-all-start.1 = ((f32[8,72,128]{2,1,0:T(8,128)}), f32[8,72,128]{2,1,0:T(8,128)S(1)}, u32[]{:S(2)}, u32[]{:S(2)}) async-start(f32[8,72,128]{2,1,0:T(8,128)} %pad_maximum_fusion.19), calls=%async_computation.1 | async-start | bytes 589824 | tf_op jit(solution)/shard_map/while/body/eval_jaxpr/all_to_all | solution.py:55
  169.1 4.9 %copy-start = (f32[2,8,128,1024]{3,2,1,0:T(8,128)S(1)}, f32[2,8,128,1024]{3,2,1,0:T(8,128)}, u32[]{:S(2)}) copy-start(f32[2,8,128,1024]{3,2,1,0:T(8,128)} %get-tuple-element.502) | copy-start | bytes 25165828 | tf_op jit(solution)/shard_map/while
  176.7 12.3 %all-to-all-start.1 = ((f32[8,72,128]{2,1,0:T(8,128)}), f32[8,72,128]{2,1,0:T(8,128)S(1)}, u32[]{:S(2)}, u32[]{:S(2)}) async-start(f32[8,72,128]{2,1,0:T(8,128)} %pad_maximum_fusion.19), calls=%async_computation.1 | async-start | bytes 589824 | tf_op jit(solution)/shard_map/while/body/eval_jaxpr/all_to_all | solution.py:55
  203.6 4.9 %copy-start = (f32[2,8,128,1024]{3,2,1,0:T(8,128)S(1)}, f32[2,8,128,1024]{3,2,1,0:T(8,128)}, u32[]{:S(2)}) copy-start(f32[2,8,128,1024]{3,2,1,0:T(8,128)} %get-tuple-element.502) | copy-start | bytes 25165828 | tf_op jit(solution)/shard_map/while
  211.1 12.3 %all-to-all-start.1 = ((f32[8,72,128]{2,1,0:T(8,128)}), f32[8,72,128]{2,1,0:T(8,128)S(1)}, u32[]{:S(2)}, u32[]{:S(2)}) async-start(f32[8,72,128]{2,1,0:T(8,128)} %pad_maximum_fusion.19), calls=%async_computation.1 | async-start | bytes 589824 | tf_op jit(solution)/shard_map/while/body/eval_jaxpr/all_to_all | solution.py:55
  242.1 0.5 copy-start.2

commit v10 on v9

--- a/solution.py
+++ b/solution.py
@@ -113,7 +113,9 @@
         return (green, integral, deltas)
 
     carry = (free_rows, integral, jnp.zeros((ITERS,), jnp.float32))
-    green, integral, deltas = lax.fori_loop(0, ITERS - 1, correction, carry)
+    for turn in range(ITERS - 1):
+        carry = correction(turn, carry)
+    green, integral, deltas = carry
     change = free_rows + step_size * integral - green
     local = jnp.sum(change * change)
     n_dev = lax.axis_size(("mom", "hist"))

time: 244 us -> 245 us (level)
  blocking collectives: 78.9 us -> 138 us
  waiting for transfers between devices: 56.1 us -> 25.3 us
  starting transfers between devices: 42.6 us -> 12.6 us
  matrix products: 40.3 us -> 47.3 us
  between operations: 1.58 us -> 5.82 us
  loops' own time: 4.19 us -> 0 us
  other arithmetic: 13.5 us -> 9.81 us
    all_to_all x1 -> x6, blocking collectives: 13.7 us -> 72 us  [hist_reduce(): y = lax.all_to_all(x, 'hist', 0, 0, tiled=True)]
    all_to_all x6 -> x1, waiting for transfers between devices: 40.5 us -> 9.69 us  [shards(): total = jnp.sum(lax.all_to_all(spread, ('mom', 'hist'), 0, 0, tiled=True))]
    all_to_all x6 -> x1, starting transfers between devices: 34 us -> 3.97 us  [shards(): total = jnp.sum(lax.all_to_all(spread, ('mom', 'hist'), 0, 0, tiled=True))]
    dot_general x6, matrix products: 10.4 us -> 20.4 us  [contract(): b = jnp.einsum('kxs,kst->kxt', x, hist_panel[1], precision=precision)]
    concatenate x6, other arithmetic: 4.39 us -> 0.14 us  [hist_reduce(): x = jnp.concatenate([x, jnp.broadcast_to(tile, (hist_n, 8, 128))], axis=1)]
    another operation x1 -> x0, loops' own time: 4.19 us -> none  [shards(): green, integral, deltas = lax.fori_loop(0, ITERS - 1, correction, carry)]
  transfers between devices with their start and end apart: 7 -> 2, of which waited for: 7 -> 2; matrix products, arithmetic and copies ran while one was open for 0% -> 0% of each run, Pallas kernels for 0% -> 0%
where the time goes in v10:
time: 245 us; the launch traced here: 244 us
  blocking collectives  138 us (56%)
  matrix products  47.3 us (19%)
  waiting for transfers between devices  25.3 us (10%)
  starting transfers between devices  12.6 us (5%)
  other arithmetic  9.81 us (4%)
  between operations  5.82 us (2%)
  local copies, waits for them, and re-layouts  4.89 us (2%)
    all_to_all x6, blocking collectives, hist_reduce(): y = lax.all_to_all(x, 'hist', 0, 0, tiled=True)  72 us
    all_to_all x5, blocking collectives, gather_rows(): lax.all_to_all(jnp.broadcast_to(block, (n_mom,) + block.shape), 'mom', 0,...  66.2 us
    dot_general x6, matrix products, contract(): b = jnp.einsum('kxs,kst->kxt', x, hist_panel[1], precision=precision)  20.4 us
    dot_general x6, matrix products, contract(): a = jnp.einsum('kxs,kst->kxt', x, hist_panel[0], precision=precision)  20.4 us
    all_to_all x1, waiting for transfers between devices, gather_rows(): lax.all_to_all(jnp.broadcast_to(block, (n_mom,) + block.shape), 'mom', 0,...  15.6 us
    all_to_all x1, waiting for transfers between devices, shards(): total = jnp.sum(lax.all_to_all(spread, ('mom', 'hist'), 0, 0, tiled=True))  9.69 us
    all_to_all x1, starting transfers between devices, gather_rows(): lax.all_to_all(jnp.broadcast_to(block, (n_mom,) + block.shape), 'mom', 0,...  8.59 us
    dot_general x13, matrix products, mm(): return jnp.dot(table, field, precision=precision)  6.46 us
  transfers between devices with their start and end apart: 2, of which 2 were waited for; matrix products, arithmetic and copies ran while one was open for 0% of the time, Pallas kernels for 0%

profile of v10, /device:TPU:1, one launch (start us, length us, event | category | flops | bytes accessed | tf_op | source)
XLA Modules:
  0.0 243.8 jit_solution(3470366168298029856)
XLA Ops:
  0.6 0.8 pad_maximum_fusion.7
  1.4 1.1 broadcast_in_dim.73
  2.5 8.6 %all-to-all-start = ((f32[16,128,128]{2,1,0:T(8,128)}), f32[16,128,128]{2,1,0:T(8,128)S(1)}, u32[]{:S(2)}, u32[]{:S(2)}) async-start(f32[16,128,128]{2,1,0:T(8,128)} %broadcast_in_dim.73), calls=%async_computation | async-start | bytes 2097152 | tf_op jit(solution)/shard_map/all_to_all | solution.py:39
  11.1 0.3 fusion.94
  11.5 15.6 %all-to-all-done = f32[16,128,128]{2,1,0:T(8,128)S(1)} async-done(((f32[16,128,128]{2,1,0:T(8,128)}), f32[16,128,128]{2,1,0:T(8,128)S(1)}, u32[]{:S(2)}, u32[]{:S(2)}) %all-to-all-start) | async-done | bytes 1048608 | tf_op jit(solution)/shard_map/all_to_all | solution.py:39
  27.5 1.0 fusion.36
  28.5 1.0 fusion.40
  29.9 0.4 fusion.44
  30.3 3.8 %fusion.22 = f32[8,8,1024]{2,1,0:T(8,128)S(1)} fusion(f32[2,8,128,1024]{3,2,1,0:T(8,128)} %param.5, f32[8,4,128]{2,1,0:T(4,128)S(1)} %copy.54, f32[8,4,128]{2,1,0:T(4,128)S(1)} %copy.53), kind=kOutput, calls=%fused_computation.22 | convolution fusion | flops 100671488 | bytes 4489216 | tf_op jit(solution)/shard_map/kxs,kst->kxt/dot_general | solution.py:88
  34.1 3.8 %fusion.10 = f32[8,8,1024]{2,1,0:T(8,128)S(1)} fusion(f32[2,8,128,1024]{3,2,1,0:T(8,128)} %param.5, f32[8,4,128]{2,1,0:T(4,128)S(1)} %copy.54, f32[8,4,128]{2,1,0:T(4,128)S(1)} %copy.53), kind=kOutput, calls=%fused_computation.10 | convolution fusion | flops 100671488 | bytes 4489216 | tf_op jit(solution)/shard_map/kxs,kst->kxt/dot_general | solution.py:89
  38.2 14.0 %all_to_all.66 = f32[8,72,128]{2,1,0:T(8,128)S(1)} all-to-all(f32[8,72,128]{2,1,0:T(8,128)S(1)} %pad_maximum_fusion), channel_id=1, replica_groups=mesh['mom'=16,'hist'=8] {'hist'}, dimensions={0} | all-to-all | bytes 589824 | tf_op jit(solution)/shard_map/all_to_all | solution.py:55
  52.3 13.4 %all_to_all.67 = f32[16,64,128]{2,1,0:T(8,128)S(1)} all-to-all(f32[16,64,128]{2,1,0:T(8,128)S(1)} %broadcast_in_dim.75), channel_id=1, replica_groups=mesh['mom'=16,'hist'=8] {'mom'}, dimensions={0} | all-to-all | bytes 1048576 | tf_op jit(solution)/shard_map/all_to_all | solution.py:39
  65.9 0.6 fusion.48
  66.7 0.2 fusion.52
  66.9 3.3 %fusion.20 = f32[8,8,1024]{2,1,0:T(8,128)S(1)} fusion(f32[2,8,128,1024]{3,2,1,0:T(8,128)} %param.5, f32[8,4,128]{2,1,0:T(4,128)S(1)} %copy.57, f32[8,4,128]{2,1,0:T(4,128)S(1)} %copy.56), kind=kOutput, calls=%fused_computation.20 | convolution fusion | flops 50339840 | bytes 4489216 | tf_op jit(solution)/shard_map/kxs,kst->kxt/dot_general | solution.py:88
  70.3 3.3 %fusion.8 = f32[8,8,1024]{2,1,0:T(8,128)S(1)} fusion(f32[2,8,128,1024]{3,2,1,0:T(8,128)} %param.5, f32[8,4,128]{2,1,0:T(4,128)S(1)} %copy.57, f32[8,4,128]{2,1,0:T(4,128)S(1)} %copy.56), kind=kOutput, calls=%fused_computation.8 | convolution fusion | flops 50339840 | bytes 4489216 | tf_op jit(solution)/shard_map/kxs,kst->kxt/dot_general | solution.py:89
  74.1 11.3 %all_to_all.68 = f32[8,72,128]{2,1,0:T(8,128)S(1)} all-to-all(f32[8,72,128]{2,1,0:T(8,128)S(1)} %pad_maximum_fusion.1), channel_id=1, replica_groups=mesh['mom'=16,'hist'=8] {'hist'}, dimensions={0} | all-to-all | bytes 589824 | tf_op jit(solution)/shard_map/all_to_all | solution.py:55
  85.5 0.6 slice_reduce_fusion.10
  86.9 13.2 %all_to_all.69 = f32[16,64,128]{2,1,0:T(8,128)S(1)} all-to-all(f32[16,64,128]{2,1,0:T(8,128)S(1)} %broadcast_in_dim.78), channel_id=1, replica_groups=mesh['mom'=16,'hist'=8] {'mom'}, dimensions={0} | all-to-all | bytes 1048576 | tf_op jit(solution)/shard_map/all_to_all | solution.py:39
  100.2 0.6 fusion.56
  101.3 3.3 %fusion.18 = f32[8,8,1024]{2,1,0:T(8,128)S(1)} fusion(f32[2,8,128,1024]{3,2,1,0:T(8,128)} %param.5, f32[8,4,128]{2,1,0:T(4,128)S(1)} %copy.60, f32[8,4,128]{2,1,0:T(4,128)S(1)} %copy.59), kind=kOutput, calls=%fused_computation.18 | convolution fusion | flops 50339840 | bytes 4489216 | tf_op jit(solution)/shard_map/kxs,kst->kxt/dot_general | solution.py:88
  104.6 3.3 %fusion.6 = f32[8,8,1024]{2,1,0:T(8,128)S(1)} fusion(f32[2,8,128,1024]{3,2,1,0:T(8,128)} %param.5, f32[8,4,128]{2,1,0:T(4,128)S(1)} %copy.60, f32[8,4,128]{2,1,0:T(4,128)S(1)} %copy.59), kind=kOutput, calls=%fused_computation.6 | convolution fusion | flops 50339840 | bytes 4489216 | tf_op jit(solution)/shard_map/kxs,kst->kxt/dot_general | solution.py:89
  108.5 11.6 %all_to_all.70 = f32[8,72,128]{2,1,0:T(8,128)S(1)} all-to-all(f32[8,72,128]{2,1,0:T(8,128)S(1)} %pad_maximum_fusion.2), channel_id=1, replica_groups=mesh['mom'=16,'hist'=8] {'hist'}, dimensions={0} | all-to-all | bytes 589824 | tf_op jit(solution)/shard_map/all_to_all | solution.py:55
  120.1 0.6 slice_reduce_fusion.9
  121.5 13.2 %all_to_all.71 = f32[16,64,128]{2,1,0:T(8,128)S(1)} all-to-all(f32[16,64,128]{2,1,0:T(8,128)S(1)} %broadcast_in_dim.81), channel_id=1, replica_groups=mesh['mom'=16,'hist'=8] {'mom'}, dimensions={0} | all-to-all | bytes 1048576 | tf_op jit(solution)/shard_map/all_to_all | solution.py:39
  134.8 0.6 fusion.64
  135.9 3.3 %fusion.16 = f32[8,8,1024]{2,1,0:T(8,128)S(1)} fusion(f32[2,8,128,1024]{3,2,1,0:T(8,128)} %param.5, f32[8,4,128]{2,1,0:T(4,128)S(1)} %copy.63, f32[8,4,128]{2,1,0:T(4,128)S(1)} %copy.62), kind=kOutput, calls=%fused_computation.16 | convolution fusion | flops 50339840 | bytes 4489216 | tf_op jit(solution)/shard_map/kxs,kst->kxt/dot_general | solution.py:88
  139.2 3.3 %fusion.4 = f32[8,8,1024]{2,1,0:T(8,128)S(1)} fusion(f32[2,8,128,1024]{3,2,1,0:T(8,128)} %param.5, f32[8,4,128]{2,1,0:T(4,128)S(1)} %copy.63, f32[8,4,128]{2,1,0:T(4,128)S(1)} %copy.62), kind=kOutput, calls=%fused_computation.4 | convolution fusion | flops 50339840 | bytes 4489216 | tf_op jit(solution)/shard_map/kxs,kst->kxt/dot_general | solution.py:89
  143.1 11.6 %all_to_all.72 = f32[8,72,128]{2,1,0:T(8,128)S(1)} all-to-all(f32[8,72,128]{2,1,0:T(8,128)S(1)} %pad_maximum_fusion.3), channel_id=1, replica_groups=mesh['mom'=16,'hist'=8] {'hist'}, dimensions={0} | all-to-all | bytes 589824 | tf_op jit(solution)/shard_map/all_to_all | solution.py:55
  154.7 0.7 slice_reduce_fusion.8
  156.3 13.2 %all_to_all.73 = f32[16,64,128]{2,1,0:T(8,128)S(1)} all-to-all(f32[16,64,128]{2,1,0:T(8,128)S(1)} %broadcast_in_dim.84), channel_id=1, replica_groups=mesh['mom'=16,'hist'=8] {'mom'}, dimensions={0} | all-to-all | bytes 1048576 | tf_op jit(solution)/shard_map/all_to_all | solution.py:39
  169.6 0.6 fusion.72
  170.6 3.3 %fusion.14 = f32[8,8,1024]{2,1,0:T(8,128)S(1)} fusion(f32[2,8,128,1024]{3,2,1,0:T(8,128)} %param.5, f32[8,4,128]{2,1,0:T(4,128)S(1)} %copy.66, f32[8,4,128]{2,1,0:T(4,128)S(1)} %copy.65), kind=kOutput, calls=%fused_computation.14 | convolution fusion | flops 50339840 | bytes 4489216 | tf_op jit(solution)/shard_map/kxs,kst->kxt/dot_general | solution.py:88
  174.0 3.3 %fusion.2 = f32[8,8,1024]{2,1,0:T(8,128)S(1)} fusion(f32[2,8,128,1024]{3,2,1,0:T(8,128)} %param.5, f32[8,4,128]{2,1,0:T(4,128)S(1)} %copy.66, f32[8,4,128]{2,1,0:T(4,128)S(1)} %copy.65), kind=kOutput, calls=%fused_computation.2 | convolution fusion | flops 50339840 | bytes 4489216 | tf_op jit(solution)/shard_map/kxs,kst->kxt/dot_general | solution.py:89
  177.8 11.8 %all_to_all.74 = f32[8,72,128]{2,1,0:T(8,128)S(1)} all-to-all(f32[8,72,128]{2,1,0:T(8,128)S(1)} %pad_maximum_fusion.4), channel_id=1, replica_groups=mesh['mom'=16,'hist'=8] {'hist'}, dimensions={0} | all-to-all | bytes 589824 | tf_op jit(solution)/shard_map/all_to_all | solution.py:55
  189.7 0.7 slice_reduce_fusion.7
  191.2 13.2 %all_to_all.75 = f32[16,64,128]{2,1,0:T(8,128)S(1)} all-to-all(f32[16,64,128]{2,1,0:T(8,128)S(1)} %broadcast_in_dim.87), channel_id=1, replica_groups=mesh['mom'=16,'hist'=8] {'mom'}, dimensions={0} | all-to-all | bytes 1048576 | tf_op jit(solution)/shard_map/all_to_all | solution.py:39
  204.6 0.6 fusion.80
  205.6 3.3 %fusion.12 = f32[8,8,1024]{2,1,0:T(8,128)S(1)} fusion(f32[2,8,128,1024]{3,2,1,0:T(8,128)} %param.5, f32[8,4,128]{2,1,0:T(4,128)S(1)} %copy.69, f32[8,4,128]{2,1,0:T(4,128)S(1)} %copy.68), kind=kOutput, calls=%fused_computation.12 | convolution fusion | flops 50339840 | bytes 4489216 | tf_op jit(solution)/shard_map/kxs,kst->kxt/dot_general | solution.py:88
  209.0 3.3 %fusion = f32[8,8,1024]{2,1,0:T(8,128)S(1)} fusion(f32[2,8,128,1024]{3,2,1,0:T(8,128)} %param.5, f32[8,4,128]{2,1,0:T(4,128)S(1)} %copy.69, f32[8,4,128]{2,1,0:T(4,128)S(1)} %copy.68), kind=kOutput, calls=%fused_computation | convolution fusion | flops 50339840 | bytes 4489216 | tf_op jit(solution)/shard_map/kxs,kst->kxt/dot_general | solution.py:89
  212.8 11.6 %all_to_all.76 = f32[8,72,128]{2,1,0:T(8,128)S(1)} all-to-all(f32[8,72,128]{2,1,0:T(8,128)S(1)} %pad_maximum_fusion.5), channel_id=1, replica_groups=mesh['mom'=16,'hist'=8] {'hist'}, dimensions={0} | all-to-all | bytes 589824 | tf_op jit(solution)/shard_map/all_to_all | solution.py:55
  224.5 0.7 slice_reduce_fusion.6
  225.9 0.7 multiply_reduce_fusion.5
  226.6 1.3 broadcast_in_dim.90
  228.0 4.0 %all-to-all-start.12 = ((f32[128,1,1]{2,1,0:T(1,128)}), f32[128,1,1]{2,1,0:T(1,128)S(1)}, u32[]{:S(2)}, u32[]{:S(2)}) async-start(f32[128,1,1]{2,1,0:T(1,128)} %broadcast_in_dim.90), calls=%async_computation.12 | async-start | bytes 131072 | tf_op jit(solution)/shard_map/all_to_all | solution.py:123
  232.0 9.7 %all-to-all-done.12 = f32[128,1,1]{2,1,0:T(1,128)S(1)} async-done(((f32[128,1,1]{2,1,0:T(1,128)}), f32[128,1,1]{2,1,0:T(1,128)S(1)}, u32[]{:S(2)}, u32[]{:S(2)}) %all-to-all-start.12) | async-done | bytes 544 | tf_op jit(solution)/shard_map/all_to_all | solution.py:123
  241.7 0.7 reduce_sum.199
  243.2 0.6 divide_add_fusion
  (132 shorter events, 6.8 us)
Async XLA Ops:
  2.5 24.6 %all-to-all-start = ((f32[16,128,128]{2,1,0:T(8,128)}), f32[16,128,128]{2,1,0:T(8,128)S(1)}, u32[]{:S(2)}, u32[]{:S(2)}) async-start(f32[16,128,128]{2,1,0:T(8,128)} %broadcast_in_dim.73), calls=%async_computation | async-start | bytes 2097152 | tf_op jit(solution)/shard_map/all_to_all | solution.py:39
  29.7 22.5 %copy-start = (f32[2,8,4,128]{3,2,1,0:T(4,128)S(1)}, f32[2,8,4,128]{3,2,1,0:T(4,128)}, u32[]{:S(2)}) copy-start(f32[2,8,4,128]{3,2,1,0:T(4,128)} %param.6) | copy-start | bytes 98308
  228.0 13.8 %all-to-all-start.12 = ((f32[128,1,1]{2,1,0:T(1,128)}), f32[128,1,1]{2,1,0:T(1,128)S(1)}, u32[]{:S(2)}, u32[]{:S(2)}) async-start(f32[128,1,1]{2,1,0:T(1,128)} %broadcast_in_dim.90), calls=%async_computation.12 | async-start | bytes 131072 | tf_op jit(solution)/shard_map/all_to_all | solution.py:123
  243.2 0.6 copy-start.1
